TPU v7x, 128 devices: a whole 4x4x4 slice. The times are simulated.
128 devices in a mesh: epoch: 8 (over z, y_hi), row: 16 (over y_lo, x, core).
Axes of the slice: x: 4, y: 4 (y_hi: 2, y_lo: 2; y = y_hi * 2 + y_lo), z: 4, core: 2. Of those that a mesh axis runs over, the one named last changes fastest.
Arguments:
- field: bfloat16 [1024, 512, 512], P('epoch', 'row'), may hold values from -6 to 6
- factor: bfloat16 [1024, 1024], P('epoch'), may hold values from -0.1875 to 0.1875
- kappa: float32 [512, 512], P('row'), may hold values from 0.05 to 1
Outputs:
- product: float32 [1024, 512, 512], P('epoch', 'row')
All inputs are finite; a program needn't handle non-finite values.
Results may differ from a plain program's by a relative error of at most 0.0004.
Values may be sent and summed in bfloat16 or wider, within the bound.
No kernel may reach another device: no remote copies, remote signals or barrier semaphores. Data moves between devices by JAX's collectives and lax.ppermute only.
A program may use at most 192 MiB of HBM per device.

v0:
```python
import jax
import jax.numpy as jnp
from jax import lax
from jax.sharding import PartitionSpec as P


def with_halo(x, sides, width):
    for axis, dim in sides:
        size, length = (lax.axis_size(axis), x.shape[dim])
        up = [(i, (i + 1) % size) for i in range(size - 1)]
        down = [(j, i) for i, j in up]
        last = lax.slice_in_dim(x, length - width, length, axis=dim)
        first = lax.slice_in_dim(x, 0, width, axis=dim)
        before = lax.ppermute(last, axis, up)
        after = lax.ppermute(first, axis, down)
        x = jnp.concatenate([before, x, after], axis=dim)
    return x


def stencil(padded, kappa):
    center = padded[:, 1:-1, :]
    sides = jnp.pad(center, ((0, 0), (0, 0), (1, 1)))
    upper = padded[:, :-2, :]
    below = padded[:, 2:, :]
    return (kappa + 4.0) * center - (upper + below + sides[:, :, :-2] + sides[:, :, 2:])


def single_rim(values):
    return with_halo(values, (("row", 1),), 1)


def body(field, factor, kappa):
    epochs = field.shape[0]
    slab = field.shape[1]
    width = field.shape[2]
    count = lax.axis_size("epoch")
    order = epochs * count
    global_rows = lax.axis_index("epoch") * epochs + lax.broadcasted_iota(
        jnp.int32, (epochs, order), 0
    )
    global_cols = lax.broadcasted_iota(jnp.int32, (epochs, order), 1)
    lower = jnp.where(global_cols <= global_rows, factor, jnp.zeros_like(factor))
    piece = lax.all_gather(field, "epoch", axis=0, tiled=True)
    many = piece.shape[0]
    timed = jnp.dot(
        lower, piece.reshape(many, slab * width), preferred_element_type=jnp.float32
    ).reshape(epochs, slab, width)
    first = stencil(single_rim(timed), kappa)
    return stencil(single_rim(first), kappa)


def solution(mesh):
    in_specs = (P("epoch", "row", None), P("epoch", None), P("row", None))
    out_specs = P("epoch", "row", None)
    return jax.shard_map(body, mesh=mesh, in_specs=in_specs, out_specs=out_specs, check_vma=False)
```

profile of v0, /device:TPU:7, one launch (start us, length us, event | category | flops | bytes accessed | tf_op | source)
XLA Modules:
  0.0 493.1 jit_solution(14374441201835860905)
XLA Ops:
  6.5 0.0 all-gather.2.cloned.1.call-start
  6.5 0.7 all-gather.2.cloned.1.call-update
  7.3 0.0 copy-start
  7.3 338.7 %all-gather.2.cloned.1.call-done = bf16[1024,32,512]{2,1,0:T(8,128)(2,1)} async-done(((bf16[128,32,512]{2,1,0:T(8,128)(2,1)}), bf16[1024,32,512]{2,1,0:T(8,128)(2,1)}) %all-gather.2.cloned.1.call-update) | async-done | bytes 33554448 | tf_op jit(solution)/shard_map/all_gather | solution.py:43
  345.9 45.1 %copy.8 = bf16[1024,32,512]{0,2,1:T(8,128)(2,1)} copy(bf16[1024,32,512]{2,1,0:T(8,128)(2,1)} %all-gather.2.cloned.1.call-done) | data formatting | bytes 67108864 | tf_op jit(solution)/shard_map/reshape | solution.py:46
  391.1 0.0 copy-done
  391.1 0.0 copy-start.1
  391.1 18.8 %fusion = f32[128,32,512]{2,0,1:T(8,128)} fusion(bf16[1024,32,512]{0,2,1:T(8,128)(2,1)} %copy.8, bf16[128,1024]{1,0:T(8,128)(2,1)S(1)} %copy-done, s32[128]{0:T(128)S(1)} %iota_add_fusion), kind=kOutput, calls=%fused_computation | convolution fusion | flops 4295229440 | bytes 42205696 | tf_op jit(solution)/shard_map/dot_general | solution.py:45
  409.9 1.1 fusion.17
  411.0 3.2 collective-permute-start
  414.1 1.9 collective-permute-start.1
  416.1 0.0 copy-done.1
  416.1 1.3 collective-permute-done
  417.4 6.5 %collective-permute-done.1 = f32[128,1,512]{2,0,1:T(8,128)S(1)} collective-permute-done((f32[128,1,512]{2,0,1:T(8,128)S(1)}, f32[128,1,512]{2,0,1:T(8,128)S(1)}, u32[]{:S(2)}, u32[]{:S(2)}) %collective-permute-start.1) | collective-permute-done | bytes 262176 | tf_op jit(solution)/shard_map/ppermute | solution.py:15
  423.9 18.9 %fusion.4 = f32[128,32,512]{2,0,1:T(8,128)} fusion(f32[128,32,512]{2,0,1:T(8,128)} %fusion, f32[128,1,512]{2,0,1:T(8,128)S(1)} %collective-permute-done.1, f32[128,1,512]{2,0,1:T(8,128)S(1)} %collective-permute-done, f32[32,512]{1,0:T(8,128)S(1)} %broadcast_add_fusion), kind=kLoop, calls=%fused_computation.8 | loop fusion | flops 14680064 | bytes 17367040 | tf_op jit(solution)/shard_map/sub | solution.py:25
  442.9 1.1 fusion.16
  443.9 1.9 collective-permute-start.2
  445.9 2.6 collective-permute-start.3
  448.5 0.7 collective-permute-done.2
  449.2 6.5 %collective-permute-done.3 = f32[128,1,512]{2,0,1:T(8,128)S(1)} collective-permute-done((f32[128,1,512]{2,0,1:T(8,128)S(1)}, f32[128,1,512]{2,0,1:T(8,128)S(1)}, u32[]{:S(2)}, u32[]{:S(2)}) %collective-permute-start.3) | collective-permute-done | bytes 262176 | tf_op jit(solution)/shard_map/ppermute | solution.py:15
  455.7 18.9 %fusion.7 = f32[128,32,512]{2,0,1:T(8,128)} fusion(f32[128,32,512]{2,0,1:T(8,128)} %fusion.4, f32[128,1,512]{2,0,1:T(8,128)S(1)} %collective-permute-done.3, f32[128,1,512]{2,0,1:T(8,128)S(1)} %collective-permute-done.2, f32[32,512]{1,0:T(8,128)S(1)} %broadcast_add_fusion), kind=kLoop, calls=%fused_computation.11 | loop fusion | flops 14680064 | bytes 17367040 | tf_op jit(solution)/shard_map/sub | solution.py:25
  474.6 11.6 %copy.7 = f32[128,32,512]{2,1,0:T(8,128)} copy(f32[128,32,512]{2,0,1:T(8,128)} %fusion.7) | data formatting | bytes 16777216 | tf_op jit(solution)/shard_map/sub | solution.py:25
  (2 shorter events, 0.0 us)
Async XLA Ops:
  6.5 339.4 %all-gather.2.cloned.1.call-start = ((), (), s32[]{:S(2)}) async-start(), calls=%async_computation | async-start | bytes 37748736 | tf_op jit(solution)/shard_map/all_gather | solution.py:43
  7.3 383.8 %copy-start = (bf16[128,1024]{1,0:T(8,128)(2,1)S(1)}, bf16[128,1024]{1,0:T(8,128)(2,1)}, u32[]{:S(2)}) copy-start(bf16[128,1024]{1,0:T(8,128)(2,1)} %param.4) | copy-start | bytes 786436
  391.1 25.0 %copy-start.1 = (f32[32,512]{1,0:T(8,128)S(1)}, f32[32,512]{1,0:T(8,128)}, u32[]{:S(2)}) copy-start(f32[32,512]{1,0:T(8,128)} %param.5) | copy-start | bytes 196612
  411.0 6.5 %collective-permute-start = (f32[128,1,512]{2,0,1:T(8,128)S(1)}, f32[128,1,512]{2,0,1:T(8,128)S(1)}, u32[]{:S(2)}, u32[]{:S(2)}) collective-permute-start(f32[128,1,512]{2,0,1:T(8,128)S(1)} %get-tuple-element.7), channel_id=1, source_target_pairs={{0,1},{1,2},{2,3},{3,4},{4,5},{5,6},{6,7},{7,8},{8,9},{9,10},{10,1... | collective-permute-start | bytes 786440 | tf_op jit(solution)/shard_map/ppermute | solution.py:14
  414.1 9.8 %collective-permute-start.1 = (f32[128,1,512]{2,0,1:T(8,128)S(1)}, f32[128,1,512]{2,0,1:T(8,128)S(1)}, u32[]{:S(2)}, u32[]{:S(2)}) collective-permute-start(f32[128,1,512]{2,0,1:T(8,128)S(1)} %get-tuple-element.8), channel_id=1, source_target_pairs={{1,0},{2,1},{3,2},{4,3},{5,4},{6,5},{7,6},{8,7},{9,8},{10,9},{11,1... | collective-permute-start | bytes 786440 | tf_op jit(solution)/shard_map/ppermute | solution.py:15
  443.9 5.2 %collective-permute-start.2 = (f32[128,1,512]{2,0,1:T(8,128)S(1)}, f32[128,1,512]{2,0,1:T(8,128)S(1)}, u32[]{:S(2)}, u32[]{:S(2)}) collective-permute-start(f32[128,1,512]{2,0,1:T(8,128)S(1)} %get-tuple-element.5), channel_id=1, source_target_pairs={{0,1},{1,2},{2,3},{3,4},{4,5},{5,6},{6,7},{7,8},{8,9},{9,10},{10,1... | collective-permute-start | bytes 786440 | tf_op jit(solution)/shard_map/ppermute | solution.py:14
  445.9 9.8 %collective-permute-start.3 = (f32[128,1,512]{2,0,1:T(8,128)S(1)}, f32[128,1,512]{2,0,1:T(8,128)S(1)}, u32[]{:S(2)}, u32[]{:S(2)}) collective-permute-start(f32[128,1,512]{2,0,1:T(8,128)S(1)} %get-tuple-element.6), channel_id=1, source_target_pairs={{1,0},{2,1},{3,2},{4,3},{5,4},{6,5},{7,6},{8,7},{9,8},{10,9},{11,1... | collective-permute-start | bytes 786440 | tf_op jit(solution)/shard_map/ppermute | solution.py:15
Sparse Core Ops, SparseCore 0:
  9.7 336.1 all-gather.1
where the time goes:
time: 495 us; the launch traced here: 493 us
  waiting for transfers between devices  354 us (72%)
  local copies, waits for them, and re-layouts  58.9 us (12%)
  other arithmetic  37.9 us (8%)
  matrix products  18.8 us (4%)
  between operations  13.5 us (3%)
  starting transfers between devices  9.59 us (2%)
    all_gather x1, waiting for transfers between devices, body(): piece = lax.all_gather(field, 'epoch', axis=0, tiled=True)  339 us
    reshape x1, local copies, waits for them, and re-layouts, body(): piece.reshape(many, slab * width)  45.1 us
    sub x2, other arithmetic, stencil(): (kappa + 4.0) * center  37.9 us
    dot_general x1, matrix products, body(): jnp.dot(lower, piece.reshape(many, slab * width), preferred_element_type=...  18.8 us
    ppermute x2, waiting for transfers between devices, with_halo(): after = lax.ppermute(first, axis, down)  13 us
    sub x1, local copies, waits for them, and re-layouts, stencil(): (kappa + 4.0) * center  11.6 us
  transfers between devices with their start and end apart: 5, of which 5 were waited for; matrix products, arithmetic and copies ran while one was open for 0% of the time, Pallas kernels for 0%

commit v1 on v0

--- a/solution.py
+++ b/solution.py
@@ -31,20 +31,24 @@
 
 def body(field, factor, kappa):
     epochs = field.shape[0]
-    slab = field.shape[1]
-    width = field.shape[2]
     count = lax.axis_size("epoch")
     order = epochs * count
-    global_rows = lax.axis_index("epoch") * epochs + lax.broadcasted_iota(
-        jnp.int32, (epochs, order), 0
-    )
+    me = lax.axis_index("epoch")
+    global_rows = me * epochs + lax.broadcasted_iota(jnp.int32, (epochs, order), 0)
     global_cols = lax.broadcasted_iota(jnp.int32, (epochs, order), 1)
     lower = jnp.where(global_cols <= global_rows, factor, jnp.zeros_like(factor))
-    piece = lax.all_gather(field, "epoch", axis=0, tiled=True)
-    many = piece.shape[0]
-    timed = jnp.dot(
-        lower, piece.reshape(many, slab * width), preferred_element_type=jnp.float32
-    ).reshape(epochs, slab, width)
+    own = jnp.transpose(field, (1, 2, 0))
+
+    def term(block, source):
+        start = jnp.clip(source, 0, count - 1) * epochs
+        part = lax.dynamic_slice_in_dim(lower, start, epochs, 1)
+        return jnp.einsum("ts,ijs->tij", part, block, preferred_element_type=jnp.float32)
+
+    timed = term(own, me)
+    for shift in range(1, count):
+        pairs = [(e, e + shift) for e in range(count - shift)]
+        got = lax.ppermute(own, "epoch", pairs)
+        timed = timed + term(got, me - shift)
     first = stencil(single_rim(timed), kappa)
     return stencil(single_rim(first), kappa)
 

time: 495 us -> 574 us (1.16)
  the two profiles are of different devices: /device:TPU:7 before, /device:TPU:40 now
where the time goes in v1:
time: 574 us; the launch traced here: 573 us
  waiting for transfers between devices  402 us (70%)
  matrix products  71.3 us (12%)
  starting transfers between devices  39.8 us (7%)
  other arithmetic  38 us (7%)
  local copies, waits for them, and re-layouts  21.8 us (4%)
    ppermute x7, waiting for transfers between devices, body(): got = lax.ppermute(own, 'epoch', pairs)  391 us
    dot_general x8, matrix products, term(): jnp.einsum('ts,ijs->tij', part, block, preferred_element_type=jnp.float32)  71.3 us
    sub x2, other arithmetic, stencil(): (kappa + 4.0) * center  37.9 us
    ppermute x7, starting transfers between devices, body(): got = lax.ppermute(own, 'epoch', pairs)  24.1 us
    ppermute x2, starting transfers between devices, with_halo(): after = lax.ppermute(first, axis, down)  11.9 us
    sub x1, local copies, waits for them, and re-layouts, stencil(): (kappa + 4.0) * center  11.6 us
  transfers between devices with their start and end apart: 11, of which 8 were waited for; matrix products, arithmetic and copies ran while one was open for 8% of the time, Pallas kernels for 0%

profile of v1, /device:TPU:40, one launch (start us, length us, event | category | flops | bytes accessed | tf_op | source)
XLA Modules:
  0.0 573.2 jit_solution(12887719731171517259)
XLA Ops:
  0.0 8.0 %copy.4 = bf16[128,32,512]{0,2,1:T(8,128)(2,1)} copy(bf16[128,32,512]{2,1,0:T(8,128)(2,1)} %param.3) | data formatting | bytes 8388608 | tf_op args[0]
  8.0 8.6 %collective-permute-start.4 = (bf16[32,512,128]{2,1,0:T(8,128)(2,1)}, bf16[32,512,128]{2,1,0:T(8,128)(2,1)}, u32[]{:S(2)}, u32[]{:S(2)}) collective-permute-start(bf16[32,512,128]{2,1,0:T(8,128)(2,1)} %bitcast.36), channel_id=1, source_target_pairs={{0,80},{16,96},{32,112},{1,81},{17,97},{33,113},{2,82},{18,98},{34... | collective-permute-start | bytes 12582920 | tf_op jit(solution)/shard_map/ppermute | solution.py:50
  16.6 3.3 collective-permute-start.3
  19.8 3.2 collective-permute-start.2
  23.0 1.9 collective-permute-start.1
  24.9 1.9 collective-permute-start
  26.9 79.0 %collective-permute-done.4 = bf16[32,512,128]{2,1,0:T(8,128)(2,1)} collective-permute-done((bf16[32,512,128]{2,1,0:T(8,128)(2,1)}, bf16[32,512,128]{2,1,0:T(8,128)(2,1)}, u32[]{:S(2)}, u32[]{:S(2)}) %collective-permute-start.4) | collective-permute-done | bytes 4194336 | tf_op jit(solution)/shard_map/ppermute | solution.py:50
  105.9 2.6 collective-permute-start.5
  108.5 176.4 %collective-permute-done.3 = bf16[32,512,128]{2,1,0:T(8,128)(2,1)} collective-permute-done((bf16[32,512,128]{2,1,0:T(8,128)(2,1)}, bf16[32,512,128]{2,1,0:T(8,128)(2,1)}, u32[]{:S(2)}, u32[]{:S(2)}) %collective-permute-start.3) | collective-permute-done | bytes 4194336 | tf_op jit(solution)/shard_map/ppermute | solution.py:50
  284.9 2.6 collective-permute-start.6
  287.7 6.7 %fusion.25 = f32[128,32,512]{2,0,1:T(8,128)} fusion(bf16[128,1024]{1,0:T(8,128)(2,1)S(1)} %fusion.8, s32[]{:T(128)S(6)} %select_n.29, bf16[128,32,512]{0,2,1:T(8,128)(2,1)} %copy.4), kind=kOutput, calls=%fused_computation.33 | convolution fusion | flops 536870912 | bytes 12615684 | tf_op jit(solution)/shard_map/ts,ijs->tij/dot_general | solution.py:45
  294.4 6.7 %fusion.15 = f32[128,32,512]{2,0,1:T(8,128)} fusion(bf16[32,512,128]{2,1,0:T(8,128)(2,1)} %collective-permute-done.4, bf16[128,1024]{1,0:T(8,128)(2,1)S(1)} %fusion.8, s32[]{:T(128)S(6)} %select_n.34), kind=kOutput, calls=%fused_computation.23 | convolution fusion | flops 536870912 | bytes 12615684 | tf_op jit(solution)/shard_map/ts,ijs->tij/dot_general | solution.py:45
  301.1 6.7 %fusion.17 = f32[128,32,512]{2,0,1:T(8,128)} fusion(bf16[32,512,128]{2,1,0:T(8,128)(2,1)} %collective-permute-done.3, bf16[128,1024]{1,0:T(8,128)(2,1)S(1)} %fusion.8, s32[]{:T(128)S(6)} %select_n.33), kind=kOutput, calls=%fused_computation.25 | convolution fusion | flops 536870912 | bytes 12615684 | tf_op jit(solution)/shard_map/ts,ijs->tij/dot_general | solution.py:45
  307.7 6.7 %fusion.19 = f32[128,32,512]{2,0,1:T(8,128)} fusion(bf16[32,512,128]{2,1,0:T(8,128)(2,1)} %collective-permute-done.2, bf16[128,1024]{1,0:T(8,128)(2,1)S(1)} %fusion.8, s32[]{:T(128)S(6)} %select_n.32), kind=kOutput, calls=%fused_computation.27 | convolution fusion | flops 536870912 | bytes 12615684 | tf_op jit(solution)/shard_map/ts,ijs->tij/dot_general | solution.py:45
  314.4 63.7 %collective-permute-done.1 = bf16[32,512,128]{2,1,0:T(8,128)(2,1)} collective-permute-done((bf16[32,512,128]{2,1,0:T(8,128)(2,1)}, bf16[32,512,128]{2,1,0:T(8,128)(2,1)}, u32[]{:S(2)}, u32[]{:S(2)}) %collective-permute-start.1) | collective-permute-done | bytes 4194336 | tf_op jit(solution)/shard_map/ppermute | solution.py:50
  378.1 6.7 %fusion.21 = f32[128,32,512]{2,0,1:T(8,128)} fusion(bf16[32,512,128]{2,1,0:T(8,128)(2,1)} %collective-permute-done.1, bf16[128,1024]{1,0:T(8,128)(2,1)S(1)} %fusion.8, s32[]{:T(128)S(6)} %select_n.31), kind=kOutput, calls=%fused_computation.29 | convolution fusion | flops 536870912 | bytes 12615684 | tf_op jit(solution)/shard_map/ts,ijs->tij/dot_general | solution.py:45
  384.7 71.6 %collective-permute-done = bf16[32,512,128]{2,1,0:T(8,128)(2,1)} collective-permute-done((bf16[32,512,128]{2,1,0:T(8,128)(2,1)}, bf16[32,512,128]{2,1,0:T(8,128)(2,1)}, u32[]{:S(2)}, u32[]{:S(2)}) %collective-permute-start) | collective-permute-done | bytes 4194336 | tf_op jit(solution)/shard_map/ppermute | solution.py:50
  456.4 6.7 %fusion.23 = f32[128,32,512]{2,0,1:T(8,128)} fusion(bf16[32,512,128]{2,1,0:T(8,128)(2,1)} %collective-permute-done, bf16[128,1024]{1,0:T(8,128)(2,1)S(1)} %fusion.8, s32[]{:T(128)S(6)} %select_n.30), kind=kOutput, calls=%fused_computation.31 | convolution fusion | flops 536870912 | bytes 12615684 | tf_op jit(solution)/shard_map/ts,ijs->tij/dot_general | solution.py:45
  463.0 6.8 %fusion.13 = f32[128,32,512]{2,0,1:T(8,128)} fusion(bf16[32,512,128]{2,1,0:T(8,128)(2,1)} %collective-permute-done.5, bf16[128,1024]{1,0:T(8,128)(2,1)S(1)} %fusion.8, s32[]{:T(128)S(6)} %select_n.35), kind=kOutput, calls=%fused_computation.21 | convolution fusion | flops 536870912 | bytes 12615684 | tf_op jit(solution)/shard_map/ts,ijs->tij/dot_general | solution.py:45
  469.9 24.5 %add_add_fusion = f32[128,32,512]{2,0,1:T(8,128)} fusion(f32[128,32,512]{2,0,1:T(8,128)} %fusion.13, f32[128,32,512]{2,0,1:T(8,128)} %fusion.15, f32[128,32,512]{2,0,1:T(8,128)} %fusion.17, f32[128,32,512]{2,0,1:T(8,128)} %fusion.19, f32[128,32,512]{2,0,1:T(8,128)} %fusion.21, f32[128,32,512]{2,0,1:T(8,128)} %fusion.25, f32[128,32,512]{2,0,1:T(8,128)} %fusion.23, ...), kind=kOutput, calls=%fused_computation.16 | convolution fusion | flops 551550976 | bytes 71335936 | tf_op jit(solution)/shard_map/ts,ijs->tij/dot_general | solution.py:45
  494.3 1.1 fusion.45
  495.4 1.9 collective-permute-start.7
  497.3 5.9 %collective-permute-start.8 = (f32[128,1,512]{2,0,1:T(8,128)S(1)}, f32[128,1,512]{2,0,1:T(8,128)S(1)}, u32[]{:S(2)}, u32[]{:S(2)}) collective-permute-start(f32[128,1,512]{2,0,1:T(8,128)S(1)} %get-tuple-element.8), channel_id=1, source_target_pairs={{1,0},{2,1},{3,2},{4,3},{5,4},{6,5},{7,6},{8,7},{9,8},{10,9},{11,1... | collective-permute-start | bytes 786440 | tf_op jit(solution)/shard_map/ppermute | solution.py:15
  503.3 1.9 collective-permute-done.7
  505.2 1.8 collective-permute-done.8
  506.9 18.9 %fusion.2 = f32[128,32,512]{2,0,1:T(8,128)} fusion(f32[128,32,512]{2,0,1:T(8,128)} %add_add_fusion, f32[128,1,512]{2,0,1:T(8,128)S(1)} %collective-permute-done.8, f32[128,1,512]{2,0,1:T(8,128)S(1)} %collective-permute-done.7, f32[32,512]{1,0:T(8,128)S(1)} %broadcast_add_fusion), kind=kLoop, calls=%fused_computation.6 | loop fusion | flops 14680064 | bytes 17367040 | tf_op jit(solution)/shard_map/sub | solution.py:25
  526.9 5.9 %collective-permute-start.10 = (f32[128,1,512]{2,0,1:T(8,128)S(1)}, f32[128,1,512]{2,0,1:T(8,128)S(1)}, u32[]{:S(2)}, u32[]{:S(2)}) collective-permute-start(f32[128,1,512]{2,0,1:T(8,128)S(1)} %get-tuple-element.6), channel_id=1, source_target_pairs={{1,0},{2,1},{3,2},{4,3},{5,4},{6,5},{7,6},{8,7},{9,8},{10,9},{11,1... | collective-permute-start | bytes 786440 | tf_op jit(solution)/shard_map/ppermute | solution.py:15
  532.8 1.9 collective-permute-start.9
  534.8 1.9 collective-permute-done.10
  536.7 5.9 %collective-permute-done.9 = f32[128,1,512]{2,0,1:T(8,128)S(1)} collective-permute-done((f32[128,1,512]{2,0,1:T(8,128)S(1)}, f32[128,1,512]{2,0,1:T(8,128)S(1)}, u32[]{:S(2)}, u32[]{:S(2)}) %collective-permute-start.9) | collective-permute-done | bytes 262176 | tf_op jit(solution)/shard_map/ppermute | solution.py:14
  542.6 19.0 %fusion.5 = f32[128,32,512]{2,0,1:T(8,128)} fusion(f32[128,32,512]{2,0,1:T(8,128)} %fusion.2, f32[128,1,512]{2,0,1:T(8,128)S(1)} %collective-permute-done.10, f32[128,1,512]{2,0,1:T(8,128)S(1)} %collective-permute-done.9, f32[32,512]{1,0:T(8,128)S(1)} %broadcast_add_fusion), kind=kLoop, calls=%fused_computation.9 | loop fusion | flops 14680064 | bytes 17367040 | tf_op jit(solution)/shard_map/sub | solution.py:25
  561.6 11.6 %copy.5 = f32[128,32,512]{2,1,0:T(8,128)} copy(f32[128,32,512]{2,0,1:T(8,128)} %fusion.5) | data formatting | bytes 16777216 | tf_op jit(solution)/shard_map/sub | solution.py:25
  (11 shorter events, 1.2 us)
Async XLA Ops:
  0.0 287.5 %copy-start = (bf16[128,1024]{1,0:T(8,128)(2,1)S(1)}, bf16[128,1024]{1,0:T(8,128)(2,1)}, u32[]{:S(2)}) copy-start(bf16[128,1024]{1,0:T(8,128)(2,1)} %param.4) | copy-start | bytes 786436
  8.0 97.9 %collective-permute-start.4 = (bf16[32,512,128]{2,1,0:T(8,128)(2,1)}, bf16[32,512,128]{2,1,0:T(8,128)(2,1)}, u32[]{:S(2)}, u32[]{:S(2)}) collective-permute-start(bf16[32,512,128]{2,1,0:T(8,128)(2,1)} %bitcast.36), channel_id=1, source_target_pairs={{0,80},{16,96},{32,112},{1,81},{17,97},{33,113},{2,82},{18,98},{34... | collective-permute-start | bytes 12582920 | tf_op jit(solution)/shard_map/ppermute | solution.py:50
  16.6 268.4 %collective-permute-start.3 = (bf16[32,512,128]{2,1,0:T(8,128)(2,1)}, bf16[32,512,128]{2,1,0:T(8,128)(2,1)}, u32[]{:S(2)}, u32[]{:S(2)}) collective-permute-start(bf16[32,512,128]{2,1,0:T(8,128)(2,1)} %bitcast.37), channel_id=1, source_target_pairs={{0,64},{16,80},{32,96},{48,112},{1,65},{17,81},{33,97},{49,113},{2... | collective-permute-start | bytes 12582920 | tf_op jit(solution)/shard_map/ppermute | solution.py:50
  19.8 287.9 %collective-permute-start.2 = (bf16[32,512,128]{2,1,0:T(8,128)(2,1)}, bf16[32,512,128]{2,1,0:T(8,128)(2,1)}, u32[]{:S(2)}, u32[]{:S(2)}) collective-permute-start(bf16[32,512,128]{2,1,0:T(8,128)(2,1)} %bitcast.38), channel_id=1, source_target_pairs={{0,48},{16,64},{32,80},{48,96},{64,112},{1,49},{17,65},{33,81},{49... | collective-permute-start | bytes 12582920 | tf_op jit(solution)/shard_map/ppermute | solution.py:50
  23.0 355.0 %collective-permute-start.1 = (bf16[32,512,128]{2,1,0:T(8,128)(2,1)}, bf16[32,512,128]{2,1,0:T(8,128)(2,1)}, u32[]{:S(2)}, u32[]{:S(2)}) collective-permute-start(bf16[32,512,128]{2,1,0:T(8,128)(2,1)} %bitcast.39), channel_id=1, source_target_pairs={{0,32},{16,48},{32,64},{48,80},{64,96},{80,112},{1,33},{17,49},{33... | collective-permute-start | bytes 12582920 | tf_op jit(solution)/shard_map/ppermute | solution.py:50
  24.9 431.4 %collective-permute-start = (bf16[32,512,128]{2,1,0:T(8,128)(2,1)}, bf16[32,512,128]{2,1,0:T(8,128)(2,1)}, u32[]{:S(2)}, u32[]{:S(2)}) collective-permute-start(bf16[32,512,128]{2,1,0:T(8,128)(2,1)} %bitcast.40), channel_id=1, source_target_pairs={{0,16},{16,32},{32,48},{48,64},{64,80},{80,96},{96,112},{1,17},{17... | collective-permute-start | bytes 12582920 | tf_op jit(solution)/shard_map/ppermute | solution.py:50
  105.9 357.1 %collective-permute-start.5 = (bf16[32,512,128]{2,1,0:T(8,128)(2,1)}, bf16[32,512,128]{2,1,0:T(8,128)(2,1)}, u32[]{:S(2)}, u32[]{:S(2)}) collective-permute-start(bf16[32,512,128]{2,1,0:T(8,128)(2,1)} %bitcast.41), channel_id=1, source_target_pairs={{0,96},{16,112},{1,97},{17,113},{2,98},{18,114},{3,99},{19,115},{4... | collective-permute-start | bytes 12582920 | tf_op jit(solution)/shard_map/ppermute | solution.py:50
  284.9 184.9 %collective-permute-start.6 = (bf16[32,512,128]{2,1,0:T(8,128)(2,1)}, bf16[32,512,128]{2,1,0:T(8,128)(2,1)}, u32[]{:S(2)}, u32[]{:S(2)}) collective-permute-start(bf16[32,512,128]{2,1,0:T(8,128)(2,1)} %bitcast.42), channel_id=1, source_target_pairs={{0,112},{1,113},{2,114},{3,115},{4,116},{5,117},{6,118},{7,119},{8... | collective-permute-start | bytes 12582920 | tf_op jit(solution)/shard_map/ppermute | solution.py:50
  469.9 33.4 %copy-start.1 = (f32[32,512]{1,0:T(8,128)S(1)}, f32[32,512]{1,0:T(8,128)}, u32[]{:S(2)}) copy-start(f32[32,512]{1,0:T(8,128)} %param.5) | copy-start | bytes 196612
  495.4 9.8 %collective-permute-start.7 = (f32[128,1,512]{2,0,1:T(8,128)S(1)}, f32[128,1,512]{2,0,1:T(8,128)S(1)}, u32[]{:S(2)}, u32[]{:S(2)}) collective-permute-start(f32[128,1,512]{2,0,1:T(8,128)S(1)} %get-tuple-element.7), channel_id=1, source_target_pairs={{0,1},{1,2},{2,3},{3,4},{4,5},{5,6},{6,7},{7,8},{8,9},{9,10},{10,1... | collective-permute-start | bytes 786440 | tf_op jit(solution)/shard_map/ppermute | solution.py:14
  497.3 9.6 %collective-permute-start.8 = (f32[128,1,512]{2,0,1:T(8,128)S(1)}, f32[128,1,512]{2,0,1:T(8,128)S(1)}, u32[]{:S(2)}, u32[]{:S(2)}) collective-permute-start(f32[128,1,512]{2,0,1:T(8,128)S(1)} %get-tuple-element.8), channel_id=1, source_target_pairs={{1,0},{2,1},{3,2},{4,3},{5,4},{6,5},{7,6},{8,7},{9,8},{10,9},{11,1... | collective-permute-start | bytes 786440 | tf_op jit(solution)/shard_map/ppermute | solution.py:15
  526.9 9.8 %collective-permute-start.10 = (f32[128,1,512]{2,0,1:T(8,128)S(1)}, f32[128,1,512]{2,0,1:T(8,128)S(1)}, u32[]{:S(2)}, u32[]{:S(2)}) collective-permute-start(f32[128,1,512]{2,0,1:T(8,128)S(1)} %get-tuple-element.6), channel_id=1, source_target_pairs={{1,0},{2,1},{3,2},{4,3},{5,4},{6,5},{7,6},{8,7},{9,8},{10,9},{11,1... | collective-permute-start | bytes 786440 | tf_op jit(solution)/shard_map/ppermute | solution.py:15
  532.8 9.8 %collective-permute-start.9 = (f32[128,1,512]{2,0,1:T(8,128)S(1)}, f32[128,1,512]{2,0,1:T(8,128)S(1)}, u32[]{:S(2)}, u32[]{:S(2)}) collective-permute-start(f32[128,1,512]{2,0,1:T(8,128)S(1)} %get-tuple-element.5), channel_id=1, source_target_pairs={{0,1},{1,2},{2,3},{3,4},{4,5},{5,6},{6,7},{7,8},{8,9},{9,10},{10,1... | collective-permute-start | bytes 786440 | tf_op jit(solution)/shard_map/ppermute | solution.py:14

commit v2 on v1

--- a/solution.py
+++ b/solution.py
@@ -2,6 +2,8 @@
 import jax.numpy as jnp
 from jax import lax
 from jax.sharding import PartitionSpec as P
+
+CHUNKS = 4
 
 
 def with_halo(x, sides, width):
@@ -30,25 +32,24 @@
 
 
 def body(field, factor, kappa):
-    epochs = field.shape[0]
+    epochs, slab, width = field.shape
     count = lax.axis_size("epoch")
     order = epochs * count
     me = lax.axis_index("epoch")
     global_rows = me * epochs + lax.broadcasted_iota(jnp.int32, (epochs, order), 0)
     global_cols = lax.broadcasted_iota(jnp.int32, (epochs, order), 1)
     lower = jnp.where(global_cols <= global_rows, factor, jnp.zeros_like(factor))
-    own = jnp.transpose(field, (1, 2, 0))
-
-    def term(block, source):
-        start = jnp.clip(source, 0, count - 1) * epochs
-        part = lax.dynamic_slice_in_dim(lower, start, epochs, 1)
-        return jnp.einsum("ts,ijs->tij", part, block, preferred_element_type=jnp.float32)
-
-    timed = term(own, me)
-    for shift in range(1, count):
-        pairs = [(e, e + shift) for e in range(count - shift)]
-        got = lax.ppermute(own, "epoch", pairs)
-        timed = timed + term(got, me - shift)
+    lower = lower.reshape(epochs, count, epochs)
+    step = slab // CHUNKS
+    parts = []
+    for c in range(CHUNKS):
+        rows = lax.slice_in_dim(field, c * step, (c + 1) * step, axis=1)
+        rows = jnp.transpose(rows, (1, 2, 0))
+        got = lax.all_gather(rows, "epoch", axis=0)
+        parts.append(
+            jnp.einsum("tes,eijs->tij", lower, got, preferred_element_type=jnp.float32)
+        )
+    timed = jnp.concatenate(parts, axis=1)
     first = stencil(single_rim(timed), kappa)
     return stencil(single_rim(first), kappa)
 

time: 574 us -> 532 us (0.927)
  the two profiles are of different devices: /device:TPU:40 before, /device:TPU:62 now
where the time goes in v2:
time: 532 us; the launch traced here: 525 us
  waiting for transfers between devices  399 us (75%)
  other arithmetic  40.8 us (8%)
  matrix products  32 us (6%)
  local copies, waits for them, and re-layouts  29.6 us (6%)
  between operations  13.2 us (2%)
  starting transfers between devices  9.93 us (2%)
    all_gather x4, waiting for transfers between devices, body(): got = lax.all_gather(rows, 'epoch', axis=0)  390 us
    sub x2, other arithmetic, stencil(): (kappa + 4.0) * center  36.9 us
    dot_general x4, matrix products, body(): jnp.einsum('tes,eijs->tij', lower, got, preferred_element_type=jnp.float32)  32 us
    sub x1, local copies, waits for them, and re-layouts, stencil(): (kappa + 4.0) * center  11.6 us
  transfers between devices with their start and end apart: 8, of which 7 were waited for; matrix products, arithmetic and copies ran while one was open for 8% of the time, Pallas kernels for 0%

profile of v2, /device:TPU:62, one launch (start us, length us, event | category | flops | bytes accessed | tf_op | source)
XLA Modules:
  0.0 524.6 jit_solution(4901286669514001718)
XLA Ops:
  6.5 3.4 fusion.14
  10.0 2.8 copy.42
  12.8 0.0 all-gather.9.cloned.1.call-start
  12.8 1.7 copy.39
  14.5 0.0 all-gather.11.cloned.1.call-start
  14.6 1.7 copy.40
  16.4 0.0 all-gather.13.cloned.1.call-start
  16.4 1.7 copy.41
  18.2 100.7 %all-gather.15.cloned.1.call-done = bf16[64,512,128]{2,1,0:T(8,128)(2,1)} async-done(((bf16[8,512,128]{2,1,0:T(8,128)(2,1)}), bf16[64,512,128]{2,1,0:T(8,128)(2,1)}) %all-gather.15.cloned.1.call-update) | async-done | bytes 8388624 | tf_op jit(solution)/shard_map/all_gather | solution.py:48
  118.9 6.2 %convolution_bitcast_fusion = f32[128,8,512]{2,0,1:T(8,128)S(1)} fusion(bf16[8,8,512,128]{3,2,1,0:T(8,128)(2,1)} %bitcast.77, bf16[128,1024]{1,0:T(8,128)(2,1)S(1)} %copy-done.3, s32[128]{0:T(128)S(1)} %iota_add_fusion), kind=kOutput, calls=%fused_computation.15 | convolution fusion | flops 1074003968 | bytes 10748416 | tf_op jit(solution)/shard_map/tes,eijs->tij/dot_general | solution.py:50
  125.1 1.9 collective-permute-start
  127.1 5.7 %collective-permute-done = f32[128,1,512]{2,0,1:T(8,128)S(1)} collective-permute-done((f32[128,1,512]{2,0,1:T(8,128)S(1)}, f32[128,1,512]{2,0,1:T(8,128)S(1)}, u32[]{:S(2)}, u32[]{:S(2)}) %collective-permute-start) | collective-permute-done | bytes 262176 | tf_op jit(solution)/shard_map/ppermute | solution.py:16
  132.8 0.7 constant_dynamic-update-slice_fusion.4
  133.6 92.7 %all-gather.9.cloned.1.call-done = bf16[64,512,128]{2,1,0:T(8,128)(2,1)} async-done(((bf16[8,512,128]{2,1,0:T(8,128)(2,1)}), bf16[64,512,128]{2,1,0:T(8,128)(2,1)}) %all-gather.9.cloned.1.call-update) | async-done | bytes 8388624 | tf_op jit(solution)/shard_map/all_gather | solution.py:48
  226.2 8.3 %constant_dynamic-update-slice_fusion.3 = (f32[128,33,512]{2,0,1:T(8,128)}, f32[128,33,512]{2,0,1:T(8,128)}, f32[128,8,512]{2,0,1:T(8,128)S(1)}) fusion(f32[128,33,512]{2,0,1:T(8,128)} %constant_dynamic-update-slice_fusion.4, bf16[8,8,512,128]{3,2,1,0:T(8,128)(2,1)} %bitcast.76, bf16[128,1024]{1,0:T(8,128)(2,1)S(1)} %copy-done.3, s32[128]{0:T(128)S(1)} %iota_add_fusion), kind=kOutput, calls=%fused_computation.31 | convolution fusion | flops 1074003968 | bytes 14942720 | tf_op jit(solution)/shard_map/tes,eijs->tij/dot_general | solution.py:50
  234.5 1.3 copy-done
  235.8 2.1 collective-permute-start.1
  237.9 98.2 %all-gather.11.cloned.1.call-done = bf16[64,512,128]{2,1,0:T(8,128)(2,1)} async-done(((bf16[8,512,128]{2,1,0:T(8,128)(2,1)}), bf16[64,512,128]{2,1,0:T(8,128)(2,1)}) %all-gather.11.cloned.1.call-update) | async-done | bytes 8388624 | tf_op jit(solution)/shard_map/all_gather | solution.py:48
  336.1 9.0 %constant_dynamic-update-slice_fusion.2 = (f32[128,33,512]{2,0,1:T(8,128)}, f32[128,33,512]{2,0,1:T(8,128)}, f32[128,8,512]{2,0,1:T(8,128)}) fusion(f32[128,33,512]{2,0,1:T(8,128)} %get-tuple-element.17, f32[128,33,512]{2,0,1:T(8,128)} %get-tuple-element.18, bf16[8,8,512,128]{3,2,1,0:T(8,128)(2,1)} %bitcast.74, bf16[128,1024]{1,0:T(8,128)(2,1)S(1)} %copy-done.3, ...), kind=kOutput, calls=%fused_computation.30 | convolution fusion | flops 1074003968 | bytes 14942720 | tf_op jit(solution)/shard_map/tes,eijs->tij/dot_general | solution.py:50
  345.1 98.2 %all-gather.13.cloned.1.call-done = bf16[64,512,128]{2,1,0:T(8,128)(2,1)} async-done(((bf16[8,512,128]{2,1,0:T(8,128)(2,1)}), bf16[64,512,128]{2,1,0:T(8,128)(2,1)}) %all-gather.13.cloned.1.call-update) | async-done | bytes 8388624 | tf_op jit(solution)/shard_map/all_gather | solution.py:48
  443.4 8.5 %constant_dynamic-update-slice_fusion.1 = (f32[128,33,512]{2,0,1:T(8,128)}, f32[128,33,512]{2,0,1:T(8,128)}, f32[128,8,512]{2,0,1:T(8,128)S(1)}) fusion(f32[128,33,512]{2,0,1:T(8,128)} %get-tuple-element.15, f32[128,33,512]{2,0,1:T(8,128)} %get-tuple-element.16, bf16[8,8,512,128]{3,2,1,0:T(8,128)(2,1)} %bitcast.75, bf16[128,1024]{1,0:T(8,128)(2,1)S(1)} %copy-done.3, ...), kind=kOutput, calls=%fused_computation.29 | convolution fusion | flops 1074003968 | bytes 14942720 | tf_op jit(solution)/shard_map/tes,eijs->tij/dot_general | solution.py:50
  451.8 3.9 pad_maximum_fusion.2
  455.7 2.7 constant_dynamic-update-slice_fusion
  458.4 0.7 constant_dynamic-update-slice_fusion.5
  459.1 17.9 %fusion.2 = f32[128,32,512]{2,0,1:T(8,128)} fusion(f32[128,32,512]{2,0,1:T(8,128)} %pad_maximum_fusion.2, f32[128,33,512]{2,0,1:T(8,128)} %constant_dynamic-update-slice_fusion.5, f32[128,33,512]{2,0,1:T(8,128)} %get-tuple-element.11, f32[32,512]{1,0:T(8,128)S(1)} %broadcast_add_fusion), kind=kLoop, calls=%fused_computation.6 | loop fusion | flops 10485760 | bytes 33619968 | tf_op jit(solution)/shard_map/sub | solution.py:27
  477.0 1.1 fusion.13
  478.1 1.9 collective-permute-start.2
  480.0 3.9 collective-permute-start.3
  483.9 1.9 collective-permute-done.2
  485.8 1.8 collective-permute-done.3
  487.6 18.9 %fusion.5 = f32[128,32,512]{2,0,1:T(8,128)} fusion(f32[128,32,512]{2,0,1:T(8,128)} %fusion.2, f32[128,1,512]{2,0,1:T(8,128)S(1)} %collective-permute-done.3, f32[128,1,512]{2,0,1:T(8,128)S(1)} %collective-permute-done.2, f32[32,512]{1,0:T(8,128)S(1)} %broadcast_add_fusion), kind=kLoop, calls=%fused_computation.9 | loop fusion | flops 14680064 | bytes 17367040 | tf_op jit(solution)/shard_map/sub | solution.py:27
  506.5 11.6 %copy.34 = f32[128,32,512]{2,1,0:T(8,128)} copy(f32[128,32,512]{2,0,1:T(8,128)} %fusion.5) | data formatting | bytes 16777216 | tf_op jit(solution)/shard_map/sub | solution.py:27
  (19 shorter events, 0.1 us)
Async XLA Ops:
  6.5 112.3 %all-gather.15.cloned.1.call-start = ((), (), s32[]{:S(2)}) async-start(), calls=%async_computation.3 | async-start | bytes 9437184 | tf_op jit(solution)/shard_map/all_gather | solution.py:48
  10.0 108.9 %copy-start.3 = (bf16[128,1024]{1,0:T(8,128)(2,1)S(1)}, bf16[128,1024]{1,0:T(8,128)(2,1)}, u32[]{:S(2)}) copy-start(bf16[128,1024]{1,0:T(8,128)(2,1)} %param.4) | copy-start | bytes 786436
  12.8 213.5 %all-gather.9.cloned.1.call-start = ((), (), s32[]{:S(2)}) async-start(), calls=%async_computation | async-start | bytes 9437184 | tf_op jit(solution)/shard_map/all_gather | solution.py:48
  14.5 321.6 %all-gather.11.cloned.1.call-start = ((), (), s32[]{:S(2)}) async-start(), calls=%async_computation.1 | async-start | bytes 9437184 | tf_op jit(solution)/shard_map/all_gather | solution.py:48
  14.6 112.5 %copy-start.4 = (f32[32,512]{1,0:T(8,128)S(1)}, f32[32,512]{1,0:T(8,128)}, u32[]{:S(2)}) copy-start(f32[32,512]{1,0:T(8,128)} %param.5) | copy-start | bytes 196612
  16.4 427.0 %all-gather.13.cloned.1.call-start = ((), (), s32[]{:S(2)}) async-start(), calls=%async_computation.2 | async-start | bytes 9437184 | tf_op jit(solution)/shard_map/all_gather | solution.py:48
  125.1 7.7 %collective-permute-start = (f32[128,1,512]{2,0,1:T(8,128)S(1)}, f32[128,1,512]{2,0,1:T(8,128)S(1)}, u32[]{:S(2)}, u32[]{:S(2)}) collective-permute-start(f32[128,1,512]{2,0,1:T(8,128)S(1)} %slice.68), channel_id=1, source_target_pairs={{0,1},{1,2},{2,3},{3,4},{4,5},{5,6},{6,7},{7,8},{8,9},{9,10},{10,1... | collective-permute-start | bytes 786440 | tf_op jit(solution)/shard_map/ppermute | solution.py:16
  234.5 1.3 copy-start
  235.8 222.5 %collective-permute-start.1 = (f32[128,1,512]{2,0,1:T(8,128)S(1)}, f32[128,1,512]{2,0,1:T(8,128)S(1)}, u32[]{:S(2)}, u32[]{:S(2)}) collective-permute-start(f32[128,1,512]{2,0,1:T(8,128)S(1)} %slice.70), channel_id=1, source_target_pairs={{1,0},{2,1},{3,2},{4,3},{5,4},{6,5},{7,6},{8,7},{9,8},{10,9},{11,1... | collective-permute-start | bytes 786440 | tf_op jit(solution)/shard_map/ppermute | solution.py:17
  443.3 8.5 %copy-start.1 = (f32[128,8,512]{2,0,1:T(8,128)S(1)}, f32[128,8,512]{2,0,1:T(8,128)}, u32[]{:S(2)}) copy-start(f32[128,8,512]{2,0,1:T(8,128)} %copy-done) | copy-start | bytes 6291460
  443.4 8.5 %copy-start.2 = (f32[128,8,512]{2,0,1:T(8,128)S(1)}, f32[128,8,512]{2,0,1:T(8,128)}, u32[]{:S(2)}) copy-start(f32[128,8,512]{2,0,1:T(8,128)} %get-tuple-element.20) | copy-start | bytes 6291460
  478.1 7.7 %collective-permute-start.2 = (f32[128,1,512]{2,0,1:T(8,128)S(1)}, f32[128,1,512]{2,0,1:T(8,128)S(1)}, u32[]{:S(2)}, u32[]{:S(2)}) collective-permute-start(f32[128,1,512]{2,0,1:T(8,128)S(1)} %get-tuple-element.5), channel_id=1, source_target_pairs={{0,1},{1,2},{2,3},{3,4},{4,5},{5,6},{6,7},{7,8},{8,9},{9,10},{10,1... | collective-permute-start | bytes 786440 | tf_op jit(solution)/shard_map/ppermute | solution.py:16
  480.0 7.5 %collective-permute-start.3 = (f32[128,1,512]{2,0,1:T(8,128)S(1)}, f32[128,1,512]{2,0,1:T(8,128)S(1)}, u32[]{:S(2)}, u32[]{:S(2)}) collective-permute-start(f32[128,1,512]{2,0,1:T(8,128)S(1)} %get-tuple-element.6), channel_id=1, source_target_pairs={{1,0},{2,1},{3,2},{4,3},{5,4},{6,5},{7,6},{8,7},{9,8},{10,9},{11,1... | collective-permute-start | bytes 786440 | tf_op jit(solution)/shard_map/ppermute | solution.py:17
Sparse Core Ops, SparseCore 0:
  12.9 105.9 all-gather.14
  121.2 104.9 all-gather.8
  228.6 107.4 all-gather.10
  338.3 104.9 all-gather.12

commit v3 on v1

--- a/solution.py
+++ b/solution.py
@@ -2,6 +2,8 @@
 import jax.numpy as jnp
 from jax import lax
 from jax.sharding import PartitionSpec as P
+
+GATHERED_ROWS = 16
 
 
 def with_halo(x, sides, width):
@@ -30,25 +32,28 @@
 
 
 def body(field, factor, kappa):
-    epochs = field.shape[0]
+    epochs, slab, width = field.shape
     count = lax.axis_size("epoch")
     order = epochs * count
     me = lax.axis_index("epoch")
     global_rows = me * epochs + lax.broadcasted_iota(jnp.int32, (epochs, order), 0)
     global_cols = lax.broadcasted_iota(jnp.int32, (epochs, order), 1)
     lower = jnp.where(global_cols <= global_rows, factor, jnp.zeros_like(factor))
+    lower = lower.reshape(epochs, count, epochs)
     own = jnp.transpose(field, (1, 2, 0))
-
-    def term(block, source):
-        start = jnp.clip(source, 0, count - 1) * epochs
-        part = lax.dynamic_slice_in_dim(lower, start, epochs, 1)
-        return jnp.einsum("ts,ijs->tij", part, block, preferred_element_type=jnp.float32)
-
-    timed = term(own, me)
+    head = own[:GATHERED_ROWS]
+    tail = own[GATHERED_ROWS:]
+    gathered = lax.all_gather(head, "epoch", axis=0)
+    slots = [tail]
     for shift in range(1, count):
         pairs = [(e, e + shift) for e in range(count - shift)]
-        got = lax.ppermute(own, "epoch", pairs)
-        timed = timed + term(got, me - shift)
+        slots.append(lax.ppermute(tail, "epoch", pairs))
+    stacked = jnp.stack(slots, axis=0)
+    source = jnp.clip(me - jnp.arange(count), 0, count - 1)
+    weights = jnp.take(lower, source, axis=1)
+    part_a = jnp.einsum("tes,eijs->tij", lower, gathered, preferred_element_type=jnp.float32)
+    part_b = jnp.einsum("tes,eijs->tij", weights, stacked, preferred_element_type=jnp.float32)
+    timed = jnp.concatenate([part_a, part_b], axis=1)
     first = stencil(single_rim(timed), kappa)
     return stencil(single_rim(first), kappa)
 

time: 574 us -> 463 us (0.81)
  the two profiles are of different devices: /device:TPU:40 before, /device:TPU:62 now
where the time goes in v3:
time: 463 us; the launch traced here: 455 us
  waiting for transfers between devices  293 us (63%)
  local copies, waits for them, and re-layouts  56.1 us (12%)
  other arithmetic  37.8 us (8%)
  starting transfers between devices  27.6 us (6%)
  matrix products  26.6 us (6%)
  between operations  13.6 us (3%)
    ppermute x7, waiting for transfers between devices, body(): slots.append(lax.ppermute(tail, 'epoch', pairs))  156 us
    all_gather x1, waiting for transfers between devices, body(): gathered = lax.all_gather(head, 'epoch', axis=0)  132 us
    unnamed x19, local copies, waits for them, and re-layouts  33.7 us
    sub x2, other arithmetic, stencil(): (kappa + 4.0) * center  29.2 us
    ppermute x7, starting transfers between devices, body(): slots.append(lax.ppermute(tail, 'epoch', pairs))  18.6 us
    dot_general x1, matrix products, body(): jnp.einsum('tes,eijs->tij', weights, stacked, preferred_element_type=jnp....  13.4 us
    dot_general x1, matrix products, body(): jnp.einsum('tes,eijs->tij', lower, gathered, preferred_element_type=jnp.f...  13.2 us
    sub x1, local copies, waits for them, and re-layouts, stencil(): (kappa + 4.0) * center  11.6 us
  transfers between devices with their start and end apart: 12, of which 5 were waited for; matrix products, arithmetic and copies ran while one was open for 14% of the time, Pallas kernels for 0%

profile of v3, /device:TPU:62, one launch (start us, length us, event | category | flops | bytes accessed | tf_op | source)
XLA Modules:
  0.0 455.0 jit_solution(17006859426269067331)
XLA Ops:
  6.5 7.9 %copy.38 = bf16[128,32,512]{0,2,1:T(8,128)(2,1)} copy(bf16[128,32,512]{2,1,0:T(8,128)(2,1)} %param.3) | data formatting | bytes 8388608 | tf_op args[0]
  14.4 4.6 %fusion.16 = (bf16[16,512,128]{2,1,0:T(8,128)(2,1)}, bf16[16,512,128]{2,1,0:T(8,128)(2,1)}) fusion(bf16[32,512,128]{2,1,0:T(8,128)(2,1)} %bitcast.55), kind=kLoop, calls=%fused_computation.45 | loop fusion | bytes 8388608 | tf_op jit(solution)/shard_map/slice | solution.py:44
  19.1 4.5 collective-permute-start
  23.6 3.5 collective-permute-start.1
  27.2 3.0 collective-permute-start.2
  30.2 2.7 collective-permute-start.3
  34.0 3.8 bitcast_dynamic-update-slice_fusion.6
  37.8 56.0 %collective-permute-done = bf16[16,512,128]{2,1,0:T(8,128)(2,1)} collective-permute-done((bf16[16,512,128]{2,1,0:T(8,128)(2,1)}, bf16[16,512,128]{2,1,0:T(8,128)(2,1)}, u32[]{:S(2)}, u32[]{:S(2)}) %collective-permute-start) | collective-permute-done | bytes 2097184 | tf_op jit(solution)/shard_map/ppermute | solution.py:50
  93.8 2.0 collective-permute-start.5
  95.8 99.9 %collective-permute-done.1 = bf16[16,512,128]{2,1,0:T(8,128)(2,1)} collective-permute-done((bf16[16,512,128]{2,1,0:T(8,128)(2,1)}, bf16[16,512,128]{2,1,0:T(8,128)(2,1)}, u32[]{:S(2)}, u32[]{:S(2)}) %collective-permute-start.1) | collective-permute-done | bytes 2097184 | tf_op jit(solution)/shard_map/ppermute | solution.py:50
  195.7 2.0 collective-permute-start.6
  198.6 3.3 bitcast_dynamic-update-slice_fusion.5
  201.9 3.3 bitcast_dynamic-update-slice_fusion.4
  205.3 3.4 bitcast_dynamic-update-slice_fusion.3
  208.6 3.4 bitcast_dynamic-update-slice_fusion.2
  212.0 1.6 bitcast_dynamic-update-slice_fusion.1
  213.6 3.4 bitcast_dynamic-update-slice_fusion
  217.0 3.4 bitcast_dynamic-update-slice_fusion.7
  220.4 13.4 %convolution_bitcast_fusion.1 = f32[128,16,512]{2,0,1:T(8,128)} fusion(bf16[8,16,512,128]{3,2,0,1:T(8,128)(2,1)} %bitcast_dynamic-update-slice_fusion.7, bf16[8,128,128]{2,1,0:T(8,128)(2,1)S(1)} %gather_fusion, pred[8]{0:T(512)(128)(4,1)S(1)} %compare_and_fusion), kind=kOutput, calls=%fused_computation.21 | convolution fusion | flops 2147614720 | bytes 21233672 | tf_op jit(solution)/shard_map/tes,eijs->tij/dot_general | solution.py:55
  234.8 1.9 collective-permute-start.7
  236.7 131.5 %all-gather.3.cloned.1.call-done = bf16[128,512,128]{2,1,0:T(8,128)(2,1)} async-done(((bf16[16,512,128]{2,1,0:T(8,128)(2,1)}), bf16[128,512,128]{2,1,0:T(8,128)(2,1)}) %all-gather.3.cloned.1.call-update) | async-done | bytes 16777232 | tf_op jit(solution)/shard_map/all_gather | solution.py:46
  368.2 13.2 %convolution_bitcast_fusion = f32[128,16,512]{2,0,1:T(8,128)} fusion(bf16[128,8,128,1]{0,2,3,1:T(8,128)(2,1)S(1)} %bitcast.59, bf16[8,16,512,128]{3,2,1,0:T(8,128)(2,1)} %bitcast.57), kind=kOutput, calls=%fused_computation.20 | convolution fusion | flops 2147483648 | bytes 21233664 | tf_op jit(solution)/shard_map/tes,eijs->tij/dot_general | solution.py:54
  382.4 2.5 collective-permute-start.8
  384.9 8.5 %pad_maximum_fusion.6 = f32[128,32,512]{2,0,1:T(8,128)} fusion(f32[128,16,512]{2,0,1:T(8,128)} %convolution_bitcast_fusion.1, f32[128,16,512]{2,0,1:T(8,128)} %convolution_bitcast_fusion), kind=kLoop, calls=%fused_computation.19 | loop fusion | flops 2097152 | bytes 16777216 | tf_op jit(solution)/shard_map/concatenate | solution.py:56
  393.4 10.3 %fusion.2 = f32[128,32,512]{2,0,1:T(8,128)S(1)} fusion(f32[128,32,512]{2,0,1:T(8,128)} %pad_maximum_fusion.6, f32[128,1,512]{2,0,1:T(8,128)S(1)} %collective-permute-done.8, f32[128,16,512]{2,0,1:T(8,128)S(1)} %copy-done, f32[128,16,512]{2,0,1:T(8,128)S(1)} %copy-done.1, f32[128,1,512]{2,0,1:T(8,128)S(1)} %collective-permute-done.7, ...), kind=kLoop, calls=%fused_computation.7 | loop fusion | flops 18874368 | bytes 25755648 | tf_op jit(solution)/shard_map/sub | solution.py:27
  403.8 3.4 copy-done.2
  407.2 2.7 collective-permute-start.10
  409.9 1.9 collective-permute-start.9
  411.9 1.9 collective-permute-done.10
  413.8 3.8 collective-permute-done.9
  417.6 18.9 %fusion.5 = f32[128,32,512]{2,0,1:T(8,128)} fusion(f32[128,32,512]{2,0,1:T(8,128)} %copy-done.2, f32[128,1,512]{2,0,1:T(8,128)S(1)} %collective-permute-done.10, f32[128,1,512]{2,0,1:T(8,128)S(1)} %collective-permute-done.9, f32[32,512]{1,0:T(8,128)S(1)} %broadcast_add_fusion), kind=kLoop, calls=%fused_computation.10 | loop fusion | flops 14680064 | bytes 17367040 | tf_op jit(solution)/shard_map/sub | solution.py:27
  436.5 11.6 %copy.49 = f32[128,32,512]{2,1,0:T(8,128)} copy(f32[128,32,512]{2,0,1:T(8,128)} %fusion.5) | data formatting | bytes 16777216 | tf_op jit(solution)/shard_map/sub | solution.py:27
  (31 shorter events, 3.9 us)
Async XLA Ops:
  6.5 27.1 %copy-start.3 = (bf16[128,1024]{1,0:T(8,128)(2,1)S(1)}, bf16[128,1024]{1,0:T(8,128)(2,1)}, u32[]{:S(2)}) copy-start(bf16[128,1024]{1,0:T(8,128)(2,1)} %param.4) | copy-start | bytes 786436
  6.5 361.7 %all-gather.3.cloned.1.call-start = ((), (), s32[]{:S(2)}) async-start(), calls=%async_computation | async-start | bytes 18874368 | tf_op jit(solution)/shard_map/all_gather | solution.py:46
  14.4 81.4 %copy-start.4 = (f32[32,512]{1,0:T(8,128)S(1)}, f32[32,512]{1,0:T(8,128)}, u32[]{:S(2)}) copy-start(f32[32,512]{1,0:T(8,128)} %param.5) | copy-start | bytes 196612
  19.1 74.7 %collective-permute-start = (bf16[16,512,128]{2,1,0:T(8,128)(2,1)}, bf16[16,512,128]{2,1,0:T(8,128)(2,1)}, u32[]{:S(2)}, u32[]{:S(2)}) collective-permute-start(bf16[16,512,128]{2,1,0:T(8,128)(2,1)} %get-tuple-element.8), channel_id=1, source_target_pairs={{0,16},{16,32},{32,48},{48,64},{64,80},{80,96},{96,112},{1,17},{17... | collective-permute-start | bytes 6291464 | tf_op jit(solution)/shard_map/ppermute | solution.py:50
  23.6 172.1 %collective-permute-start.1 = (bf16[16,512,128]{2,1,0:T(8,128)(2,1)}, bf16[16,512,128]{2,1,0:T(8,128)(2,1)}, u32[]{:S(2)}, u32[]{:S(2)}) collective-permute-start(bf16[16,512,128]{2,1,0:T(8,128)(2,1)} %get-tuple-element.8), channel_id=1, source_target_pairs={{0,32},{16,48},{32,64},{48,80},{64,96},{80,112},{1,33},{17,49},{33... | collective-permute-start | bytes 6291464 | tf_op jit(solution)/shard_map/ppermute | solution.py:50
  27.2 178.1 %collective-permute-start.2 = (bf16[16,512,128]{2,1,0:T(8,128)(2,1)}, bf16[16,512,128]{2,1,0:T(8,128)(2,1)}, u32[]{:S(2)}, u32[]{:S(2)}) collective-permute-start(bf16[16,512,128]{2,1,0:T(8,128)(2,1)} %get-tuple-element.8), channel_id=1, source_target_pairs={{0,48},{16,64},{32,80},{48,96},{64,112},{1,49},{17,65},{33,81},{49... | collective-permute-start | bytes 6291464 | tf_op jit(solution)/shard_map/ppermute | solution.py:50
  30.2 178.4 %collective-permute-start.3 = (bf16[16,512,128]{2,1,0:T(8,128)(2,1)}, bf16[16,512,128]{2,1,0:T(8,128)(2,1)}, u32[]{:S(2)}, u32[]{:S(2)}) collective-permute-start(bf16[16,512,128]{2,1,0:T(8,128)(2,1)} %get-tuple-element.8), channel_id=1, source_target_pairs={{0,64},{16,80},{32,96},{48,112},{1,65},{17,81},{33,97},{49,113},{2... | collective-permute-start | bytes 6291464 | tf_op jit(solution)/shard_map/ppermute | solution.py:50
  32.9 179.1 %collective-permute-start.4 = (bf16[16,512,128]{2,1,0:T(8,128)(2,1)}, bf16[16,512,128]{2,1,0:T(8,128)(2,1)S(1)}, u32[]{:S(2)}, u32[]{:S(2)}) collective-permute-start(bf16[16,512,128]{2,1,0:T(8,128)(2,1)} %get-tuple-element.8), channel_id=1, source_target_pairs={{0,80},{16,96},{32,112},{1,81},{17,97},{33,113},{2,82},{18,98},{34... | collective-permute-start | bytes 6291464 | tf_op jit(solution)/shard_map/ppermute | solution.py:50
  93.8 119.8 %collective-permute-start.5 = (bf16[16,512,128]{2,1,0:T(8,128)(2,1)}, bf16[16,512,128]{2,1,0:T(8,128)(2,1)}, u32[]{:S(2)}, u32[]{:S(2)}) collective-permute-start(bf16[16,512,128]{2,1,0:T(8,128)(2,1)} %get-tuple-element.8), channel_id=1, source_target_pairs={{0,96},{16,112},{1,97},{17,113},{2,98},{18,114},{3,99},{19,115},{4... | collective-permute-start | bytes 6291464 | tf_op jit(solution)/shard_map/ppermute | solution.py:50
  195.7 21.3 %collective-permute-start.6 = (bf16[16,512,128]{2,1,0:T(8,128)(2,1)}, bf16[16,512,128]{2,1,0:T(8,128)(2,1)}, u32[]{:S(2)}, u32[]{:S(2)}) collective-permute-start(bf16[16,512,128]{2,1,0:T(8,128)(2,1)} %get-tuple-element.8), channel_id=1, source_target_pairs={{0,112},{1,113},{2,114},{3,115},{4,116},{5,117},{6,118},{7,119},{8... | collective-permute-start | bytes 6291464 | tf_op jit(solution)/shard_map/ppermute | solution.py:50
  234.8 158.6 %collective-permute-start.7 = (f32[128,1,512]{2,0,1:T(8,128)S(1)}, f32[128,1,512]{2,0,1:T(8,128)S(1)}, u32[]{:S(2)}, u32[]{:S(2)}) collective-permute-start(f32[128,1,512]{2,0,1:T(8,128)S(1)} %slice.64), channel_id=1, source_target_pairs={{0,1},{1,2},{2,3},{3,4},{4,5},{5,6},{6,7},{7,8},{8,9},{9,10},{10,1... | collective-permute-start | bytes 786440 | tf_op jit(solution)/shard_map/ppermute | solution.py:16
  382.4 11.0 %copy-start = (f32[128,16,512]{2,0,1:T(8,128)S(1)}, f32[128,16,512]{2,0,1:T(8,128)}, u32[]{:S(2)}) copy-start(f32[128,16,512]{2,0,1:T(8,128)} %convolution_bitcast_fusion.1) | copy-start | bytes 12582916
  382.4 11.0 %copy-start.1 = (f32[128,16,512]{2,0,1:T(8,128)S(1)}, f32[128,16,512]{2,0,1:T(8,128)}, u32[]{:S(2)}) copy-start(f32[128,16,512]{2,0,1:T(8,128)} %convolution_bitcast_fusion) | copy-start | bytes 12582916
  382.4 11.0 %collective-permute-start.8 = (f32[128,1,512]{2,0,1:T(8,128)S(1)}, f32[128,1,512]{2,0,1:T(8,128)S(1)}, u32[]{:S(2)}, u32[]{:S(2)}) collective-permute-start(f32[128,1,512]{2,0,1:T(8,128)S(1)} %slice.65), channel_id=1, source_target_pairs={{1,0},{2,1},{3,2},{4,3},{5,4},{6,5},{7,6},{8,7},{9,8},{10,9},{11,1... | collective-permute-start | bytes 786440 | tf_op jit(solution)/shard_map/ppermute | solution.py:17
  403.8 3.4 copy-start.2
  407.2 6.6 %collective-permute-start.10 = (f32[128,1,512]{2,0,1:T(8,128)S(1)}, f32[128,1,512]{2,0,1:T(8,128)S(1)}, u32[]{:S(2)}, u32[]{:S(2)}) collective-permute-start(f32[128,1,512]{2,0,1:T(8,128)S(1)} %get-tuple-element.6), channel_id=1, source_target_pairs={{1,0},{2,1},{3,2},{4,3},{5,4},{6,5},{7,6},{8,7},{9,8},{10,9},{11,1... | collective-permute-start | bytes 786440 | tf_op jit(solution)/shard_map/ppermute | solution.py:17
  409.9 7.7 %collective-permute-start.9 = (f32[128,1,512]{2,0,1:T(8,128)S(1)}, f32[128,1,512]{2,0,1:T(8,128)S(1)}, u32[]{:S(2)}, u32[]{:S(2)}) collective-permute-start(f32[128,1,512]{2,0,1:T(8,128)S(1)} %get-tuple-element.5), channel_id=1, source_target_pairs={{0,1},{1,2},{2,3},{3,4},{4,5},{5,6},{6,7},{7,8},{8,9},{9,10},{10,1... | collective-permute-start | bytes 786440 | tf_op jit(solution)/shard_map/ppermute | solution.py:16
Sparse Core Ops, SparseCore 0:
  19.2 348.9 all-gather.2

commit v4 on v3

v4 whole, which is shorter than its diff:
```python
import jax
import jax.numpy as jnp
from jax import lax
from jax.sharding import PartitionSpec as P

GATHERED_ROWS = 16
HALO = 2


def neighbours(x, width):
    size = lax.axis_size("row")
    up = [(i, i + 1) for i in range(size - 1)]
    down = [(i + 1, i) for i in range(size - 1)]
    above = lax.ppermute(x[x.shape[0] - width:], "row", up)
    below = lax.ppermute(x[:width], "row", down)
    return above, below


def side_sum(v):
    padded = jnp.pad(v, [(0, 0)] * (v.ndim - 1) + [(1, 1)])
    return padded[..., :-2] + padded[..., 2:]


def body(field, factor, kappa):
    epochs, slab, width = field.shape
    count = lax.axis_size("epoch")
    order = epochs * count
    me = lax.axis_index("epoch")
    global_rows = me * epochs + lax.broadcasted_iota(jnp.int32, (epochs, order), 0)
    global_cols = lax.broadcasted_iota(jnp.int32, (epochs, order), 1)
    lower = jnp.where(global_cols <= global_rows, factor, jnp.zeros_like(factor))
    lower = lower.reshape(epochs, count, epochs)
    own = jnp.transpose(field, (1, 2, 0))
    head = own[:GATHERED_ROWS]
    tail = own[GATHERED_ROWS:]
    gathered = lax.all_gather(head, "epoch", axis=0)
    slots = [tail]
    for shift in range(1, count):
        pairs = [(e, e + shift) for e in range(count - shift)]
        slots.append(lax.ppermute(tail, "epoch", pairs))
    stacked = jnp.stack(slots, axis=0)
    source = jnp.clip(me - jnp.arange(count), 0, count - 1)
    weights = jnp.take(lower, source, axis=1)
    part_a = jnp.einsum("tes,eijs->itj", lower, gathered, preferred_element_type=jnp.float32)
    part_b = jnp.einsum("tes,eijs->itj", weights, stacked, preferred_element_type=jnp.float32)
    timed = jnp.concatenate([part_a, part_b], axis=0)

    above, below = neighbours(timed, HALO)
    k_above, k_below = neighbours(kappa, 1)
    ext = jnp.concatenate([above, timed, below], axis=0)
    gain = jnp.concatenate([k_above, kappa, k_below], axis=0)[:, None, :] + 4.0
    once = gain * ext[1:-1] - (ext[:-2] + ext[2:] + side_sum(ext[1:-1]))
    pos = lax.axis_index("row")
    rows = lax.broadcasted_iota(jnp.int32, (slab + 2, 1, 1), 0)
    outside = ((rows == 0) & (pos == 0)) | ((rows == slab + 1) & (pos == lax.axis_size("row") - 1))
    once = jnp.where(outside, jnp.zeros_like(once), once)
    product = gain[1:-1] * once[1:-1] - (once[:-2] + once[2:] + side_sum(once[1:-1]))
    return jnp.transpose(product, (1, 0, 2))


def solution(mesh):
    in_specs = (P("epoch", "row", None), P("epoch", None), P("row", None))
    out_specs = P("epoch", "row", None)
    return jax.shard_map(body, mesh=mesh, in_specs=in_specs, out_specs=out_specs, check_vma=False)
```

time: 463 us -> 449 us (0.970)
  the two profiles are of different devices: /device:TPU:62 before, /device:TPU:1 now
where the time goes in v4:
time: 449 us; the launch traced here: 448 us
  waiting for transfers between devices  290 us (65%)
  local copies, waits for them, and re-layouts  54.8 us (12%)
  starting transfers between devices  41.5 us (9%)
  other arithmetic  28.9 us (6%)
  matrix products  18.6 us (4%)
  between operations  13.6 us (3%)
    ppermute x7, waiting for transfers between devices, body(): slots.append(lax.ppermute(tail, 'epoch', pairs))  180 us
    all_gather x1, waiting for transfers between devices, body(): gathered = lax.all_gather(head, 'epoch', axis=0)  107 us
    unnamed x23, local copies, waits for them, and re-layouts  33.3 us
    ppermute x7, starting transfers between devices, body(): slots.append(lax.ppermute(tail, 'epoch', pairs))  30.4 us
    select_n x1, other arithmetic, body(): once = jnp.where(outside, jnp.zeros_like(once), once)  13.8 us
    transpose x1, local copies, waits for them, and re-layouts, body(): return jnp.transpose(product, (1, 0, 2))  10.3 us
    dot_general x1, matrix products, body(): jnp.einsum('tes,eijs->itj', lower, gathered, preferred_element_type=jnp.f...  10.1 us
  transfers between devices with their start and end apart: 12, of which 6 were waited for; matrix products, arithmetic and copies ran while one was open for 11% of the time, Pallas kernels for 0%

profile of v4, /device:TPU:1, one launch (start us, length us, event | category | flops | bytes accessed | tf_op | source)
XLA Modules:
  0.0 447.6 jit_solution(9884737661501636085)
XLA Ops:
  6.5 7.9 %copy.54 = bf16[128,32,512]{0,2,1:T(8,128)(2,1)} copy(bf16[128,32,512]{2,1,0:T(8,128)(2,1)} %param.3) | data formatting | bytes 8388608 | tf_op args[0]
  14.4 4.8 %fusion.15 = (bf16[16,512,128]{2,1,0:T(8,128)(2,1)}, bf16[16,512,128]{2,1,0:T(8,128)(2,1)}) fusion(bf16[32,512,128]{2,1,0:T(8,128)(2,1)} %bitcast.65), kind=kLoop, calls=%fused_computation.41 | loop fusion | bytes 8388608 | tf_op jit(solution)/shard_map/slice | solution.py:34
  19.2 7.0 %collective-permute-start.2 = (bf16[16,512,128]{2,1,0:T(8,128)(2,1)}, bf16[16,512,128]{2,1,0:T(8,128)(2,1)}, u32[]{:S(2)}, u32[]{:S(2)}) collective-permute-start(bf16[16,512,128]{2,1,0:T(8,128)(2,1)} %get-tuple-element.6), channel_id=1, source_target_pairs={{0,16},{16,32},{32,48},{48,64},{64,80},{80,96},{96,112},{1,17},{17... | collective-permute-start | bytes 6291464 | tf_op jit(solution)/shard_map/ppermute | solution.py:40
  26.2 3.6 collective-permute-start.3
  29.8 4.4 collective-permute-start.4
  34.1 2.8 collective-permute-start.5
  38.6 3.4 bitcast_dynamic-update-slice_fusion.6
  42.0 50.0 %collective-permute-done.2 = bf16[16,512,128]{2,1,0:T(8,128)(2,1)} collective-permute-done((bf16[16,512,128]{2,1,0:T(8,128)(2,1)}, bf16[16,512,128]{2,1,0:T(8,128)(2,1)}, u32[]{:S(2)}, u32[]{:S(2)}) %collective-permute-start.2) | collective-permute-done | bytes 2097184 | tf_op jit(solution)/shard_map/ppermute | solution.py:40
  91.9 8.7 %collective-permute-start.7 = (bf16[16,512,128]{2,1,0:T(8,128)(2,1)}, bf16[16,512,128]{2,1,0:T(8,128)(2,1)}, u32[]{:S(2)}, u32[]{:S(2)}) collective-permute-start(bf16[16,512,128]{2,1,0:T(8,128)(2,1)} %get-tuple-element.6), channel_id=1, source_target_pairs={{0,96},{16,112},{1,97},{17,113},{2,98},{18,114},{3,99},{19,115},{4... | collective-permute-start | bytes 6291464 | tf_op jit(solution)/shard_map/ppermute | solution.py:40
  100.7 94.5 %collective-permute-done.3 = bf16[16,512,128]{2,1,0:T(8,128)(2,1)} collective-permute-done((bf16[16,512,128]{2,1,0:T(8,128)(2,1)}, bf16[16,512,128]{2,1,0:T(8,128)(2,1)}, u32[]{:S(2)}, u32[]{:S(2)}) %collective-permute-start.3) | collective-permute-done | bytes 2097184 | tf_op jit(solution)/shard_map/ppermute | solution.py:40
  195.2 2.6 collective-permute-start.8
  198.7 3.4 bitcast_dynamic-update-slice_fusion.5
  202.0 3.3 bitcast_dynamic-update-slice_fusion.4
  205.4 3.4 bitcast_dynamic-update-slice_fusion.3
  208.7 31.5 %collective-permute-done.5 = bf16[16,512,128]{2,1,0:T(8,128)(2,1)} collective-permute-done((bf16[16,512,128]{2,1,0:T(8,128)(2,1)}, bf16[16,512,128]{2,1,0:T(8,128)(2,1)}, u32[]{:S(2)}, u32[]{:S(2)}) %collective-permute-start.5) | collective-permute-done | bytes 2097184 | tf_op jit(solution)/shard_map/ppermute | solution.py:40
  240.2 3.4 bitcast_dynamic-update-slice_fusion.2
  245.3 4.2 collective-permute-done.7
  249.4 3.4 bitcast_dynamic-update-slice_fusion
  252.8 4.0 bitcast_dynamic-update-slice_fusion.7
  256.8 8.5 %convolution_bitcast_fusion.1 = f32[16,128,512]{1,2,0:T(8,128)S(1)} fusion(bf16[8,16,512,128]{3,2,0,1:T(8,128)(2,1)} %bitcast_dynamic-update-slice_fusion.7, bf16[8,128,128]{2,1,0:T(8,128)(2,1)S(1)} %gather_fusion, pred[8]{0:T(512)(128)(4,1)S(1)} %compare_and_fusion), kind=kOutput, calls=%fused_computation.13 | convolution fusion | flops 2147614720 | bytes 21233672 | tf_op jit(solution)/shard_map/tes,eijs->itj/dot_general | solution.py:45
  265.4 2.0 copy-done
  267.4 3.4 collective-permute-start.9
  270.9 107.2 %all-gather.3.cloned.1.call-done = bf16[128,512,128]{2,1,0:T(8,128)(2,1)} async-done(((bf16[16,512,128]{2,1,0:T(8,128)(2,1)}), bf16[128,512,128]{2,1,0:T(8,128)(2,1)}) %all-gather.3.cloned.1.call-update) | async-done | bytes 16777232 | tf_op jit(solution)/shard_map/all_gather | solution.py:36
  378.0 10.1 %convolution_bitcast_fusion = f32[16,128,512]{1,2,0:T(8,128)} fusion(bf16[128,8,128,1]{0,2,3,1:T(8,128)(2,1)S(1)} %bitcast.69, bf16[8,16,512,128]{3,2,1,0:T(8,128)(2,1)} %bitcast.67), kind=kOutput, calls=%fused_computation.12 | convolution fusion | flops 2147483648 | bytes 21233664 | tf_op jit(solution)/shard_map/tes,eijs->itj/dot_general | solution.py:44
  389.2 3.0 collective-permute-start.10
  392.2 2.6 collective-permute-start
  394.8 2.1 collective-permute-start.1
  396.9 2.8 collective-permute-done.1
  401.8 7.3 %pad_maximum_fusion = f32[34,128,512]{1,2,0:T(8,128)} fusion(f32[2,128,512]{1,2,0:T(8,128)S(1)} %collective-permute-done.10, f32[16,128,512]{1,2,0:T(8,128)} %copy-done, f32[16,128,512]{1,2,0:T(8,128)} %convolution_bitcast_fusion, f32[2,128,512]{1,2,0:T(8,128)S(1)} %collective-permute-done.9), kind=kLoop, calls=%fused_computation.1 | loop fusion | flops 6684672 | bytes 18350080 | tf_op jit(solution)/shard_map/concatenate | solution.py:50
  409.5 13.8 %fusion.2 = f32[34,128,512]{1,2,0:T(8,128)S(1)} fusion(f32[16,128,512]{1,2,0:T(8,128)S(1)} %copy-done.1, f32[16,128,512]{1,2,0:T(8,128)S(1)} %copy-done.2, f32[2,128,512]{1,2,0:T(8,128)S(1)} %collective-permute-done.9, f32[2,128,512]{1,2,0:T(8,128)} %copy-done.3, f32[34,128,512]{1,2,0:T(8,128)} %pad_maximum_fusion, f32[34,512]{1,0:T(8,128)} %maximum_add_fusion.1, ...), kind=kLoop, calls=%fused_computation.7 | loop fusion | flops 22282240 | bytes 27332642 | tf_op jit(solution)/shard_map/jit(_where)/select_n | solution.py:56
  424.2 6.3 %fusion.5 = f32[128,32,512]{0,2,1:T(8,128)} fusion(f32[34,128,512]{1,2,0:T(8,128)S(1)} %fusion.2, f32[32,128,512]{1,2,0:T(8,128)S(1)} %slice.72, f32[32,512]{1,0:T(8,128)S(1)} %copy-done.5), kind=kLoop, calls=%fused_computation.11 | loop fusion | flops 10485760 | bytes 33619968 | tf_op jit(solution)/shard_map/transpose | solution.py:58
  430.5 10.3 %copy.67 = f32[128,32,512]{2,1,0:T(8,128)} copy(f32[128,32,512]{0,2,1:T(8,128)} %fusion.5) | data formatting | bytes 16777216 | tf_op jit(solution)/shard_map/transpose | solution.py:58
  (38 shorter events, 8.5 us)
Async XLA Ops:
  6.5 31.8 %copy-start.6 = (bf16[128,1024]{1,0:T(8,128)(2,1)S(1)}, bf16[128,1024]{1,0:T(8,128)(2,1)}, u32[]{:S(2)}) copy-start(bf16[128,1024]{1,0:T(8,128)(2,1)} %param.4) | copy-start | bytes 786436
  6.5 371.5 %all-gather.3.cloned.1.call-start = ((), (), s32[]{:S(2)}) async-start(), calls=%async_computation | async-start | bytes 18874368 | tf_op jit(solution)/shard_map/all_gather | solution.py:36
  19.2 72.7 %collective-permute-start.2 = (bf16[16,512,128]{2,1,0:T(8,128)(2,1)}, bf16[16,512,128]{2,1,0:T(8,128)(2,1)}, u32[]{:S(2)}, u32[]{:S(2)}) collective-permute-start(bf16[16,512,128]{2,1,0:T(8,128)(2,1)} %get-tuple-element.6), channel_id=1, source_target_pairs={{0,16},{16,32},{32,48},{48,64},{64,80},{80,96},{96,112},{1,17},{17... | collective-permute-start | bytes 6291464 | tf_op jit(solution)/shard_map/ppermute | solution.py:40
  26.2 169.0 %collective-permute-start.3 = (bf16[16,512,128]{2,1,0:T(8,128)(2,1)}, bf16[16,512,128]{2,1,0:T(8,128)(2,1)}, u32[]{:S(2)}, u32[]{:S(2)}) collective-permute-start(bf16[16,512,128]{2,1,0:T(8,128)(2,1)} %get-tuple-element.6), channel_id=1, source_target_pairs={{0,32},{16,48},{32,64},{48,80},{64,96},{80,112},{1,33},{17,49},{33... | collective-permute-start | bytes 6291464 | tf_op jit(solution)/shard_map/ppermute | solution.py:40
  29.8 175.6 %collective-permute-start.4 = (bf16[16,512,128]{2,1,0:T(8,128)(2,1)}, bf16[16,512,128]{2,1,0:T(8,128)(2,1)}, u32[]{:S(2)}, u32[]{:S(2)}) collective-permute-start(bf16[16,512,128]{2,1,0:T(8,128)(2,1)} %get-tuple-element.6), channel_id=1, source_target_pairs={{0,48},{16,64},{32,80},{48,96},{64,112},{1,49},{17,65},{33,81},{49... | collective-permute-start | bytes 6291464 | tf_op jit(solution)/shard_map/ppermute | solution.py:40
  34.1 206.1 %collective-permute-start.5 = (bf16[16,512,128]{2,1,0:T(8,128)(2,1)}, bf16[16,512,128]{2,1,0:T(8,128)(2,1)}, u32[]{:S(2)}, u32[]{:S(2)}) collective-permute-start(bf16[16,512,128]{2,1,0:T(8,128)(2,1)} %get-tuple-element.6), channel_id=1, source_target_pairs={{0,64},{16,80},{32,96},{48,112},{1,65},{17,81},{33,97},{49,113},{2... | collective-permute-start | bytes 6291464 | tf_op jit(solution)/shard_map/ppermute | solution.py:40
  36.9 206.7 %collective-permute-start.6 = (bf16[16,512,128]{2,1,0:T(8,128)(2,1)}, bf16[16,512,128]{2,1,0:T(8,128)(2,1)S(1)}, u32[]{:S(2)}, u32[]{:S(2)}) collective-permute-start(bf16[16,512,128]{2,1,0:T(8,128)(2,1)} %get-tuple-element.6), channel_id=1, source_target_pairs={{0,80},{16,96},{32,112},{1,81},{17,97},{33,113},{2,82},{18,98},{34... | collective-permute-start | bytes 6291464 | tf_op jit(solution)/shard_map/ppermute | solution.py:40
  91.9 157.5 %collective-permute-start.7 = (bf16[16,512,128]{2,1,0:T(8,128)(2,1)}, bf16[16,512,128]{2,1,0:T(8,128)(2,1)}, u32[]{:S(2)}, u32[]{:S(2)}) collective-permute-start(bf16[16,512,128]{2,1,0:T(8,128)(2,1)} %get-tuple-element.6), channel_id=1, source_target_pairs={{0,96},{16,112},{1,97},{17,113},{2,98},{18,114},{3,99},{19,115},{4... | collective-permute-start | bytes 6291464 | tf_op jit(solution)/shard_map/ppermute | solution.py:40
  195.2 57.5 %collective-permute-start.8 = (bf16[16,512,128]{2,1,0:T(8,128)(2,1)}, bf16[16,512,128]{2,1,0:T(8,128)(2,1)}, u32[]{:S(2)}, u32[]{:S(2)}) collective-permute-start(bf16[16,512,128]{2,1,0:T(8,128)(2,1)} %get-tuple-element.6), channel_id=1, source_target_pairs={{0,112},{1,113},{2,114},{3,115},{4,116},{5,117},{6,118},{7,119},{8... | collective-permute-start | bytes 6291464 | tf_op jit(solution)/shard_map/ppermute | solution.py:40
  265.4 2.0 copy-start
  267.4 133.6 %collective-permute-start.9 = (f32[2,128,512]{1,2,0:T(8,128)S(1)}, f32[2,128,512]{1,2,0:T(8,128)S(1)}, u32[]{:S(2)}, u32[]{:S(2)}) collective-permute-start(f32[2,128,512]{1,2,0:T(8,128)S(1)} %slice.69), channel_id=1, source_target_pairs={{0,1},{1,2},{2,3},{3,4},{4,5},{5,6},{6,7},{7,8},{8,9},{9,10},{10,1... | collective-permute-start | bytes 1572872 | tf_op jit(solution)/shard_map/ppermute | solution.py:14
  378.0 14.2 %copy-start.4 = (f32[32,512]{1,0:T(8,128)S(1)}, f32[32,512]{1,0:T(8,128)}, u32[]{:S(2)}) copy-start(f32[32,512]{1,0:T(8,128)} %param.5) | copy-start | bytes 196612
  389.2 11.8 %collective-permute-start.10 = (f32[2,128,512]{1,2,0:T(8,128)S(1)}, f32[2,128,512]{1,2,0:T(8,128)S(1)}, u32[]{:S(2)}, u32[]{:S(2)}) collective-permute-start(f32[2,128,512]{1,2,0:T(8,128)S(1)} %slice.71), channel_id=1, source_target_pairs={{1,0},{2,1},{3,2},{4,3},{5,4},{6,5},{7,6},{8,7},{9,8},{10,9},{11,1... | collective-permute-start | bytes 1572872 | tf_op jit(solution)/shard_map/ppermute | solution.py:15
  392.2 4.7 %collective-permute-start = (f32[1,512]{1,0:T(1,128)S(1)}, f32[1,512]{1,0:T(1,128)S(1)}, u32[]{:S(2)}, u32[]{:S(2)}) collective-permute-start(f32[1,512]{1,0:T(1,128)S(1)} %get-tuple-element.7), channel_id=1, source_target_pairs={{0,1},{1,2},{2,3},{3,4},{4,5},{5,6},{6,7},{7,8},{8,9},{9,10},{10,1... | collective-permute-start | bytes 6152 | tf_op jit(solution)/shard_map/ppermute | solution.py:14
  394.8 4.9 %collective-permute-start.1 = (f32[1,512]{1,0:T(1,128)S(1)}, f32[1,512]{1,0:T(1,128)S(1)}, u32[]{:S(2)}, u32[]{:S(2)}) collective-permute-start(f32[1,512]{1,0:T(1,128)S(1)} %get-tuple-element.8), channel_id=1, source_target_pairs={{1,0},{2,1},{3,2},{4,3},{5,4},{6,5},{7,6},{8,7},{9,8},{10,9},{11,1... | collective-permute-start | bytes 6152 | tf_op jit(solution)/shard_map/ppermute | solution.py:15
  401.0 8.1 %copy-start.1 = (f32[16,128,512]{1,2,0:T(8,128)S(1)}, f32[16,128,512]{1,2,0:T(8,128)}, u32[]{:S(2)}) copy-start(f32[16,128,512]{1,2,0:T(8,128)} %copy-done) | copy-start | bytes 12582916
  401.0 8.5 %copy-start.2 = (f32[16,128,512]{1,2,0:T(8,128)S(1)}, f32[16,128,512]{1,2,0:T(8,128)}, u32[]{:S(2)}) copy-start(f32[16,128,512]{1,2,0:T(8,128)} %convolution_bitcast_fusion) | copy-start | bytes 12582916
  401.0 0.8 copy-start.3
  423.3 0.8 copy-start.5
Sparse Core Ops, SparseCore 0:
  19.3 358.6 all-gather.2

commit v5 on v4

--- a/solution.py
+++ b/solution.py
@@ -34,10 +34,18 @@
     head = own[:GATHERED_ROWS]
     tail = own[GATHERED_ROWS:]
     gathered = lax.all_gather(head, "epoch", axis=0)
+    a, b = count - 2, count - 1
+    skip = {(e, b) for e in range(a) if e % 2 == a % 2} | {(e, a) for e in range(a) if e % 2 == b % 2}
     slots = [tail]
     for shift in range(1, count):
-        pairs = [(e, e + shift) for e in range(count - shift)]
-        slots.append(lax.ppermute(tail, "epoch", pairs))
+        pairs = [(e, e + shift) for e in range(count - shift) if (e, e + shift) not in skip]
+        slots.append(lax.ppermute(tail, "epoch", pairs) if pairs else jnp.zeros_like(tail))
+    relay = list(range(2, a + 1, 2))
+    swapped = lax.ppermute(jnp.stack([slots[k] for k in relay]), "epoch", [(a, b), (b, a)])
+    for m, k in enumerate(relay):
+        at_a, at_b = k - 1, k + 1
+        slots[at_a] = jnp.where(me == a, swapped[m], slots[at_a])
+        slots[at_b] = jnp.where(me == b, swapped[m], slots[at_b])
     stacked = jnp.stack(slots, axis=0)
     source = jnp.clip(me - jnp.arange(count), 0, count - 1)
     weights = jnp.take(lower, source, axis=1)

time: 449 us -> 518 us (1.15)
  the two profiles are of different devices: /device:TPU:1 before, /device:TPU:119 now
where the time goes in v5:
time: 518 us; the launch traced here: 517 us
  waiting for transfers between devices  388 us (75%)
  other arithmetic  44 us (8%)
  local copies, waits for them, and re-layouts  31.8 us (6%)
  starting transfers between devices  25.3 us (5%)
  matrix products  14.7 us (3%)
  between operations  13.8 us (3%)
    ppermute x6, waiting for transfers between devices, body(): lax.ppermute(tail, 'epoch', pairs)  382 us
    unnamed x28, local copies, waits for them, and re-layouts  14.3 us
    select_n x1, other arithmetic, body(): once = jnp.where(outside, jnp.zeros_like(once), once)  13.9 us
  transfers between devices with their start and end apart: 12, of which 5 were waited for; matrix products, arithmetic and copies ran while one was open for 7% of the time, Pallas kernels for 0%

profile of v5, /device:TPU:119, one launch (start us, length us, event | category | flops | bytes accessed | tf_op | source)
XLA Modules:
  0.0 517.1 jit_solution(3531603549222820247)
XLA Ops:
  6.5 7.9 %copy.58 = bf16[128,32,512]{0,2,1:T(8,128)(2,1)} copy(bf16[128,32,512]{2,1,0:T(8,128)(2,1)} %param.3) | data formatting | bytes 8388608 | tf_op args[0]
  14.4 4.7 fusion.18
  19.2 1.4 collective-permute-start.2
  20.6 1.3 collective-permute-start.3
  21.9 1.3 collective-permute-start.4
  23.2 77.9 %collective-permute-done.2 = bf16[16,512,128]{2,1,0:T(8,128)(2,1)S(1)} collective-permute-done((bf16[16,512,128]{2,1,0:T(8,128)(2,1)}, bf16[16,512,128]{2,1,0:T(8,128)(2,1)S(1)}, u32[]{:S(2)}, u32[]{:S(2)}) %collective-permute-start.2) | collective-permute-done | bytes 2097184 | tf_op jit(solution)/shard_map/ppermute | solution.py:42
  101.1 3.4 collective-permute-done.3
  104.5 46.8 %collective-permute-done.4 = bf16[16,512,128]{2,1,0:T(8,128)(2,1)S(1)} collective-permute-done((bf16[16,512,128]{2,1,0:T(8,128)(2,1)}, bf16[16,512,128]{2,1,0:T(8,128)(2,1)S(1)}, u32[]{:S(2)}, u32[]{:S(2)}) %collective-permute-start.4) | collective-permute-done | bytes 2097184 | tf_op jit(solution)/shard_map/ppermute | solution.py:42
  151.3 3.2 pad_maximum_fusion.3
  154.5 1.9 collective-permute-start.5
  156.4 1.3 collective-permute-start.6
  157.7 2.0 collective-permute-start.7
  159.7 2.0 collective-permute-start.8
  162.9 1.9 bitcast_dynamic-update-slice_fusion.5
  164.8 254.4 %collective-permute-done.6 = bf16[16,512,128]{2,1,0:T(8,128)(2,1)} collective-permute-done((bf16[16,512,128]{2,1,0:T(8,128)(2,1)}, bf16[16,512,128]{2,1,0:T(8,128)(2,1)}, u32[]{:S(2)}, u32[]{:S(2)}) %collective-permute-start.6) | collective-permute-done | bytes 2097184 | tf_op jit(solution)/shard_map/ppermute | solution.py:42
  419.2 2.9 bitcast_dynamic-update-slice_fusion.4
  422.4 3.3 bitcast_dynamic-update-slice_fusion.2
  426.1 3.3 fusion.7
  429.8 2.2 fusion.8
  432.0 4.6 convolution_bitcast_fusion.1
  436.6 2.0 copy-done
  438.7 4.5 collective-permute-start.9
  443.2 10.1 %convolution_bitcast_fusion = f32[16,128,512]{1,2,0:T(8,128)} fusion(bf16[128,8,128,1]{0,2,3,1:T(8,128)(2,1)S(1)} %bitcast.95, bf16[8,16,512,128]{3,2,1,0:T(8,128)(2,1)} %bitcast.90), kind=kOutput, calls=%fused_computation.13 | convolution fusion | flops 2147483648 | bytes 21233664 | tf_op jit(solution)/shard_map/tes,eijs->itj/dot_general | solution.py:52
  453.3 1.1 slice.89
  454.4 1.9 collective-permute-start.10
  456.3 5.8 %collective-permute-start = (f32[1,512]{1,0:T(1,128)S(1)}, f32[1,512]{1,0:T(1,128)S(1)}, u32[]{:S(2)}, u32[]{:S(2)}) collective-permute-start(f32[1,512]{1,0:T(1,128)S(1)} %get-tuple-element.7), channel_id=1, source_target_pairs={{0,1},{1,2},{2,3},{3,4},{4,5},{5,6},{6,7},{7,8},{8,9},{9,10},{10,1... | collective-permute-start | bytes 6152 | tf_op jit(solution)/shard_map/ppermute | solution.py:14
  462.1 1.9 collective-permute-start.1
  464.1 5.1 collective-permute-done.1
  471.2 7.3 %pad_maximum_fusion = f32[34,128,512]{1,2,0:T(8,128)} fusion(f32[2,128,512]{1,2,0:T(8,128)S(1)} %collective-permute-done.10, f32[16,128,512]{1,2,0:T(8,128)} %copy-done, f32[16,128,512]{1,2,0:T(8,128)} %convolution_bitcast_fusion, f32[2,128,512]{1,2,0:T(8,128)S(1)} %collective-permute-done.9), kind=kLoop, calls=%fused_computation.1 | loop fusion | flops 6684672 | bytes 18350080 | tf_op jit(solution)/shard_map/concatenate | solution.py:58
  478.9 13.9 %fusion.2 = f32[34,128,512]{1,2,0:T(8,128)S(1)} fusion(f32[16,128,512]{1,2,0:T(8,128)S(1)} %copy-done.1, f32[16,128,512]{1,2,0:T(8,128)S(1)} %copy-done.2, f32[2,128,512]{1,2,0:T(8,128)S(1)} %collective-permute-done.9, f32[2,128,512]{1,2,0:T(8,128)} %copy-done.7, f32[34,128,512]{1,2,0:T(8,128)} %pad_maximum_fusion, f32[34,512]{1,0:T(8,128)} %maximum_add_fusion.1, ...), kind=kLoop, calls=%fused_computation.7 | loop fusion | flops 22282240 | bytes 27332642 | tf_op jit(solution)/shard_map/jit(_where)/select_n | solution.py:64
  493.6 6.4 %fusion.5 = f32[128,32,512]{0,2,1:T(8,128)} fusion(f32[34,128,512]{1,2,0:T(8,128)S(1)} %fusion.2, f32[32,128,512]{1,2,0:T(8,128)S(1)} %slice.90, f32[32,512]{1,0:T(8,128)S(1)} %copy-done.9), kind=kLoop, calls=%fused_computation.11 | loop fusion | flops 10485760 | bytes 33619968 | tf_op jit(solution)/shard_map/transpose | solution.py:66
  500.0 10.3 %copy.72 = f32[128,32,512]{2,1,0:T(8,128)} copy(f32[128,32,512]{0,2,1:T(8,128)} %fusion.5) | data formatting | bytes 16777216 | tf_op jit(solution)/shard_map/transpose | solution.py:66
  (47 shorter events, 5.3 us)
Async XLA Ops:
  6.5 436.7 %all-gather.3.cloned.1.call-start = ((), (), s32[]{:S(2)}) async-start(), calls=%async_computation | async-start | bytes 18874368 | tf_op jit(solution)/shard_map/all_gather | solution.py:36
  19.2 142.5 %copy-start.10 = (bf16[128,1024]{1,0:T(8,128)(2,1)S(1)}, bf16[128,1024]{1,0:T(8,128)(2,1)}, u32[]{:S(2)}) copy-start(bf16[128,1024]{1,0:T(8,128)(2,1)} %param.4) | copy-start | bytes 786436
  19.2 81.9 %collective-permute-start.2 = (bf16[16,512,128]{2,1,0:T(8,128)(2,1)}, bf16[16,512,128]{2,1,0:T(8,128)(2,1)S(1)}, u32[]{:S(2)}, u32[]{:S(2)}) collective-permute-start(bf16[16,512,128]{2,1,0:T(8,128)(2,1)} %get-tuple-element.6), channel_id=1, source_target_pairs={{0,32},{16,48},{32,64},{48,80},{64,96},{80,112},{1,33},{17,49},{33... | collective-permute-start | bytes 6291464 | tf_op jit(solution)/shard_map/ppermute | solution.py:42
  20.6 83.9 %collective-permute-start.3 = (bf16[16,512,128]{2,1,0:T(8,128)(2,1)}, bf16[16,512,128]{2,1,0:T(8,128)(2,1)S(1)}, u32[]{:S(2)}, u32[]{:S(2)}) collective-permute-start(bf16[16,512,128]{2,1,0:T(8,128)(2,1)} %get-tuple-element.6), channel_id=1, source_target_pairs={{0,64},{16,80},{32,96},{48,112},{1,65},{17,81},{33,97},{49,113},{2... | collective-permute-start | bytes 6291464 | tf_op jit(solution)/shard_map/ppermute | solution.py:42
  21.9 129.4 %collective-permute-start.4 = (bf16[16,512,128]{2,1,0:T(8,128)(2,1)}, bf16[16,512,128]{2,1,0:T(8,128)(2,1)S(1)}, u32[]{:S(2)}, u32[]{:S(2)}) collective-permute-start(bf16[16,512,128]{2,1,0:T(8,128)(2,1)} %get-tuple-element.6), channel_id=1, source_target_pairs={{0,96},{16,112},{1,97},{17,113},{2,98},{18,114},{3,99},{19,115},{4... | collective-permute-start | bytes 6291464 | tf_op jit(solution)/shard_map/ppermute | solution.py:42
  101.1 53.3 %copy-start.5 = (bf16[16,512,128]{2,1,0:T(8,128)(2,1)}, bf16[16,512,128]{2,1,0:T(8,128)(2,1)S(1)}, u32[]{:S(2)}) copy-start(bf16[16,512,128]{2,1,0:T(8,128)(2,1)S(1)} %collective-permute-done.2) | copy-start | bytes 6291460
  104.5 46.8 %copy-start.3 = (bf16[16,512,128]{2,1,0:T(8,128)(2,1)}, bf16[16,512,128]{2,1,0:T(8,128)(2,1)S(1)}, u32[]{:S(2)}) copy-start(bf16[16,512,128]{2,1,0:T(8,128)(2,1)S(1)} %collective-permute-done.3) | copy-start | bytes 6291460
  154.5 264.7 %collective-permute-start.5 = (bf16[3,16,512,128]{3,2,1,0:T(8,128)(2,1)}, bf16[3,16,512,128]{3,2,1,0:T(8,128)(2,1)}, u32[]{:S(2)}, u32[]{:S(2)}) collective-permute-start(bf16[3,16,512,128]{3,2,1,0:T(8,128)(2,1)} %pad_maximum_fusion.3), channel_id=1, source_target_pairs={{96,112},{112,96},{97,113},{113,97},{98,114},{114,98},{99,115},{11... | collective-permute-start | bytes 18874376 | tf_op jit(solution)/shard_map/ppermute | solution.py:44
  156.4 262.8 %collective-permute-start.6 = (bf16[16,512,128]{2,1,0:T(8,128)(2,1)}, bf16[16,512,128]{2,1,0:T(8,128)(2,1)}, u32[]{:S(2)}, u32[]{:S(2)}) collective-permute-start(bf16[16,512,128]{2,1,0:T(8,128)(2,1)} %get-tuple-element.6), channel_id=1, source_target_pairs={{0,16},{16,32},{32,48},{48,64},{64,80},{96,112},{1,17},{17,33},{33... | collective-permute-start | bytes 6291464 | tf_op jit(solution)/shard_map/ppermute | solution.py:42
  157.7 264.7 %collective-permute-start.7 = (bf16[16,512,128]{2,1,0:T(8,128)(2,1)}, bf16[16,512,128]{2,1,0:T(8,128)(2,1)}, u32[]{:S(2)}, u32[]{:S(2)}) collective-permute-start(bf16[16,512,128]{2,1,0:T(8,128)(2,1)} %get-tuple-element.6), channel_id=1, source_target_pairs={{0,48},{16,64},{32,80},{1,49},{17,65},{33,81},{2,50},{18,66},{34,8... | collective-permute-start | bytes 6291464 | tf_op jit(solution)/shard_map/ppermute | solution.py:42
  159.7 266.4 %collective-permute-start.8 = (bf16[16,512,128]{2,1,0:T(8,128)(2,1)}, bf16[16,512,128]{2,1,0:T(8,128)(2,1)}, u32[]{:S(2)}, u32[]{:S(2)}) collective-permute-start(bf16[16,512,128]{2,1,0:T(8,128)(2,1)} %get-tuple-element.6), channel_id=1, source_target_pairs={{0,80},{1,81},{2,82},{3,83},{4,84},{5,85},{6,86},{7,87},{8,88},{9,... | collective-permute-start | bytes 6291464 | tf_op jit(solution)/shard_map/ppermute | solution.py:42
  162.8 259.3 %copy-start.6 = (bf16[16,512,128]{2,1,0:T(8,128)(2,1)S(1)}, bf16[16,512,128]{2,1,0:T(8,128)(2,1)}, u32[]{:S(2)}) copy-start(bf16[16,512,128]{2,1,0:T(8,128)(2,1)} %copy-done.5) | copy-start | bytes 6291460
  164.8 261.0 %copy-start.4 = (bf16[16,512,128]{2,1,0:T(8,128)(2,1)S(1)}, bf16[16,512,128]{2,1,0:T(8,128)(2,1)}, u32[]{:S(2)}) copy-start(bf16[16,512,128]{2,1,0:T(8,128)(2,1)} %copy-done.3) | copy-start | bytes 6291460
  436.6 2.0 copy-start
  438.7 31.7 %collective-permute-start.9 = (f32[2,128,512]{1,2,0:T(8,128)S(1)}, f32[2,128,512]{1,2,0:T(8,128)S(1)}, u32[]{:S(2)}, u32[]{:S(2)}) collective-permute-start(f32[2,128,512]{1,2,0:T(8,128)S(1)} %slice.87), channel_id=1, source_target_pairs={{0,1},{1,2},{2,3},{3,4},{4,5},{5,6},{6,7},{7,8},{8,9},{9,10},{10,1... | collective-permute-start | bytes 1572872 | tf_op jit(solution)/shard_map/ppermute | solution.py:14
  443.2 13.1 %copy-start.8 = (f32[32,512]{1,0:T(8,128)S(1)}, f32[32,512]{1,0:T(8,128)}, u32[]{:S(2)}) copy-start(f32[32,512]{1,0:T(8,128)} %param.5) | copy-start | bytes 196612
  454.4 16.0 %collective-permute-start.10 = (f32[2,128,512]{1,2,0:T(8,128)S(1)}, f32[2,128,512]{1,2,0:T(8,128)S(1)}, u32[]{:S(2)}, u32[]{:S(2)}) collective-permute-start(f32[2,128,512]{1,2,0:T(8,128)S(1)} %slice.89), channel_id=1, source_target_pairs={{1,0},{2,1},{3,2},{4,3},{5,4},{6,5},{7,6},{8,7},{9,8},{10,9},{11,1... | collective-permute-start | bytes 1572872 | tf_op jit(solution)/shard_map/ppermute | solution.py:15
  456.3 7.7 %collective-permute-start = (f32[1,512]{1,0:T(1,128)S(1)}, f32[1,512]{1,0:T(1,128)S(1)}, u32[]{:S(2)}, u32[]{:S(2)}) collective-permute-start(f32[1,512]{1,0:T(1,128)S(1)} %get-tuple-element.7), channel_id=1, source_target_pairs={{0,1},{1,2},{2,3},{3,4},{4,5},{5,6},{6,7},{7,8},{8,9},{9,10},{10,1... | collective-permute-start | bytes 6152 | tf_op jit(solution)/shard_map/ppermute | solution.py:14
  462.1 7.0 %collective-permute-start.1 = (f32[1,512]{1,0:T(1,128)S(1)}, f32[1,512]{1,0:T(1,128)S(1)}, u32[]{:S(2)}, u32[]{:S(2)}) collective-permute-start(f32[1,512]{1,0:T(1,128)S(1)} %get-tuple-element.8), channel_id=1, source_target_pairs={{1,0},{2,1},{3,2},{4,3},{5,4},{6,5},{7,6},{8,7},{9,8},{10,9},{11,1... | collective-permute-start | bytes 6152 | tf_op jit(solution)/shard_map/ppermute | solution.py:15
  470.4 8.1 %copy-start.1 = (f32[16,128,512]{1,2,0:T(8,128)S(1)}, f32[16,128,512]{1,2,0:T(8,128)}, u32[]{:S(2)}) copy-start(f32[16,128,512]{1,2,0:T(8,128)} %copy-done) | copy-start | bytes 12582916
  470.4 8.5 %copy-start.2 = (f32[16,128,512]{1,2,0:T(8,128)S(1)}, f32[16,128,512]{1,2,0:T(8,128)}, u32[]{:S(2)}) copy-start(f32[16,128,512]{1,2,0:T(8,128)} %convolution_bitcast_fusion) | copy-start | bytes 12582916
  470.4 0.8 copy-start.7
  492.8 0.8 copy-start.9
Sparse Core Ops, SparseCore 0:
  19.3 320.7 all-gather.2

commit v6 on v4

v6 whole, which is shorter than its diff:
```python
import jax
import jax.numpy as jnp
from jax import lax
from jax.sharding import PartitionSpec as P

EDGE = 8
HALO = 2


def neighbours(top, bottom, width):
    size = lax.axis_size("row")
    up = [(i, i + 1) for i in range(size - 1)]
    down = [(i + 1, i) for i in range(size - 1)]
    above = lax.ppermute(bottom[bottom.shape[0] - width:], "row", up)
    below = lax.ppermute(top[:width], "row", down)
    return above, below


def side_sum(v):
    padded = jnp.pad(v, [(0, 0)] * (v.ndim - 1) + [(1, 1)])
    return padded[..., :-2] + padded[..., 2:]


def double_stencil(ext, gain_once, gain_out, first_outside=None, last_outside=None):
    once = gain_once * ext[1:-1] - (ext[:-2] + ext[2:] + side_sum(ext[1:-1]))
    if first_outside is not None or last_outside is not None:
        rows = lax.broadcasted_iota(jnp.int32, (once.shape[0], 1, 1), 0)
        outside = jnp.zeros(rows.shape, jnp.bool_)
        if first_outside is not None:
            outside = outside | ((rows == 0) & first_outside)
        if last_outside is not None:
            outside = outside | ((rows == once.shape[0] - 1) & last_outside)
        once = jnp.where(outside, jnp.zeros_like(once), once)
    return gain_out * once[1:-1] - (once[:-2] + once[2:] + side_sum(once[1:-1]))


def body(field, factor, kappa):
    epochs, slab, width = field.shape
    count = lax.axis_size("epoch")
    order = epochs * count
    me = lax.axis_index("epoch")
    global_rows = me * epochs + lax.broadcasted_iota(jnp.int32, (epochs, order), 0)
    global_cols = lax.broadcasted_iota(jnp.int32, (epochs, order), 1)
    lower = jnp.where(global_cols <= global_rows, factor, jnp.zeros_like(factor))
    lower = lower.reshape(epochs, count, epochs)
    middle = jnp.transpose(field[:, EDGE:slab - EDGE], (1, 2, 0))
    gathered = lax.all_gather(middle, "epoch", axis=0)
    edges = jnp.transpose(
        jnp.concatenate([field[:, :EDGE], field[:, slab - EDGE:]], axis=1), (1, 2, 0)
    )
    slots = [edges]
    for shift in range(1, count):
        pairs = [(e, e + shift) for e in range(count - shift)]
        slots.append(lax.ppermute(edges, "epoch", pairs))
    stacked = jnp.stack(slots, axis=0)
    source = jnp.clip(me - jnp.arange(count), 0, count - 1)
    weights = jnp.take(lower, source, axis=1)
    timed_edges = jnp.einsum("tes,eijs->itj", weights, stacked, preferred_element_type=jnp.float32)
    top, bottom = timed_edges[:EDGE], timed_edges[EDGE:]

    above, below = neighbours(top, bottom, HALO)
    k_above, k_below = neighbours(kappa, kappa, 1)
    gain = jnp.concatenate([k_above, kappa, k_below], axis=0)[:, None, :] + 4.0
    pos = lax.axis_index("row")
    last = lax.axis_size("row") - 1
    out_top = double_stencil(
        jnp.concatenate([above, top], axis=0),
        gain[0:EDGE], gain[1:EDGE - 1], first_outside=pos == 0,
    )
    out_bottom = double_stencil(
        jnp.concatenate([bottom, below], axis=0),
        gain[slab - EDGE + 2:slab + 2], gain[slab - EDGE + 3:slab + 1], last_outside=pos == last,
    )
    timed_middle = jnp.einsum("tes,eijs->itj", lower, gathered, preferred_element_type=jnp.float32)
    ext = jnp.concatenate([top[EDGE - 2 * HALO:], timed_middle, bottom[:2 * HALO]], axis=0)
    out_middle = double_stencil(ext, gain[EDGE - 2:slab - EDGE + 4], gain[EDGE - 1:slab - EDGE + 3])
    product = jnp.concatenate([out_top, out_middle, out_bottom], axis=0)
    return jnp.transpose(product, (1, 0, 2))


def solution(mesh):
    in_specs = (P("epoch", "row", None), P("epoch", None), P("row", None))
    out_specs = P("epoch", "row", None)
    return jax.shard_map(body, mesh=mesh, in_specs=in_specs, out_specs=out_specs, check_vma=False)
```

time: 449 us -> 404 us (0.90)
  the two profiles are of different devices: /device:TPU:1 before, /device:TPU:62 now
where the time goes in v6:
time: 404 us; the launch traced here: 403 us
  waiting for transfers between devices  262 us (65%)
  local copies, waits for them, and re-layouts  49 us (12%)
  other arithmetic  28.7 us (7%)
  starting transfers between devices  26.3 us (7%)
  matrix products  23.8 us (6%)
  between operations  13.8 us (3%)
    ppermute x7, waiting for transfers between devices, body(): slots.append(lax.ppermute(edges, 'epoch', pairs))  154 us
    all_gather x1, waiting for transfers between devices, body(): gathered = lax.all_gather(middle, 'epoch', axis=0)  104 us
    unnamed x26, local copies, waits for them, and re-layouts  22.4 us
    ppermute x7, starting transfers between devices, body(): slots.append(lax.ppermute(edges, 'epoch', pairs))  16.1 us
    dot_general x1, matrix products, body(): jnp.einsum('tes,eijs->itj', lower, gathered, preferred_element_type=jnp.f...  13.4 us
    dot_general x1, matrix products, body(): jnp.einsum('tes,eijs->itj', weights, stacked, preferred_element_type=jnp....  10.4 us
    transpose x1, local copies, waits for them, and re-layouts, body(): return jnp.transpose(product, (1, 0, 2))  8.25 us
  transfers between devices with their start and end apart: 12, of which 5 were waited for; matrix products, arithmetic and copies ran while one was open for 15% of the time, Pallas kernels for 0%

profile of v6, /device:TPU:62, one launch (start us, length us, event | category | flops | bytes accessed | tf_op | source)
XLA Modules:
  0.0 403.3 jit_solution(4285420025604277026)
XLA Ops:
  8.1 3.0 copy.79
  11.2 1.7 fusion.31
  16.4 4.5 %collective-permute-start.2 = (bf16[16,512,128]{2,1,0:T(8,128)(2,1)}, bf16[16,512,128]{2,1,0:T(8,128)(2,1)}, u32[]{:S(2)}, u32[]{:S(2)}) collective-permute-start(bf16[16,512,128]{2,1,0:T(8,128)(2,1)} %fusion.20), channel_id=1, source_target_pairs={{0,16},{16,32},{32,48},{48,64},{64,80},{80,96},{96,112},{1,17},{17... | collective-permute-start | bytes 6291464 | tf_op jit(solution)/shard_map/ppermute | solution.py:54
  20.9 3.5 collective-permute-start.3
  24.4 3.0 collective-permute-start.4
  27.4 2.7 collective-permute-start.5
  30.1 1.9 collective-permute-start
  35.0 3.2 collective-permute-start.1
  40.5 50.6 %collective-permute-done.2 = bf16[16,512,128]{2,1,0:T(8,128)(2,1)} collective-permute-done((bf16[16,512,128]{2,1,0:T(8,128)(2,1)}, bf16[16,512,128]{2,1,0:T(8,128)(2,1)}, u32[]{:S(2)}, u32[]{:S(2)}) %collective-permute-start.2) | collective-permute-done | bytes 2097184 | tf_op jit(solution)/shard_map/ppermute | solution.py:54
  91.9 103.3 %collective-permute-done.3 = bf16[16,512,128]{2,1,0:T(8,128)(2,1)} collective-permute-done((bf16[16,512,128]{2,1,0:T(8,128)(2,1)}, bf16[16,512,128]{2,1,0:T(8,128)(2,1)}, u32[]{:S(2)}, u32[]{:S(2)}) %collective-permute-start.3) | collective-permute-done | bytes 2097184 | tf_op jit(solution)/shard_map/ppermute | solution.py:54
  196.6 3.3 bitcast_dynamic-update-slice_fusion.5
  200.0 3.3 bitcast_dynamic-update-slice_fusion.4
  203.3 3.4 bitcast_dynamic-update-slice_fusion.3
  206.7 3.3 bitcast_dynamic-update-slice_fusion.2
  210.0 1.6 bitcast_dynamic-update-slice_fusion.1
  213.3 1.7 bitcast_dynamic-update-slice_fusion.7
  215.0 10.4 %convolution_bitcast_fusion.1 = f32[16,128,512]{1,2,0:T(8,128)S(1)} fusion(bf16[8,16,512,128]{3,2,0,1:T(8,128)(2,1)} %bitcast_dynamic-update-slice_fusion.7, bf16[8,128,128]{2,1,0:T(8,128)(2,1)S(1)} %gather_fusion, pred[8]{0:T(512)(128)(4,1)S(1)} %compare_and_fusion.1), kind=kOutput, calls=%fused_computation.20 | convolution fusion | flops 2147614720 | bytes 21233672 | tf_op jit(solution)/shard_map/tes,eijs->itj/dot_general | solution.py:58
  226.5 1.9 collective-permute-start.10
  228.4 3.2 collective-permute-start.9
  233.4 2.5 fusion.29
  235.9 3.3 collective-permute-done.9
  239.2 2.7 fusion.6
  241.9 2.0 fusion.15
  246.2 3.1 copy.70
  249.2 4.1 %fusion.11 = f32[8,128,512]{1,2,0:T(8,128)S(1)} fusion(f32[8,128,512]{1,2,0:T(8,128)S(1)} %get-tuple-element.8, f32[2,128,512]{1,2,0:T(8,128)} %collective-permute-done.10, f32[8,128,512]{1,2,0:T(8,128)} %get-tuple-element.19, f32[8,512]{1,0:T(8,128)S(1)} %get-tuple-element.16, pred[8]{0:T(512)(128)(4,1)S(1)} %copy-done.6), kind=kLoop, calls=%fused_computation.27 | loop fusion | flops 3670016 | bytes 6832136 | tf_op jit(solution)/shard_map/jit(_where)/select_n | solution.py:33
  255.8 104.1 %all-gather.3.cloned.1.call-done = bf16[128,512,128]{2,1,0:T(8,128)(2,1)} async-done(((bf16[16,512,128]{2,1,0:T(8,128)(2,1)}), bf16[128,512,128]{2,1,0:T(8,128)(2,1)}) %all-gather.3.cloned.1.call-update) | async-done | bytes 16777232 | tf_op jit(solution)/shard_map/all_gather | solution.py:47
  359.9 13.4 %convolution_bitcast_fusion = f32[16,128,512]{2,1,0:T(8,128)} fusion(bf16[128,8,128,1]{0,2,3,1:T(8,128)(2,1)S(1)} %bitcast.82, bf16[8,16,512,128]{3,2,1,0:T(8,128)(2,1)} %bitcast.79), kind=kOutput, calls=%fused_computation.19 | convolution fusion | flops 2147483648 | bytes 21233664 | tf_op jit(solution)/shard_map/tes,eijs->itj/dot_general | solution.py:74
  373.3 2.9 pad_maximum_fusion
  377.2 4.3 %fusion.2 = f32[22,128,512]{2,1,0:T(8,128)S(1)} fusion(f32[22,128,512]{2,1,0:T(8,128)S(1)} %slice.205, f32[24,128,512]{2,1,0:T(8,128)S(1)} %pad_maximum_fusion, f32[22,512]{1,0:T(8,128)S(1)} %slice_bitcast_fusion), kind=kLoop, calls=%fused_computation.9 | loop fusion | flops 7208960 | bytes 23113728 | tf_op jit(solution)/shard_map/sub | solution.py:25
  382.1 3.7 fusion.5
  385.8 2.4 maximum_bitcast_fusion
  388.2 8.3 %copy.72 = f32[128,32,512]{2,1,0:T(8,128)} copy(f32[128,32,512]{2,0,1:T(8,128)S(1)} %maximum_bitcast_fusion) | data formatting | bytes 16777216 | tf_op jit(solution)/shard_map/transpose | solution.py:78
  (63 shorter events, 23.2 us)
Async XLA Ops:
  6.5 1.6 slice-start
  6.5 353.3 %all-gather.3.cloned.1.call-start = ((), (), s32[]{:S(2)}) async-start(), calls=%async_computation | async-start | bytes 18874368 | tf_op jit(solution)/shard_map/all_gather | solution.py:47
  14.9 15.3 %copy-start.4 = (f32[32,512]{1,0:T(8,128)S(1)}, f32[32,512]{1,0:T(8,128)}, u32[]{:S(2)}) copy-start(f32[32,512]{1,0:T(8,128)} %param.5) | copy-start | bytes 196612
  14.9 17.2 %copy-start.3 = (bf16[128,1024]{1,0:T(8,128)(2,1)S(1)}, bf16[128,1024]{1,0:T(8,128)(2,1)}, u32[]{:S(2)}) copy-start(bf16[128,1024]{1,0:T(8,128)(2,1)} %param.4) | copy-start | bytes 786436
  16.4 74.7 %collective-permute-start.2 = (bf16[16,512,128]{2,1,0:T(8,128)(2,1)}, bf16[16,512,128]{2,1,0:T(8,128)(2,1)}, u32[]{:S(2)}, u32[]{:S(2)}) collective-permute-start(bf16[16,512,128]{2,1,0:T(8,128)(2,1)} %fusion.20), channel_id=1, source_target_pairs={{0,16},{16,32},{32,48},{48,64},{64,80},{80,96},{96,112},{1,17},{17... | collective-permute-start | bytes 6291464 | tf_op jit(solution)/shard_map/ppermute | solution.py:54
  20.9 174.4 %collective-permute-start.3 = (bf16[16,512,128]{2,1,0:T(8,128)(2,1)}, bf16[16,512,128]{2,1,0:T(8,128)(2,1)}, u32[]{:S(2)}, u32[]{:S(2)}) collective-permute-start(bf16[16,512,128]{2,1,0:T(8,128)(2,1)} %fusion.20), channel_id=1, source_target_pairs={{0,32},{16,48},{32,64},{48,80},{64,96},{80,112},{1,33},{17,49},{33... | collective-permute-start | bytes 6291464 | tf_op jit(solution)/shard_map/ppermute | solution.py:54
  24.4 178.9 %collective-permute-start.4 = (bf16[16,512,128]{2,1,0:T(8,128)(2,1)}, bf16[16,512,128]{2,1,0:T(8,128)(2,1)}, u32[]{:S(2)}, u32[]{:S(2)}) collective-permute-start(bf16[16,512,128]{2,1,0:T(8,128)(2,1)} %fusion.20), channel_id=1, source_target_pairs={{0,48},{16,64},{32,80},{48,96},{64,112},{1,49},{17,65},{33,81},{49... | collective-permute-start | bytes 6291464 | tf_op jit(solution)/shard_map/ppermute | solution.py:54
  27.4 179.2 %collective-permute-start.5 = (bf16[16,512,128]{2,1,0:T(8,128)(2,1)}, bf16[16,512,128]{2,1,0:T(8,128)(2,1)}, u32[]{:S(2)}, u32[]{:S(2)}) collective-permute-start(bf16[16,512,128]{2,1,0:T(8,128)(2,1)} %fusion.20), channel_id=1, source_target_pairs={{0,64},{16,80},{32,96},{48,112},{1,65},{17,81},{33,97},{49,113},{2... | collective-permute-start | bytes 6291464 | tf_op jit(solution)/shard_map/ppermute | solution.py:54
  30.1 4.9 %collective-permute-start = (f32[1,512]{1,0:T(1,128)S(1)}, f32[1,512]{1,0:T(1,128)S(1)}, u32[]{:S(2)}, u32[]{:S(2)}) collective-permute-start(f32[1,512]{1,0:T(1,128)S(1)} %get-tuple-element.17), channel_id=1, source_target_pairs={{0,1},{1,2},{2,3},{3,4},{4,5},{5,6},{6,7},{7,8},{8,9},{9,10},{10,1... | collective-permute-start | bytes 6152 | tf_op jit(solution)/shard_map/ppermute | solution.py:14
  35.0 4.6 %collective-permute-start.1 = (f32[1,512]{1,0:T(1,128)S(1)}, f32[1,512]{1,0:T(1,128)S(1)}, u32[]{:S(2)}, u32[]{:S(2)}) collective-permute-start(f32[1,512]{1,0:T(1,128)S(1)} %get-tuple-element.18), channel_id=1, source_target_pairs={{1,0},{2,1},{3,2},{4,3},{5,4},{6,5},{7,6},{8,7},{9,8},{10,9},{11,1... | collective-permute-start | bytes 6152 | tf_op jit(solution)/shard_map/ppermute | solution.py:15
  39.6 170.4 %collective-permute-start.6 = (bf16[16,512,128]{2,1,0:T(8,128)(2,1)}, bf16[16,512,128]{2,1,0:T(8,128)(2,1)S(1)}, u32[]{:S(2)}, u32[]{:S(2)}) collective-permute-start(bf16[16,512,128]{2,1,0:T(8,128)(2,1)} %fusion.20), channel_id=1, source_target_pairs={{0,80},{16,96},{32,112},{1,81},{17,97},{33,113},{2,82},{18,98},{34... | collective-permute-start | bytes 6291464 | tf_op jit(solution)/shard_map/ppermute | solution.py:54
  91.1 120.6 %collective-permute-start.7 = (bf16[16,512,128]{2,1,0:T(8,128)(2,1)}, bf16[16,512,128]{2,1,0:T(8,128)(2,1)S(1)}, u32[]{:S(2)}, u32[]{:S(2)}) collective-permute-start(bf16[16,512,128]{2,1,0:T(8,128)(2,1)} %fusion.20), channel_id=1, source_target_pairs={{0,96},{16,112},{1,97},{17,113},{2,98},{18,114},{3,99},{19,115},{4... | collective-permute-start | bytes 6291464 | tf_op jit(solution)/shard_map/ppermute | solution.py:54
  195.2 18.1 %collective-permute-start.8 = (bf16[16,512,128]{2,1,0:T(8,128)(2,1)}, bf16[16,512,128]{2,1,0:T(8,128)(2,1)S(1)}, u32[]{:S(2)}, u32[]{:S(2)}) collective-permute-start(bf16[16,512,128]{2,1,0:T(8,128)(2,1)} %fusion.20), channel_id=1, source_target_pairs={{0,112},{1,113},{2,114},{3,115},{4,116},{5,117},{6,118},{7,119},{8... | collective-permute-start | bytes 6291464 | tf_op jit(solution)/shard_map/ppermute | solution.py:54
  225.3 6.4 %copy-start = (f32[16,128,512]{1,2,0:T(8,128)}, f32[16,128,512]{1,2,0:T(8,128)S(1)}, u32[]{:S(2)}) copy-start(f32[16,128,512]{1,2,0:T(8,128)S(1)} %convolution_bitcast_fusion.1) | copy-start | bytes 12582916
  226.5 9.4 %collective-permute-start.10 = (f32[2,128,512]{1,2,0:T(8,128)}, f32[2,128,512]{1,2,0:T(8,128)}, u32[]{:S(2)}, u32[]{:S(2)}) collective-permute-start(f32[2,128,512]{1,2,0:T(8,128)} %get-tuple-element.6), channel_id=1, source_target_pairs={{1,0},{2,1},{3,2},{4,3},{5,4},{6,5},{7,6},{8,7},{9,8},{10,9},{11,1... | collective-permute-start | bytes 1572872 | tf_op jit(solution)/shard_map/ppermute | solution.py:15
  228.4 10.8 %collective-permute-start.9 = (f32[2,128,512]{1,2,0:T(8,128)}, f32[2,128,512]{1,2,0:T(8,128)}, u32[]{:S(2)}, u32[]{:S(2)}) collective-permute-start(f32[2,128,512]{1,2,0:T(8,128)} %get-tuple-element.5), channel_id=1, source_target_pairs={{0,1},{1,2},{2,3},{3,4},{4,5},{5,6},{6,7},{7,8},{8,9},{9,10},{10,1... | collective-permute-start | bytes 1572872 | tf_op jit(solution)/shard_map/ppermute | solution.py:14
  239.2 2.7 copy-start.7
  243.9 0.7 copy-start.5
  246.2 3.1 copy-start.6
  359.8 13.4 %copy-start.2 = (f32[4,128,512]{2,1,0:T(8,128)S(1)}, f32[4,128,512]{2,1,0:T(8,128)}, u32[]{:S(2)}) copy-start(f32[4,128,512]{2,1,0:T(8,128)} %copy.69) | copy-start | bytes 3145732
  382.1 3.7 copy-start.1
Sparse Core Ops, SparseCore 0:
  11.3 348.5 all-gather.2

commit v7 on v6

--- a/solution.py
+++ b/solution.py
@@ -3,7 +3,7 @@
 from jax import lax
 from jax.sharding import PartitionSpec as P
 
-EDGE = 8
+EDGE = 12
 HALO = 2
 
 

time: 404 us -> 442 us (1.094)
  the two profiles are of different devices: /device:TPU:62 before, /device:TPU:8 now
where the time goes in v7:
time: 442 us; the launch traced here: 441 us
  waiting for transfers between devices  272 us (62%)
  local copies, waits for them, and re-layouts  71.8 us (16%)
  starting transfers between devices  40.6 us (9%)
  other arithmetic  25.5 us (6%)
  matrix products  18.1 us (4%)
  between operations  13.7 us (3%)
    ppermute x7, waiting for transfers between devices, body(): slots.append(lax.ppermute(edges, 'epoch', pairs))  260 us
    unnamed x32, local copies, waits for them, and re-layouts  34.1 us
    ppermute x7, starting transfers between devices, body(): slots.append(lax.ppermute(edges, 'epoch', pairs))  31.6 us
    dot_general x1, matrix products, body(): jnp.einsum('tes,eijs->itj', weights, stacked, preferred_element_type=jnp....  11.8 us
    ppermute x2, waiting for transfers between devices, neighbours(): above = lax.ppermute(bottom[bottom.shape[0] - width:], 'row', up)  9.89 us
  transfers between devices with their start and end apart: 12, of which 7 were waited for; matrix products, arithmetic and copies ran while one was open for 20% of the time, Pallas kernels for 0%

profile of v7, /device:TPU:8, one launch (start us, length us, event | category | flops | bytes accessed | tf_op | source)
XLA Modules:
  0.0 441.3 jit_solution(16435026930351050044)
XLA Ops:
  10.2 5.3 %fusion.31 = (bf16[128,12,512]{2,1,0:T(8,128)(2,1)}, bf16[128,12,512]{2,1,0:T(8,128)(2,1)}) fusion(bf16[128,32,512]{2,1,0:T(8,128)(2,1)} %param.3), kind=kLoop, calls=%fused_computation.74 | loop fusion | bytes 6291456 | tf_op jit(solution)/shard_map/slice | solution.py:49
  15.5 3.2 copy.77
  18.8 3.2 copy.78
  23.9 5.8 %collective-permute-start.2 = (bf16[24,512,128]{2,1,0:T(8,128)(2,1)}, bf16[24,512,128]{2,1,0:T(8,128)(2,1)}, u32[]{:S(2)}, u32[]{:S(2)}) collective-permute-start(bf16[24,512,128]{2,1,0:T(8,128)(2,1)} %fusion.20), channel_id=1, source_target_pairs={{0,16},{16,32},{32,48},{48,64},{64,80},{80,96},{96,112},{1,17},{17... | collective-permute-start | bytes 9437192 | tf_op jit(solution)/shard_map/ppermute | solution.py:54
  29.8 3.9 collective-permute-start.3
  33.7 5.6 %collective-permute-start.4 = (bf16[24,512,128]{2,1,0:T(8,128)(2,1)}, bf16[24,512,128]{2,1,0:T(8,128)(2,1)}, u32[]{:S(2)}, u32[]{:S(2)}) collective-permute-start(bf16[24,512,128]{2,1,0:T(8,128)(2,1)} %fusion.20), channel_id=1, source_target_pairs={{0,48},{16,64},{32,80},{48,96},{64,112},{1,49},{17,65},{33,81},{49... | collective-permute-start | bytes 9437192 | tf_op jit(solution)/shard_map/ppermute | solution.py:54
  39.3 2.9 collective-permute-start.5
  44.1 5.2 %collective-permute-done = f32[1,512]{1,0:T(1,128)S(1)} collective-permute-done((f32[1,512]{1,0:T(1,128)S(1)}, f32[1,512]{1,0:T(1,128)S(1)}, u32[]{:S(2)}, u32[]{:S(2)}) %collective-permute-start) | collective-permute-done | bytes 2080 | tf_op jit(solution)/shard_map/ppermute | solution.py:14
  52.5 2.9 collective-permute-start.6
  58.4 44.4 %collective-permute-done.2 = bf16[24,512,128]{2,1,0:T(8,128)(2,1)} collective-permute-done((bf16[24,512,128]{2,1,0:T(8,128)(2,1)}, bf16[24,512,128]{2,1,0:T(8,128)(2,1)}, u32[]{:S(2)}, u32[]{:S(2)}) %collective-permute-start.2) | collective-permute-done | bytes 3145760 | tf_op jit(solution)/shard_map/ppermute | solution.py:54
  102.9 7.5 %collective-permute-start.7 = (bf16[24,512,128]{2,1,0:T(8,128)(2,1)}, bf16[24,512,128]{2,1,0:T(8,128)(2,1)S(1)}, u32[]{:S(2)}, u32[]{:S(2)}) collective-permute-start(bf16[24,512,128]{2,1,0:T(8,128)(2,1)} %fusion.20), channel_id=1, source_target_pairs={{0,96},{16,112},{1,97},{17,113},{2,98},{18,114},{3,99},{19,115},{4... | collective-permute-start | bytes 9437192 | tf_op jit(solution)/shard_map/ppermute | solution.py:54
  110.5 133.4 %collective-permute-done.3 = bf16[24,512,128]{2,1,0:T(8,128)(2,1)} collective-permute-done((bf16[24,512,128]{2,1,0:T(8,128)(2,1)}, bf16[24,512,128]{2,1,0:T(8,128)(2,1)}, u32[]{:S(2)}, u32[]{:S(2)}) %collective-permute-start.3) | collective-permute-done | bytes 3145760 | tf_op jit(solution)/shard_map/ppermute | solution.py:54
  243.9 2.9 collective-permute-start.8
  247.7 2.2 gather_fusion
  251.2 4.3 bitcast_dynamic-update-slice_fusion.5
  255.5 4.3 bitcast_dynamic-update-slice_fusion.4
  259.8 4.3 bitcast_dynamic-update-slice_fusion.3
  264.1 80.5 %collective-permute-done.5 = bf16[24,512,128]{2,1,0:T(8,128)(2,1)} collective-permute-done((bf16[24,512,128]{2,1,0:T(8,128)(2,1)}, bf16[24,512,128]{2,1,0:T(8,128)(2,1)}, u32[]{:S(2)}, u32[]{:S(2)}) %collective-permute-start.5) | collective-permute-done | bytes 3145760 | tf_op jit(solution)/shard_map/ppermute | solution.py:54
  344.6 4.3 bitcast_dynamic-update-slice_fusion.2
  349.0 4.3 bitcast_dynamic-update-slice_fusion.1
  357.5 4.3 bitcast_dynamic-update-slice_fusion.7
  361.8 11.8 %convolution_bitcast_fusion = f32[24,128,512]{1,2,0:T(8,128)S(1)} fusion(bf16[8,24,512,128]{3,2,0,1:T(8,128)(2,1)} %bitcast_dynamic-update-slice_fusion.7, bf16[8,128,128]{2,1,0:T(8,128)(2,1)S(1)} %copy-done.5, pred[8]{0:T(512)(128)(4,1)S(1)} %compare_and_fusion.1), kind=kOutput, calls=%fused_computation.40 | convolution fusion | flops 3221356544 | bytes 31719432 | tf_op jit(solution)/shard_map/tes,eijs->itj/dot_general | solution.py:58
  374.7 3.0 collective-permute-start.10
  382.7 3.2 fusion.29
  386.0 4.7 %collective-permute-done.9 = f32[2,128,512]{1,2,0:T(8,128)} collective-permute-done((f32[2,128,512]{1,2,0:T(8,128)}, f32[2,128,512]{1,2,0:T(8,128)}, u32[]{:S(2)}, u32[]{:S(2)}) %collective-permute-start.9) | collective-permute-done | bytes 524320 | tf_op jit(solution)/shard_map/ppermute | solution.py:14
  390.7 3.2 fusion.3
  393.9 2.7 fusion.15
  399.5 3.2 copy.70
  402.7 6.0 %fusion.11 = f32[12,128,512]{1,2,0:T(8,128)S(1)} fusion(f32[12,128,512]{1,2,0:T(8,128)S(1)} %get-tuple-element.8, f32[2,128,512]{1,2,0:T(8,128)} %collective-permute-done.10, f32[12,128,512]{1,2,0:T(8,128)} %get-tuple-element.20, f32[12,512]{1,0:T(8,128)S(1)} %get-tuple-element.16, pred[12]{0:T(512)(128)(4,1)S(1)} %compare_and_fusion), kind=kLoop, calls=%fused_computation.24 | loop fusion | flops 5505024 | bytes 9986060 | tf_op jit(solution)/shard_map/jit(_where)/select_n | solution.py:33
  412.1 6.4 %convolution_bitcast_fusion.1 = f32[8,128,512]{2,1,0:T(8,128)S(1)} fusion(bf16[128,8,128,1]{0,2,3,1:T(8,128)(2,1)S(1)} %bitcast.82, bf16[8,8,512,128]{3,2,1,0:T(8,128)(2,1)} %bitcast.79), kind=kOutput, calls=%fused_computation.48 | convolution fusion | flops 1073741824 | bytes 10747904 | tf_op jit(solution)/shard_map/tes,eijs->itj/dot_general | solution.py:74
  419.5 2.6 fusion.2
  426.2 8.3 %copy.72 = f32[128,32,512]{2,1,0:T(8,128)} copy(f32[128,32,512]{2,0,1:T(8,128)S(1)} %maximum_bitcast_fusion) | data formatting | bytes 16777216 | tf_op jit(solution)/shard_map/transpose | solution.py:78
  (67 shorter events, 37.4 us)
Async XLA Ops:
  6.5 405.6 %all-gather.3.cloned.1.call-start = ((), (), s32[]{:S(2)}) async-start(), calls=%async_computation | async-start | bytes 9437184 | tf_op jit(solution)/shard_map/all_gather | solution.py:47
  22.0 20.2 %copy-start.10 = (f32[32,512]{1,0:T(8,128)S(1)}, f32[32,512]{1,0:T(8,128)}, u32[]{:S(2)}) copy-start(f32[32,512]{1,0:T(8,128)} %param.5) | copy-start | bytes 196612
  22.0 33.4 %copy-start.7 = (bf16[128,1024]{1,0:T(8,128)(2,1)S(1)}, bf16[128,1024]{1,0:T(8,128)(2,1)}, u32[]{:S(2)}) copy-start(bf16[128,1024]{1,0:T(8,128)(2,1)} %param.4) | copy-start | bytes 786436
  23.9 78.9 %collective-permute-start.2 = (bf16[24,512,128]{2,1,0:T(8,128)(2,1)}, bf16[24,512,128]{2,1,0:T(8,128)(2,1)}, u32[]{:S(2)}, u32[]{:S(2)}) collective-permute-start(bf16[24,512,128]{2,1,0:T(8,128)(2,1)} %fusion.20), channel_id=1, source_target_pairs={{0,16},{16,32},{32,48},{48,64},{64,80},{80,96},{96,112},{1,17},{17... | collective-permute-start | bytes 9437192 | tf_op jit(solution)/shard_map/ppermute | solution.py:54
  29.8 214.1 %collective-permute-start.3 = (bf16[24,512,128]{2,1,0:T(8,128)(2,1)}, bf16[24,512,128]{2,1,0:T(8,128)(2,1)}, u32[]{:S(2)}, u32[]{:S(2)}) collective-permute-start(bf16[24,512,128]{2,1,0:T(8,128)(2,1)} %fusion.20), channel_id=1, source_target_pairs={{0,32},{16,48},{32,64},{48,80},{64,96},{80,112},{1,33},{17,49},{33... | collective-permute-start | bytes 9437192 | tf_op jit(solution)/shard_map/ppermute | solution.py:54
  33.7 226.2 %collective-permute-start.4 = (bf16[24,512,128]{2,1,0:T(8,128)(2,1)}, bf16[24,512,128]{2,1,0:T(8,128)(2,1)}, u32[]{:S(2)}, u32[]{:S(2)}) collective-permute-start(bf16[24,512,128]{2,1,0:T(8,128)(2,1)} %fusion.20), channel_id=1, source_target_pairs={{0,48},{16,64},{32,80},{48,96},{64,112},{1,49},{17,65},{33,81},{49... | collective-permute-start | bytes 9437192 | tf_op jit(solution)/shard_map/ppermute | solution.py:54
  39.3 305.4 %collective-permute-start.5 = (bf16[24,512,128]{2,1,0:T(8,128)(2,1)}, bf16[24,512,128]{2,1,0:T(8,128)(2,1)}, u32[]{:S(2)}, u32[]{:S(2)}) collective-permute-start(bf16[24,512,128]{2,1,0:T(8,128)(2,1)} %fusion.20), channel_id=1, source_target_pairs={{0,64},{16,80},{32,96},{48,112},{1,65},{17,81},{33,97},{49,113},{2... | collective-permute-start | bytes 9437192 | tf_op jit(solution)/shard_map/ppermute | solution.py:54
  42.2 7.1 %collective-permute-start = (f32[1,512]{1,0:T(1,128)S(1)}, f32[1,512]{1,0:T(1,128)S(1)}, u32[]{:S(2)}, u32[]{:S(2)}) collective-permute-start(f32[1,512]{1,0:T(1,128)S(1)} %get-tuple-element.18), channel_id=1, source_target_pairs={{0,1},{1,2},{2,3},{3,4},{4,5},{5,6},{6,7},{7,8},{8,9},{9,10},{10,1... | collective-permute-start | bytes 6152 | tf_op jit(solution)/shard_map/ppermute | solution.py:14
  49.3 3.2 collective-permute-start.1
  52.5 296.4 %collective-permute-start.6 = (bf16[24,512,128]{2,1,0:T(8,128)(2,1)}, bf16[24,512,128]{2,1,0:T(8,128)(2,1)}, u32[]{:S(2)}, u32[]{:S(2)}) collective-permute-start(bf16[24,512,128]{2,1,0:T(8,128)(2,1)} %fusion.20), channel_id=1, source_target_pairs={{0,80},{16,96},{32,112},{1,81},{17,97},{33,113},{2,82},{18,98},{34... | collective-permute-start | bytes 9437192 | tf_op jit(solution)/shard_map/ppermute | solution.py:54
  56.3 54.1 %copy-start.6 = (bf16[128,1024]{0,1:T(8,128)(2,1)S(1)}, bf16[128,1024]{0,1:T(8,128)(2,1)}, u32[]{:S(2)}) copy-start(bf16[128,1024]{0,1:T(8,128)(2,1)} %copy.63) | copy-start | bytes 786436
  102.9 250.4 %collective-permute-start.7 = (bf16[24,512,128]{2,1,0:T(8,128)(2,1)}, bf16[24,512,128]{2,1,0:T(8,128)(2,1)S(1)}, u32[]{:S(2)}, u32[]{:S(2)}) collective-permute-start(bf16[24,512,128]{2,1,0:T(8,128)(2,1)} %fusion.20), channel_id=1, source_target_pairs={{0,96},{16,112},{1,97},{17,113},{2,98},{18,114},{3,99},{19,115},{4... | collective-permute-start | bytes 9437192 | tf_op jit(solution)/shard_map/ppermute | solution.py:54
  243.9 113.6 %collective-permute-start.8 = (bf16[24,512,128]{2,1,0:T(8,128)(2,1)}, bf16[24,512,128]{2,1,0:T(8,128)(2,1)}, u32[]{:S(2)}, u32[]{:S(2)}) collective-permute-start(bf16[24,512,128]{2,1,0:T(8,128)(2,1)} %fusion.20), channel_id=1, source_target_pairs={{0,112},{1,113},{2,114},{3,115},{4,116},{5,117},{6,118},{7,119},{8... | collective-permute-start | bytes 9437192 | tf_op jit(solution)/shard_map/ppermute | solution.py:54
  355.4 6.4 %copy-start.5 = (bf16[8,128,128]{2,1,0:T(8,128)(2,1)S(1)}, bf16[8,128,128]{2,1,0:T(8,128)(2,1)}, u32[]{:S(2)}) copy-start(bf16[8,128,128]{2,1,0:T(8,128)(2,1)} %gather_fusion) | copy-start | bytes 786436
  373.6 6.5 %copy-start = (f32[24,128,512]{1,2,0:T(8,128)}, f32[24,128,512]{1,2,0:T(8,128)S(1)}, u32[]{:S(2)}) copy-start(f32[24,128,512]{1,2,0:T(8,128)S(1)} %convolution_bitcast_fusion) | copy-start | bytes 18874372
  374.7 11.2 %collective-permute-start.10 = (f32[2,128,512]{1,2,0:T(8,128)}, f32[2,128,512]{1,2,0:T(8,128)}, u32[]{:S(2)}, u32[]{:S(2)}) collective-permute-start(f32[2,128,512]{1,2,0:T(8,128)} %get-tuple-element.6), channel_id=1, source_target_pairs={{1,0},{2,1},{3,2},{4,3},{5,4},{6,5},{7,6},{8,7},{9,8},{10,9},{11,1... | collective-permute-start | bytes 1572872 | tf_op jit(solution)/shard_map/ppermute | solution.py:15
  377.8 12.9 %collective-permute-start.9 = (f32[2,128,512]{1,2,0:T(8,128)}, f32[2,128,512]{1,2,0:T(8,128)}, u32[]{:S(2)}, u32[]{:S(2)}) collective-permute-start(f32[2,128,512]{1,2,0:T(8,128)} %get-tuple-element.5), channel_id=1, source_target_pairs={{0,1},{1,2},{2,3},{3,4},{4,5},{5,6},{6,7},{7,8},{8,9},{9,10},{10,1... | collective-permute-start | bytes 1572872 | tf_op jit(solution)/shard_map/ppermute | solution.py:14
  390.7 3.2 copy-start.9
  396.6 0.8 copy-start.8
  412.1 6.4 %copy-start.3 = (f32[4,128,512]{2,1,0:T(8,128)S(1)}, f32[4,128,512]{2,1,0:T(8,128)}, u32[]{:S(2)}) copy-start(f32[4,128,512]{2,1,0:T(8,128)} %copy.68) | copy-start | bytes 3145732
  412.1 6.4 %copy-start.4 = (f32[4,128,512]{2,1,0:T(8,128)S(1)}, f32[4,128,512]{2,1,0:T(8,128)}, u32[]{:S(2)}) copy-start(f32[4,128,512]{2,1,0:T(8,128)} %copy.69) | copy-start | bytes 3145732
  422.5 1.7 copy-start.1
  422.5 2.5 copy-start.2
Sparse Core Ops, SparseCore 0:
  10.3 341.1 all-gather.2

commit v8 on v6

--- a/solution.py
+++ b/solution.py
@@ -48,14 +48,24 @@
     edges = jnp.transpose(
         jnp.concatenate([field[:, :EDGE], field[:, slab - EDGE:]], axis=1), (1, 2, 0)
     )
+    a, b = count - 2, count - 1
+    p, q = count - 4, count - 3
     slots = [edges]
     for shift in range(1, count):
-        pairs = [(e, e + shift) for e in range(count - shift)]
+        pairs = [(e, e + shift) for e in range(count - shift) if e + shift < a or e == a]
         slots.append(lax.ppermute(edges, "epoch", pairs))
     stacked = jnp.stack(slots, axis=0)
     source = jnp.clip(me - jnp.arange(count), 0, count - 1)
     weights = jnp.take(lower, source, axis=1)
     timed_edges = jnp.einsum("tes,eijs->itj", weights, stacked, preferred_element_type=jnp.float32)
+    extra = lax.ppermute(edges, "epoch", [(q, p)])
+    target = lax.ppermute(lower, "epoch", [(a, p), (b, q)])
+    partial = jnp.einsum(
+        "tes,eijs->itj", jnp.take(target, source, axis=1), stacked, preferred_element_type=jnp.float32
+    )
+    above_block = lax.dynamic_index_in_dim(target, jnp.clip(me + 1, 0, count - 1), 1, keepdims=False)
+    partial = partial + jnp.einsum("ts,ijs->itj", above_block, extra, preferred_element_type=jnp.float32)
+    timed_edges = timed_edges + lax.ppermute(partial, "epoch", [(p, a), (q, b)])
     top, bottom = timed_edges[:EDGE], timed_edges[EDGE:]
 
     above, below = neighbours(top, bottom, HALO)

time: 404 us -> 503 us (1.25)
  the two profiles are of different devices: /device:TPU:62 before, /device:TPU:103 now
where the time goes in v8:
time: 503 us; the launch traced here: 502 us
  waiting for transfers between devices  338 us (67%)
  local copies, waits for them, and re-layouts  54.2 us (11%)
  matrix products  32.8 us (7%)
  starting transfers between devices  32.5 us (6%)
  other arithmetic  31.3 us (6%)
  between operations  13.8 us (3%)
    ppermute x1, waiting for transfers between devices, body(): timed_edges = timed_edges + lax.ppermute(partial, 'epoch', [(p, a), (q, b)])  272 us
    ppermute x6, waiting for transfers between devices, body(): slots.append(lax.ppermute(edges, 'epoch', pairs))  44.8 us
    unnamed x26, local copies, waits for them, and re-layouts  25.3 us
    ppermute x6, starting transfers between devices, body(): slots.append(lax.ppermute(edges, 'epoch', pairs))  16.2 us
    dot_general x1, matrix products, body(): jnp.einsum('tes,eijs->itj', lower, gathered, preferred_element_type=jnp.f...  13.4 us
    ppermute x1, waiting for transfers between devices, body(): target = lax.ppermute(lower, 'epoch', [(a, p), (b, q)])  11.3 us
  transfers between devices with their start and end apart: 14, of which 6 were waited for; matrix products, arithmetic and copies ran while one was open for 15% of the time, Pallas kernels for 0%

profile of v8, /device:TPU:103, one launch (start us, length us, event | category | flops | bytes accessed | tf_op | source)
XLA Modules:
  0.0 502.2 jit_solution(18399641490754405933)
XLA Ops:
  8.1 3.0 copy.83
  16.4 6.2 %collective-permute-start.2 = (bf16[16,512,128]{2,1,0:T(8,128)(2,1)}, bf16[16,512,128]{2,1,0:T(8,128)(2,1)}, u32[]{:S(2)}, u32[]{:S(2)}) collective-permute-start(bf16[16,512,128]{2,1,0:T(8,128)(2,1)} %fusion.21), channel_id=1, source_target_pairs={{0,16},{16,32},{32,48},{48,64},{64,80},{96,112},{1,17},{17,33},{33... | collective-permute-start | bytes 6291464 | tf_op jit(solution)/shard_map/ppermute | solution.py:56
  26.6 2.0 collective-permute-start.5
  30.2 11.3 %collective-permute-done.8 = bf16[128,8,128]{0,2,1:T(8,128)(2,1)S(1)} collective-permute-done((bf16[128,8,128]{0,2,1:T(8,128)(2,1)S(1)}, bf16[128,8,128]{0,2,1:T(8,128)(2,1)S(1)}, u32[]{:S(2)}, u32[]{:S(2)}) %collective-permute-start.8) | collective-permute-done | bytes 262176 | tf_op jit(solution)/shard_map/ppermute | solution.py:62
  43.5 44.8 %collective-permute-done.2 = bf16[16,512,128]{2,1,0:T(8,128)(2,1)} collective-permute-done((bf16[16,512,128]{2,1,0:T(8,128)(2,1)}, bf16[16,512,128]{2,1,0:T(8,128)(2,1)}, u32[]{:S(2)}, u32[]{:S(2)}) %collective-permute-start.2) | collective-permute-done | bytes 2097184 | tf_op jit(solution)/shard_map/ppermute | solution.py:56
  92.5 3.3 bitcast_dynamic-update-slice_fusion.4
  96.6 3.3 bitcast_dynamic-update-slice_fusion.3
  100.0 3.3 bitcast_dynamic-update-slice_fusion.2
  103.3 3.4 bitcast_dynamic-update-slice_fusion.1
  106.7 3.4 bitcast_dynamic-update-slice_fusion
  110.1 3.4 bitcast_dynamic-update-slice_fusion.6
  113.4 3.4 bitcast_dynamic-update-slice_fusion.7
  116.8 8.3 %fusion.23 = f32[16,512,128,1]{2,1,3,0:T(8,128)S(1)} fusion(bf16[8,16,512,128]{3,2,0,1:T(8,128)(2,1)} %bitcast_dynamic-update-slice_fusion.7, bf16[8,128,128]{1,2,0:T(8,128)(2,1)S(1)} %gather_fusion.1, pred[8]{0:T(512)(128)(4,1)S(1)} %compare_and_fusion), kind=kOutput, calls=%fused_computation.54 | convolution fusion | flops 2147614720 | bytes 21233672 | tf_op jit(solution)/shard_map/tes,eijs->itj/dot_general | solution.py:63
  125.1 2.7 fusion.6
  129.1 3.7 collective-permute-start
  132.8 2.1 collective-permute-start.1
  136.8 3.0 collective-permute-done.1
  140.4 8.3 %fusion.25 = f32[16,512,128,1]{2,1,3,0:T(8,128)S(1)} fusion(bf16[8,16,512,128]{3,2,0,1:T(8,128)(2,1)} %bitcast_dynamic-update-slice_fusion.7, bf16[8,128,128]{2,1,0:T(8,128)(2,1)S(1)} %gather_fusion, pred[8]{0:T(512)(128)(4,1)S(1)} %compare_and_fusion), kind=kOutput, calls=%fused_computation.56 | convolution fusion | flops 2147614720 | bytes 21233672 | tf_op jit(solution)/shard_map/tes,eijs->itj/dot_general | solution.py:60
  148.8 271.9 %collective-permute-done.10 = f32[16,128,512]{1,2,0:T(8,128)} collective-permute-done((f32[16,128,512]{1,2,0:T(8,128)}, f32[16,128,512]{1,2,0:T(8,128)}, u32[]{:S(2)}, u32[]{:S(2)}) %collective-permute-start.10) | collective-permute-done | bytes 4194336 | tf_op jit(solution)/shard_map/ppermute | solution.py:68
  420.7 2.7 bitcast_add_fusion
  424.6 5.3 %collective-permute-start.11 = (f32[2,128,512]{1,2,0:T(8,128)}, f32[2,128,512]{1,2,0:T(8,128)}, u32[]{:S(2)}, u32[]{:S(2)}) collective-permute-start(f32[2,128,512]{1,2,0:T(8,128)} %get-tuple-element.6), channel_id=1, source_target_pairs={{0,1},{1,2},{2,3},{3,4},{4,5},{5,6},{6,7},{7,8},{8,9},{9,10},{10,1... | collective-permute-start | bytes 1572872 | tf_op jit(solution)/shard_map/ppermute | solution.py:14
  433.6 2.5 fusion.42
  436.3 6.5 %collective-permute-done.12 = f32[2,128,512]{1,2,0:T(8,128)} collective-permute-done((f32[2,128,512]{1,2,0:T(8,128)}, f32[2,128,512]{1,2,0:T(8,128)}, u32[]{:S(2)}, u32[]{:S(2)}) %collective-permute-start.12) | collective-permute-done | bytes 524320 | tf_op jit(solution)/shard_map/ppermute | solution.py:15
  442.8 2.7 fusion.7
  449.2 3.1 copy.71
  452.3 4.0 fusion.12
  458.7 13.4 %convolution_bitcast_fusion = f32[16,128,512]{2,1,0:T(8,128)} fusion(bf16[128,8,128,1]{0,2,3,1:T(8,128)(2,1)S(1)} %bitcast.99, bf16[8,16,512,128]{3,2,1,0:T(8,128)(2,1)} %bitcast.95), kind=kOutput, calls=%fused_computation.23 | convolution fusion | flops 2147483648 | bytes 21233664 | tf_op jit(solution)/shard_map/tes,eijs->itj/dot_general | solution.py:84
  472.1 2.9 pad_maximum_fusion
  476.0 4.3 fusion.2
  481.0 3.7 fusion.5
  484.7 2.4 maximum_bitcast_fusion
  487.1 8.3 %copy.73 = f32[128,32,512]{2,1,0:T(8,128)} copy(f32[128,32,512]{2,0,1:T(8,128)S(1)} %maximum_bitcast_fusion) | data formatting | bytes 16777216 | tf_op jit(solution)/shard_map/transpose | solution.py:88
  (71 shorter events, 35.9 us)
Async XLA Ops:
  6.5 1.6 slice-start
  6.5 452.2 %all-gather.3.cloned.1.call-start = ((), (), s32[]{:S(2)}) async-start(), calls=%async_computation | async-start | bytes 18874368 | tf_op jit(solution)/shard_map/all_gather | solution.py:47
  14.9 13.7 %copy-start.3 = (bf16[128,1024]{1,0:T(8,128)(2,1)S(1)}, bf16[128,1024]{1,0:T(8,128)(2,1)}, u32[]{:S(2)}) copy-start(bf16[128,1024]{1,0:T(8,128)(2,1)} %param.6) | copy-start | bytes 786436
  16.4 71.9 %collective-permute-start.2 = (bf16[16,512,128]{2,1,0:T(8,128)(2,1)}, bf16[16,512,128]{2,1,0:T(8,128)(2,1)}, u32[]{:S(2)}, u32[]{:S(2)}) collective-permute-start(bf16[16,512,128]{2,1,0:T(8,128)(2,1)} %fusion.21), channel_id=1, source_target_pairs={{0,16},{16,32},{32,48},{48,64},{64,80},{96,112},{1,17},{17,33},{33... | collective-permute-start | bytes 6291464 | tf_op jit(solution)/shard_map/ppermute | solution.py:56
  22.6 73.3 %collective-permute-start.3 = (bf16[16,512,128]{2,1,0:T(8,128)(2,1)}, bf16[16,512,128]{2,1,0:T(8,128)(2,1)}, u32[]{:S(2)}, u32[]{:S(2)}) collective-permute-start(bf16[16,512,128]{2,1,0:T(8,128)(2,1)} %fusion.21), channel_id=1, source_target_pairs={{0,32},{16,48},{32,64},{48,80},{1,33},{17,49},{33,65},{49,81},{2,3... | collective-permute-start | bytes 6291464 | tf_op jit(solution)/shard_map/ppermute | solution.py:56
  24.5 75.4 %collective-permute-start.4 = (bf16[16,512,128]{2,1,0:T(8,128)(2,1)}, bf16[16,512,128]{2,1,0:T(8,128)(2,1)}, u32[]{:S(2)}, u32[]{:S(2)}) collective-permute-start(bf16[16,512,128]{2,1,0:T(8,128)(2,1)} %fusion.21), channel_id=1, source_target_pairs={{0,48},{16,64},{32,80},{1,49},{17,65},{33,81},{2,50},{18,66},{34,8... | collective-permute-start | bytes 6291464 | tf_op jit(solution)/shard_map/ppermute | solution.py:56
  26.6 76.7 %collective-permute-start.5 = (bf16[16,512,128]{2,1,0:T(8,128)(2,1)}, bf16[16,512,128]{2,1,0:T(8,128)(2,1)}, u32[]{:S(2)}, u32[]{:S(2)}) collective-permute-start(bf16[16,512,128]{2,1,0:T(8,128)(2,1)} %fusion.21), channel_id=1, source_target_pairs={{0,64},{16,80},{1,65},{17,81},{2,66},{18,82},{3,67},{19,83},{4,68}... | collective-permute-start | bytes 6291464 | tf_op jit(solution)/shard_map/ppermute | solution.py:56
  28.9 12.6 %collective-permute-start.8 = (bf16[128,8,128]{0,2,1:T(8,128)(2,1)S(1)}, bf16[128,8,128]{0,2,1:T(8,128)(2,1)S(1)}, u32[]{:S(2)}, u32[]{:S(2)}) collective-permute-start(bf16[128,8,128]{0,2,1:T(8,128)(2,1)S(1)} %bitcast.97), channel_id=1, source_target_pairs={{96,64},{112,80},{97,65},{113,81},{98,66},{114,82},{99,67},{115,83... | collective-permute-start | bytes 786440 | tf_op jit(solution)/shard_map/ppermute | solution.py:62
  41.5 65.2 %collective-permute-start.6 = (bf16[16,512,128]{2,1,0:T(8,128)(2,1)}, bf16[16,512,128]{2,1,0:T(8,128)(2,1)}, u32[]{:S(2)}, u32[]{:S(2)}) collective-permute-start(bf16[16,512,128]{2,1,0:T(8,128)(2,1)} %fusion.21), channel_id=1, source_target_pairs={{0,80},{1,81},{2,82},{3,83},{4,84},{5,85},{6,86},{7,87},{8,88},{9,... | collective-permute-start | bytes 6291464 | tf_op jit(solution)/shard_map/ppermute | solution.py:56
  88.3 21.8 %collective-permute-start.7 = (bf16[16,512,128]{2,1,0:T(8,128)(2,1)}, bf16[16,512,128]{2,1,0:T(8,128)(2,1)}, u32[]{:S(2)}, u32[]{:S(2)}) collective-permute-start(bf16[16,512,128]{2,1,0:T(8,128)(2,1)} %fusion.21), channel_id=1, source_target_pairs={} | collective-permute-start | bytes 6291464 | tf_op jit(solution)/shard_map/ppermute | solution.py:56
  95.8 29.2 %collective-permute-start.9 = (bf16[16,512,128]{2,1,0:T(8,128)(2,1)}, bf16[16,512,128]{2,1,0:T(8,128)(2,1)S(1)}, u32[]{:S(2)}, u32[]{:S(2)}) collective-permute-start(bf16[16,512,128]{2,1,0:T(8,128)(2,1)} %fusion.21), channel_id=1, source_target_pairs={{80,64},{81,65},{82,66},{83,67},{84,68},{85,69},{86,70},{87,71},{8... | collective-permute-start | bytes 6291464 | tf_op jit(solution)/shard_map/ppermute | solution.py:61
  125.1 4.0 copy-start.4
  127.8 292.9 %collective-permute-start.10 = (f32[16,128,512]{1,2,0:T(8,128)}, f32[16,128,512]{1,2,0:T(8,128)}, u32[]{:S(2)}, u32[]{:S(2)}) collective-permute-start(f32[16,128,512]{1,2,0:T(8,128)} %fusion.6), channel_id=1, source_target_pairs={{64,96},{80,112},{65,97},{81,113},{66,98},{82,114},{67,99},{83,115... | collective-permute-start | bytes 12582920 | tf_op jit(solution)/shard_map/ppermute | solution.py:68
  129.1 7.7 %collective-permute-start = (f32[1,512]{1,0:T(1,128)S(1)}, f32[1,512]{1,0:T(1,128)S(1)}, u32[]{:S(2)}, u32[]{:S(2)}) collective-permute-start(f32[1,512]{1,0:T(1,128)S(1)} %get-tuple-element.18), channel_id=1, source_target_pairs={{0,1},{1,2},{2,3},{3,4},{4,5},{5,6},{6,7},{7,8},{8,9},{9,10},{10,1... | collective-permute-start | bytes 6152 | tf_op jit(solution)/shard_map/ppermute | solution.py:14
  132.8 7.0 %collective-permute-start.1 = (f32[1,512]{1,0:T(1,128)S(1)}, f32[1,512]{1,0:T(1,128)S(1)}, u32[]{:S(2)}, u32[]{:S(2)}) collective-permute-start(f32[1,512]{1,0:T(1,128)S(1)} %get-tuple-element.19), channel_id=1, source_target_pairs={{1,0},{2,1},{3,2},{4,3},{5,4},{6,5},{7,6},{8,7},{9,8},{10,9},{11,1... | collective-permute-start | bytes 6152 | tf_op jit(solution)/shard_map/ppermute | solution.py:15
  423.4 8.5 %copy-start = (f32[16,128,512]{1,2,0:T(8,128)}, f32[16,128,512]{1,2,0:T(8,128)S(1)}, u32[]{:S(2)}) copy-start(f32[16,128,512]{1,2,0:T(8,128)S(1)} %bitcast_add_fusion) | copy-start | bytes 12582916
  424.6 11.7 %collective-permute-start.11 = (f32[2,128,512]{1,2,0:T(8,128)}, f32[2,128,512]{1,2,0:T(8,128)}, u32[]{:S(2)}, u32[]{:S(2)}) collective-permute-start(f32[2,128,512]{1,2,0:T(8,128)} %get-tuple-element.6), channel_id=1, source_target_pairs={{0,1},{1,2},{2,3},{3,4},{4,5},{5,6},{6,7},{7,8},{8,9},{9,10},{10,1... | collective-permute-start | bytes 1572872 | tf_op jit(solution)/shard_map/ppermute | solution.py:14
  429.9 12.9 %collective-permute-start.12 = (f32[2,128,512]{1,2,0:T(8,128)}, f32[2,128,512]{1,2,0:T(8,128)}, u32[]{:S(2)}, u32[]{:S(2)}) collective-permute-start(f32[2,128,512]{1,2,0:T(8,128)} %get-tuple-element.7), channel_id=1, source_target_pairs={{1,0},{2,1},{3,2},{4,3},{5,4},{6,5},{7,6},{8,7},{9,8},{10,9},{11,1... | collective-permute-start | bytes 1572872 | tf_op jit(solution)/shard_map/ppermute | solution.py:15
  442.8 2.7 copy-start.5
  442.8 2.7 copy-start.7
  449.2 3.1 copy-start.6
  458.7 13.4 %copy-start.2 = (f32[4,128,512]{2,1,0:T(8,128)S(1)}, f32[4,128,512]{2,1,0:T(8,128)}, u32[]{:S(2)}) copy-start(f32[4,128,512]{2,1,0:T(8,128)} %copy.70) | copy-start | bytes 3145732
  480.9 3.7 copy-start.1
Sparse Core Ops, SparseCore 0:
  11.3 375.2 all-gather.2

commit v9 on v7

--- a/solution.py
+++ b/solution.py
@@ -3,7 +3,7 @@
 from jax import lax
 from jax.sharding import PartitionSpec as P
 
-EDGE = 12
+EDGE = 10
 HALO = 2
 
 

time: 442 us -> 407 us (0.921)
  the two profiles are of different devices: /device:TPU:8 before, /device:TPU:62 now
where the time goes in v9:
time: 407 us
  waiting for transfers between devices  274 us (67%)
  local copies, waits for them, and re-layouts  51.7 us (13%)
  starting transfers between devices  26 us (6%)
  other arithmetic  25.9 us (6%)
  matrix products  14.6 us (4%)
  between operations  13.9 us (3%)
    ppermute x7, waiting for transfers between devices, body(): slots.append(lax.ppermute(edges, 'epoch', pairs))  174 us
    all_gather x1, waiting for transfers between devices, body(): gathered = lax.all_gather(middle, 'epoch', axis=0)  99.1 us
    unnamed x40, local copies, waits for them, and re-layouts  18.1 us
    ppermute x7, starting transfers between devices, body(): slots.append(lax.ppermute(edges, 'epoch', pairs))  16.5 us
    dot_general x1, matrix products, body(): jnp.einsum('tes,eijs->itj', lower, gathered, preferred_element_type=jnp.f...  8.91 us
    transpose x1, local copies, waits for them, and re-layouts, body(): return jnp.transpose(product, (1, 0, 2))  8.25 us
  transfers between devices with their start and end apart: 12, of which 4 were waited for; matrix products, arithmetic and copies ran while one was open for 14% of the time, Pallas kernels for 0%

profile of v9, /device:TPU:62, one launch (start us, length us, event | category | flops | bytes accessed | tf_op | source)
XLA Modules:
  0.0 406.5 jit_solution(3640503393351229490)
XLA Ops:
  6.5 3.0 slice.165
  9.6 2.9 copy.79
  12.5 4.6 %fusion.31 = (bf16[128,10,512]{2,1,0:T(8,128)(2,1)S(1)}, bf16[128,10,512]{2,1,0:T(8,128)(2,1)}) fusion(bf16[128,32,512]{2,1,0:T(8,128)(2,1)} %param.3), kind=kLoop, calls=%fused_computation.74 | loop fusion | bytes 5242880 | tf_op jit(solution)/shard_map/slice | solution.py:49
  18.8 3.1 copy.78
  23.7 4.5 %collective-permute-start.2 = (bf16[20,512,128]{2,1,0:T(8,128)(2,1)}, bf16[20,512,128]{2,1,0:T(8,128)(2,1)}, u32[]{:S(2)}, u32[]{:S(2)}) collective-permute-start(bf16[20,512,128]{2,1,0:T(8,128)(2,1)} %fusion.20), channel_id=1, source_target_pairs={{0,16},{16,32},{32,48},{48,64},{64,80},{80,96},{96,112},{1,17},{17... | collective-permute-start | bytes 7864328 | tf_op jit(solution)/shard_map/ppermute | solution.py:54
  28.2 3.5 collective-permute-start.3
  31.7 3.0 collective-permute-start.4
  34.7 2.8 collective-permute-start.5
  37.6 1.9 collective-permute-start
  42.5 2.2 collective-permute-start.1
  47.1 54.3 %collective-permute-done.2 = bf16[20,512,128]{2,1,0:T(8,128)(2,1)} collective-permute-done((bf16[20,512,128]{2,1,0:T(8,128)(2,1)}, bf16[20,512,128]{2,1,0:T(8,128)(2,1)}, u32[]{:S(2)}, u32[]{:S(2)}) %collective-permute-start.2) | collective-permute-done | bytes 2621472 | tf_op jit(solution)/shard_map/ppermute | solution.py:54
  102.2 119.6 %collective-permute-done.3 = bf16[20,512,128]{2,1,0:T(8,128)(2,1)} collective-permute-done((bf16[20,512,128]{2,1,0:T(8,128)(2,1)}, bf16[20,512,128]{2,1,0:T(8,128)(2,1)}, u32[]{:S(2)}, u32[]{:S(2)}) %collective-permute-start.3) | collective-permute-done | bytes 2621472 | tf_op jit(solution)/shard_map/ppermute | solution.py:54
  224.1 2.2 bitcast_dynamic-update-slice_fusion.5
  226.2 2.2 bitcast_dynamic-update-slice_fusion.4
  228.4 2.2 bitcast_dynamic-update-slice_fusion.3
  230.6 2.2 bitcast_dynamic-update-slice_fusion.2
  234.2 5.7 %convolution_bitcast_fusion = f32[20,128,512]{1,2,0:T(8,128)S(1)} fusion(bf16[8,20,512,128]{3,2,0,1:T(8,128)(2,1)S(1)} %bitcast_dynamic-update-slice_fusion.7, bf16[8,128,128]{2,1,0:T(8,128)(2,1)S(1)} %gather_fusion, pred[8]{0:T(512)(128)(4,1)S(1)} %copy-done.12), kind=kOutput, calls=%fused_computation.40 | convolution fusion | flops 2684485632 | bytes 26476552 | tf_op jit(solution)/shard_map/tes,eijs->itj/dot_general | solution.py:58
  241.0 1.9 collective-permute-start.10
  243.0 3.4 collective-permute-start.9
  247.5 2.6 copy.68
  251.4 2.9 fusion.29
  254.4 3.0 fusion.6
  257.4 2.4 fusion.15
  260.6 1.8 fusion.19
  262.3 2.9 copy.70
  265.3 5.2 %fusion.11 = f32[10,128,512]{1,2,0:T(8,128)S(1)} fusion(f32[10,128,512]{1,2,0:T(8,128)S(1)} %get-tuple-element.8, f32[2,128,512]{1,2,0:T(8,128)} %collective-permute-done.10, f32[10,128,512]{1,2,0:T(8,128)} %get-tuple-element.19, f32[10,512]{1,0:T(8,128)S(1)} %copy-done.8, pred[10]{0:T(512)(128)(4,1)S(1)} %copy-done.13), kind=kLoop, calls=%fused_computation.25 | loop fusion | flops 4587520 | bytes 8409098 | tf_op jit(solution)/shard_map/jit(_where)/select_n | solution.py:33
  271.6 1.8 copy.71
  273.4 99.1 %all-gather.3.cloned.1.call-done = bf16[96,512,128]{2,1,0:T(8,128)(2,1)} async-done(((bf16[12,512,128]{2,1,0:T(8,128)(2,1)}), bf16[96,512,128]{2,1,0:T(8,128)(2,1)}) %all-gather.3.cloned.1.call-update) | async-done | bytes 12582928 | tf_op jit(solution)/shard_map/all_gather | solution.py:47
  372.5 8.9 %convolution_bitcast_fusion.1 = f32[12,128,512]{2,1,0:T(8,128)S(1)} fusion(bf16[128,8,128,1]{0,2,3,1:T(8,128)(2,1)S(1)} %bitcast.82, bf16[8,12,512,128]{3,2,1,0:T(8,128)(2,1)} %bitcast.79), kind=kOutput, calls=%fused_computation.47 | convolution fusion | flops 1610612736 | bytes 15990784 | tf_op jit(solution)/shard_map/tes,eijs->itj/dot_general | solution.py:74
  382.8 3.5 fusion.2
  386.8 2.8 fusion.5
  391.4 8.3 %copy.72 = f32[128,32,512]{2,1,0:T(8,128)} copy(f32[128,32,512]{2,0,1:T(8,128)S(1)} %maximum_bitcast_fusion) | data formatting | bytes 16777216 | tf_op jit(solution)/shard_map/transpose | solution.py:78
  (76 shorter events, 22.2 us)
Async XLA Ops:
  6.5 365.9 %all-gather.3.cloned.1.call-start = ((), (), s32[]{:S(2)}) async-start(), calls=%async_computation | async-start | bytes 14155776 | tf_op jit(solution)/shard_map/all_gather | solution.py:47
  21.9 15.7 %copy-start.10 = (f32[32,512]{1,0:T(8,128)S(1)}, f32[32,512]{1,0:T(8,128)}, u32[]{:S(2)}) copy-start(f32[32,512]{1,0:T(8,128)} %param.5) | copy-start | bytes 196612
  21.9 17.6 %copy-start.7 = (bf16[128,1024]{1,0:T(8,128)(2,1)S(1)}, bf16[128,1024]{1,0:T(8,128)(2,1)}, u32[]{:S(2)}) copy-start(bf16[128,1024]{1,0:T(8,128)(2,1)} %param.4) | copy-start | bytes 786436
  23.7 77.7 %collective-permute-start.2 = (bf16[20,512,128]{2,1,0:T(8,128)(2,1)}, bf16[20,512,128]{2,1,0:T(8,128)(2,1)}, u32[]{:S(2)}, u32[]{:S(2)}) collective-permute-start(bf16[20,512,128]{2,1,0:T(8,128)(2,1)} %fusion.20), channel_id=1, source_target_pairs={{0,16},{16,32},{32,48},{48,64},{64,80},{80,96},{96,112},{1,17},{17... | collective-permute-start | bytes 7864328 | tf_op jit(solution)/shard_map/ppermute | solution.py:54
  28.2 193.7 %collective-permute-start.3 = (bf16[20,512,128]{2,1,0:T(8,128)(2,1)}, bf16[20,512,128]{2,1,0:T(8,128)(2,1)}, u32[]{:S(2)}, u32[]{:S(2)}) collective-permute-start(bf16[20,512,128]{2,1,0:T(8,128)(2,1)} %fusion.20), channel_id=1, source_target_pairs={{0,32},{16,48},{32,64},{48,80},{64,96},{80,112},{1,33},{17,49},{33... | collective-permute-start | bytes 7864328 | tf_op jit(solution)/shard_map/ppermute | solution.py:54
  31.7 196.7 %collective-permute-start.4 = (bf16[20,512,128]{2,1,0:T(8,128)(2,1)}, bf16[20,512,128]{2,1,0:T(8,128)(2,1)}, u32[]{:S(2)}, u32[]{:S(2)}) collective-permute-start(bf16[20,512,128]{2,1,0:T(8,128)(2,1)} %fusion.20), channel_id=1, source_target_pairs={{0,48},{16,64},{32,80},{48,96},{64,112},{1,49},{17,65},{33,81},{49... | collective-permute-start | bytes 7864328 | tf_op jit(solution)/shard_map/ppermute | solution.py:54
  34.7 195.8 %collective-permute-start.5 = (bf16[20,512,128]{2,1,0:T(8,128)(2,1)}, bf16[20,512,128]{2,1,0:T(8,128)(2,1)}, u32[]{:S(2)}, u32[]{:S(2)}) collective-permute-start(bf16[20,512,128]{2,1,0:T(8,128)(2,1)} %fusion.20), channel_id=1, source_target_pairs={{0,64},{16,80},{32,96},{48,112},{1,65},{17,81},{33,97},{49,113},{2... | collective-permute-start | bytes 7864328 | tf_op jit(solution)/shard_map/ppermute | solution.py:54
  37.6 4.9 %collective-permute-start = (f32[1,512]{1,0:T(1,128)S(1)}, f32[1,512]{1,0:T(1,128)S(1)}, u32[]{:S(2)}, u32[]{:S(2)}) collective-permute-start(f32[1,512]{1,0:T(1,128)S(1)} %get-tuple-element.17), channel_id=1, source_target_pairs={{0,1},{1,2},{2,3},{3,4},{4,5},{5,6},{6,7},{7,8},{8,9},{9,10},{10,1... | collective-permute-start | bytes 6152 | tf_op jit(solution)/shard_map/ppermute | solution.py:14
  39.8 7.3 %copy-start.5 = (bf16[128,1024]{0,1:T(8,128)(2,1)}, bf16[128,1024]{0,1:T(8,128)(2,1)S(1)}, u32[]{:S(2)}) copy-start(bf16[128,1024]{0,1:T(8,128)(2,1)S(1)} %fusion.21) | copy-start | bytes 786436
  42.5 3.6 collective-permute-start.1
  46.1 186.7 %collective-permute-start.6 = (bf16[20,512,128]{2,1,0:T(8,128)(2,1)}, bf16[20,512,128]{2,1,0:T(8,128)(2,1)S(1)}, u32[]{:S(2)}, u32[]{:S(2)}) collective-permute-start(bf16[20,512,128]{2,1,0:T(8,128)(2,1)} %fusion.20), channel_id=1, source_target_pairs={{0,80},{16,96},{32,112},{1,81},{17,97},{33,113},{2,82},{18,98},{34... | collective-permute-start | bytes 7864328 | tf_op jit(solution)/shard_map/ppermute | solution.py:54
  101.4 131.8 %collective-permute-start.7 = (bf16[20,512,128]{2,1,0:T(8,128)(2,1)}, bf16[20,512,128]{2,1,0:T(8,128)(2,1)S(1)}, u32[]{:S(2)}, u32[]{:S(2)}) collective-permute-start(bf16[20,512,128]{2,1,0:T(8,128)(2,1)} %fusion.20), channel_id=1, source_target_pairs={{0,96},{16,112},{1,97},{17,113},{2,98},{18,114},{3,99},{19,115},{4... | collective-permute-start | bytes 7864328 | tf_op jit(solution)/shard_map/ppermute | solution.py:54
  221.8 11.8 %collective-permute-start.8 = (bf16[20,512,128]{2,1,0:T(8,128)(2,1)}, bf16[20,512,128]{2,1,0:T(8,128)(2,1)S(1)}, u32[]{:S(2)}, u32[]{:S(2)}) collective-permute-start(bf16[20,512,128]{2,1,0:T(8,128)(2,1)} %fusion.20), channel_id=1, source_target_pairs={{0,112},{1,113},{2,114},{3,115},{4,116},{5,117},{6,118},{7,119},{8... | collective-permute-start | bytes 7864328 | tf_op jit(solution)/shard_map/ppermute | solution.py:54
  233.6 0.6 copy-start.12
  239.9 7.6 %copy-start = (f32[20,128,512]{1,2,0:T(8,128)}, f32[20,128,512]{1,2,0:T(8,128)S(1)}, u32[]{:S(2)}) copy-start(f32[20,128,512]{1,2,0:T(8,128)S(1)} %convolution_bitcast_fusion) | copy-start | bytes 15728644
  241.0 13.3 %collective-permute-start.10 = (f32[2,128,512]{1,2,0:T(8,128)}, f32[2,128,512]{1,2,0:T(8,128)}, u32[]{:S(2)}, u32[]{:S(2)}) collective-permute-start(f32[2,128,512]{1,2,0:T(8,128)} %get-tuple-element.6), channel_id=1, source_target_pairs={{1,0},{2,1},{3,2},{4,3},{5,4},{6,5},{7,6},{8,7},{9,8},{10,9},{11,1... | collective-permute-start | bytes 1572872 | tf_op jit(solution)/shard_map/ppermute | solution.py:15
  243.0 11.4 %collective-permute-start.9 = (f32[2,128,512]{1,2,0:T(8,128)}, f32[2,128,512]{1,2,0:T(8,128)}, u32[]{:S(2)}, u32[]{:S(2)}) collective-permute-start(f32[2,128,512]{1,2,0:T(8,128)} %get-tuple-element.5), channel_id=1, source_target_pairs={{0,1},{1,2},{2,3},{3,4},{4,5},{5,6},{6,7},{7,8},{8,9},{9,10},{10,1... | collective-permute-start | bytes 1572872 | tf_op jit(solution)/shard_map/ppermute | solution.py:14
  254.3 3.0 copy-start.9
  254.4 3.0 copy-start.14
  259.8 0.7 copy-start.11
  262.3 2.9 copy-start.8
  262.3 2.9 copy-start.13
  271.6 100.9 %copy-start.6 = (bf16[128,1024]{0,1:T(8,128)(2,1)S(1)}, bf16[128,1024]{0,1:T(8,128)(2,1)}, u32[]{:S(2)}) copy-start(bf16[128,1024]{0,1:T(8,128)(2,1)} %copy-done.5) | copy-start | bytes 786436
  372.5 8.9 %copy-start.3 = (f32[4,128,512]{2,1,0:T(8,128)S(1)}, f32[4,128,512]{2,1,0:T(8,128)}, u32[]{:S(2)}) copy-start(f32[4,128,512]{2,1,0:T(8,128)} %copy.68) | copy-start | bytes 3145732
  372.5 8.9 %copy-start.4 = (f32[4,128,512]{2,1,0:T(8,128)S(1)}, f32[4,128,512]{2,1,0:T(8,128)}, u32[]{:S(2)}) copy-start(f32[4,128,512]{2,1,0:T(8,128)} %copy.69) | copy-start | bytes 3145732
  386.8 2.9 copy-start.1
  386.8 2.9 copy-start.2
Sparse Core Ops, SparseCore 0:
  12.6 359.8 all-gather.2

commit v10 on v8

--- a/solution.py
+++ b/solution.py
@@ -49,10 +49,11 @@
         jnp.concatenate([field[:, :EDGE], field[:, slab - EDGE:]], axis=1), (1, 2, 0)
     )
     a, b = count - 2, count - 1
-    p, q = count - 4, count - 3
+    p, q = a - 4, b - 4
+    r, s = a - 6, b - 6
     slots = [edges]
     for shift in range(1, count):
-        pairs = [(e, e + shift) for e in range(count - shift) if e + shift < a or e == a]
+        pairs = [(e, e + shift) for e in range(count - shift) if not (e + shift >= a and e <= q)]
         slots.append(lax.ppermute(edges, "epoch", pairs))
     stacked = jnp.stack(slots, axis=0)
     source = jnp.clip(me - jnp.arange(count), 0, count - 1)
@@ -60,12 +61,17 @@
     timed_edges = jnp.einsum("tes,eijs->itj", weights, stacked, preferred_element_type=jnp.float32)
     extra = lax.ppermute(edges, "epoch", [(q, p)])
     target = lax.ppermute(lower, "epoch", [(a, p), (b, q)])
+    near = q - p + 3
     partial = jnp.einsum(
-        "tes,eijs->itj", jnp.take(target, source, axis=1), stacked, preferred_element_type=jnp.float32
+        "tes,eijs->itj",
+        jnp.take(target, source[:near], axis=1),
+        jnp.stack(slots[:near], axis=0),
+        preferred_element_type=jnp.float32,
     )
     above_block = lax.dynamic_index_in_dim(target, jnp.clip(me + 1, 0, count - 1), 1, keepdims=False)
     partial = partial + jnp.einsum("ts,ijs->itj", above_block, extra, preferred_element_type=jnp.float32)
-    timed_edges = timed_edges + lax.ppermute(partial, "epoch", [(p, a), (q, b)])
+    relayed = lax.ppermute(partial, "epoch", [(p, r), (q, s)])
+    timed_edges = timed_edges + lax.ppermute(relayed, "epoch", [(r, a), (s, b)])
     top, bottom = timed_edges[:EDGE], timed_edges[EDGE:]
 
     above, below = neighbours(top, bottom, HALO)

time: 503 us -> 521 us (1.036)
  the two profiles are of different devices: /device:TPU:103 before, /device:TPU:7 now
where the time goes in v10:
time: 521 us; the launch traced here: 520 us
  waiting for transfers between devices  349 us (67%)
  local copies, waits for them, and re-layouts  51.4 us (10%)
  starting transfers between devices  43.9 us (8%)
  matrix products  32 us (6%)
  other arithmetic  29.9 us (6%)
  between operations  13.8 us (3%)
    ppermute x6, waiting for transfers between devices, body(): slots.append(lax.ppermute(edges, 'epoch', pairs))  159 us
    ppermute x1, waiting for transfers between devices, body(): relayed = lax.ppermute(partial, 'epoch', [(p, r), (q, s)])  121 us
    ppermute x1, waiting for transfers between devices, body(): timed_edges = timed_edges + lax.ppermute(relayed, 'epoch', [(r, a), (s, b)])  60.5 us
    ppermute x6, starting transfers between devices, body(): slots.append(lax.ppermute(edges, 'epoch', pairs))  26.6 us
    unnamed x26, local copies, waits for them, and re-layouts  24.3 us
    dot_general x1, matrix products, body(): jnp.einsum('tes,eijs->itj', lower, gathered, preferred_element_type=jnp.f...  13.4 us
  transfers between devices with their start and end apart: 15, of which 7 were waited for; matrix products, arithmetic and copies ran while one was open for 14% of the time, Pallas kernels for 0%

profile of v10, /device:TPU:7, one launch (start us, length us, event | category | flops | bytes accessed | tf_op | source)
XLA Modules:
  0.0 519.7 jit_solution(16099567122157393431)
XLA Ops:
  8.1 3.1 copy.85
  14.9 2.3 fusion.29
  17.2 6.1 %collective-permute-start.2 = (bf16[16,512,128]{2,1,0:T(8,128)(2,1)}, bf16[16,512,128]{2,1,0:T(8,128)(2,1)}, u32[]{:S(2)}, u32[]{:S(2)}) collective-permute-start(bf16[16,512,128]{2,1,0:T(8,128)(2,1)} %get-tuple-element.16), channel_id=1, source_target_pairs={{0,16},{16,32},{32,48},{48,64},{64,80},{80,96},{96,112},{1,17},{17... | collective-permute-start | bytes 6291464 | tf_op jit(solution)/shard_map/ppermute | solution.py:57
  23.4 3.6 collective-permute-start.3
  27.0 4.3 collective-permute-start.4
  34.9 54.2 %collective-permute-done.2 = bf16[16,512,128]{2,1,0:T(8,128)(2,1)} collective-permute-done((bf16[16,512,128]{2,1,0:T(8,128)(2,1)}, bf16[16,512,128]{2,1,0:T(8,128)(2,1)}, u32[]{:S(2)}, u32[]{:S(2)}) %collective-permute-start.2) | collective-permute-done | bytes 2097184 | tf_op jit(solution)/shard_map/ppermute | solution.py:57
  89.1 104.8 %collective-permute-done.3 = bf16[16,512,128]{2,1,0:T(8,128)(2,1)} collective-permute-done((bf16[16,512,128]{2,1,0:T(8,128)(2,1)}, bf16[16,512,128]{2,1,0:T(8,128)(2,1)}, u32[]{:S(2)}, u32[]{:S(2)}) %collective-permute-start.3) | collective-permute-done | bytes 2097184 | tf_op jit(solution)/shard_map/ppermute | solution.py:57
  194.0 5.9 %fusion = f32[16,512,128,1]{2,1,0,3:T(8,128)S(1)} fusion(bf16[1,16,512,128]{3,2,1,0:T(8,128)(2,1)} %bitcast.12, bf16[1,16,512,128]{3,2,1,0:T(8,128)(2,1)} %bitcast.10, bf16[1,16,512,128]{3,2,1,0:T(8,128)(2,1)} %bitcast.8, bf16[1,16,512,128]{3,2,1,0:T(8,128)(2,1)} %get-tuple-element.15, bf16[4,128,128]{1,2,0:T(8,128)(2,1)S(1)} %gather_fusion.1, ...), kind=kOutput, calls=%fused_computation.2 | convolution fusion | flops 1086390272 | bytes 12713988 | tf_op jit(solution)/shard_map/tes,eijs->itj/dot_general | solution.py:65
  199.9 4.4 fusion.14
  205.5 9.1 %collective-permute-start.5 = (bf16[16,512,128]{2,1,0:T(8,128)(2,1)}, bf16[16,512,128]{2,1,0:T(8,128)(2,1)}, u32[]{:S(2)}, u32[]{:S(2)}) collective-permute-start(bf16[16,512,128]{2,1,0:T(8,128)(2,1)} %get-tuple-element.16), channel_id=1, source_target_pairs={{0,64},{16,80},{1,65},{17,81},{2,66},{18,82},{3,67},{19,83},{4,68}... | collective-permute-start | bytes 6291464 | tf_op jit(solution)/shard_map/ppermute | solution.py:57
  214.6 2.6 collective-permute-start.6
  217.3 3.8 collective-permute-start
  228.5 121.3 %collective-permute-done.10 = f32[16,128,512]{1,2,0:T(8,128)} collective-permute-done((f32[16,128,512]{1,2,0:T(8,128)}, f32[16,128,512]{1,2,0:T(8,128)}, u32[]{:S(2)}, u32[]{:S(2)}) %collective-permute-start.10) | collective-permute-done | bytes 4194336 | tf_op jit(solution)/shard_map/ppermute | solution.py:73
  352.0 3.4 bitcast_dynamic-update-slice_fusion.4
  355.4 3.3 bitcast_dynamic-update-slice_fusion.3
  358.7 3.3 bitcast_dynamic-update-slice_fusion.2
  362.1 3.4 bitcast_dynamic-update-slice_fusion.1
  365.4 3.4 bitcast_dynamic-update-slice_fusion
  372.2 8.3 %fusion.32 = f32[16,512,128,1]{2,1,3,0:T(8,128)S(1)} fusion(bf16[8,16,512,128]{3,2,0,1:T(8,128)(2,1)} %bitcast_dynamic-update-slice_fusion.7, bf16[8,128,128]{2,1,0:T(8,128)(2,1)S(1)} %gather_fusion, pred[8]{0:T(512)(128)(4,1)S(1)} %compare_and_fusion.2), kind=kOutput, calls=%fused_computation.63 | convolution fusion | flops 2147614720 | bytes 21233672 | tf_op jit(solution)/shard_map/tes,eijs->itj/dot_general | solution.py:61
  380.5 60.5 %collective-permute-done.11 = f32[16,128,512]{1,2,0:T(8,128)S(1)} collective-permute-done((f32[16,128,512]{1,2,0:T(8,128)}, f32[16,128,512]{1,2,0:T(8,128)S(1)}, u32[]{:S(2)}, u32[]{:S(2)}) %collective-permute-start.11) | collective-permute-done | bytes 4194336 | tf_op jit(solution)/shard_map/ppermute | solution.py:74
  442.6 4.2 collective-permute-start.12
  450.6 2.5 fusion.52
  453.2 6.5 %collective-permute-done.13 = f32[2,128,512]{1,2,0:T(8,128)} collective-permute-done((f32[2,128,512]{1,2,0:T(8,128)}, f32[2,128,512]{1,2,0:T(8,128)}, u32[]{:S(2)}, u32[]{:S(2)}) %collective-permute-start.13) | collective-permute-done | bytes 524320 | tf_op jit(solution)/shard_map/ppermute | solution.py:15
  459.8 2.7 fusion.15
  466.7 3.0 copy.73
  469.8 4.0 fusion.20
  476.2 13.4 %convolution_bitcast_fusion = f32[16,128,512]{2,1,0:T(8,128)} fusion(bf16[128,8,128,1]{0,2,3,1:T(8,128)(2,1)S(1)} %bitcast.102, bf16[8,16,512,128]{3,2,1,0:T(8,128)(2,1)} %bitcast.98), kind=kOutput, calls=%fused_computation.31 | convolution fusion | flops 2147483648 | bytes 21233664 | tf_op jit(solution)/shard_map/tes,eijs->itj/dot_general | solution.py:90
  489.6 2.9 pad_maximum_fusion
  493.5 4.3 fusion.10
  498.5 3.7 fusion.13
  502.2 2.4 maximum_bitcast_fusion
  504.6 8.3 %copy.75 = f32[128,32,512]{2,1,0:T(8,128)} copy(f32[128,32,512]{2,0,1:T(8,128)S(1)} %maximum_bitcast_fusion) | data formatting | bytes 16777216 | tf_op jit(solution)/shard_map/transpose | solution.py:94
  (76 shorter events, 36.8 us)
Async XLA Ops:
  6.5 1.6 slice-start
  6.5 469.7 %all-gather.3.cloned.1.call-start = ((), (), s32[]{:S(2)}) async-start(), calls=%async_computation | async-start | bytes 18874368 | tf_op jit(solution)/shard_map/all_gather | solution.py:47
  14.9 18.5 %copy-start.3 = (bf16[128,1024]{1,0:T(8,128)(2,1)S(1)}, bf16[128,1024]{1,0:T(8,128)(2,1)}, u32[]{:S(2)}) copy-start(bf16[128,1024]{1,0:T(8,128)(2,1)} %param.4) | copy-start | bytes 786436
  17.2 71.9 %collective-permute-start.2 = (bf16[16,512,128]{2,1,0:T(8,128)(2,1)}, bf16[16,512,128]{2,1,0:T(8,128)(2,1)}, u32[]{:S(2)}, u32[]{:S(2)}) collective-permute-start(bf16[16,512,128]{2,1,0:T(8,128)(2,1)} %get-tuple-element.16), channel_id=1, source_target_pairs={{0,16},{16,32},{32,48},{48,64},{64,80},{80,96},{96,112},{1,17},{17... | collective-permute-start | bytes 6291464 | tf_op jit(solution)/shard_map/ppermute | solution.py:57
  23.4 170.6 %collective-permute-start.3 = (bf16[16,512,128]{2,1,0:T(8,128)(2,1)}, bf16[16,512,128]{2,1,0:T(8,128)(2,1)}, u32[]{:S(2)}, u32[]{:S(2)}) collective-permute-start(bf16[16,512,128]{2,1,0:T(8,128)(2,1)} %get-tuple-element.16), channel_id=1, source_target_pairs={{0,32},{16,48},{32,64},{48,80},{64,96},{80,112},{1,33},{17,49},{33... | collective-permute-start | bytes 6291464 | tf_op jit(solution)/shard_map/ppermute | solution.py:57
  27.0 167.0 %collective-permute-start.4 = (bf16[16,512,128]{2,1,0:T(8,128)(2,1)}, bf16[16,512,128]{2,1,0:T(8,128)(2,1)}, u32[]{:S(2)}, u32[]{:S(2)}) collective-permute-start(bf16[16,512,128]{2,1,0:T(8,128)(2,1)} %get-tuple-element.16), channel_id=1, source_target_pairs={{0,48},{16,64},{32,80},{64,112},{1,49},{17,65},{33,81},{65,113},{2... | collective-permute-start | bytes 6291464 | tf_op jit(solution)/shard_map/ppermute | solution.py:57
  31.3 168.6 %collective-permute-start.9 = (bf16[16,512,128]{2,1,0:T(8,128)(2,1)}, bf16[16,512,128]{2,1,0:T(8,128)(2,1)}, u32[]{:S(2)}, u32[]{:S(2)}) collective-permute-start(bf16[16,512,128]{2,1,0:T(8,128)(2,1)} %get-tuple-element.16), channel_id=1, source_target_pairs={{48,32},{49,33},{50,34},{51,35},{52,36},{53,37},{54,38},{55,39},{5... | collective-permute-start | bytes 6291464 | tf_op jit(solution)/shard_map/ppermute | solution.py:62
  33.6 0.7 collective-permute-start.8
  199.9 17.4 %copy-start.4 = (f32[32,512]{1,0:T(8,128)S(1)}, f32[32,512]{1,0:T(8,128)}, u32[]{:S(2)}) copy-start(f32[32,512]{1,0:T(8,128)} %param.5) | copy-start | bytes 196612
  204.3 145.6 %collective-permute-start.10 = (f32[16,128,512]{1,2,0:T(8,128)}, f32[16,128,512]{1,2,0:T(8,128)}, u32[]{:S(2)}, u32[]{:S(2)}) collective-permute-start(f32[16,128,512]{1,2,0:T(8,128)} %fusion.14), channel_id=1, source_target_pairs={{32,0},{48,16},{33,1},{49,17},{34,2},{50,18},{35,3},{51,19},{36,4}... | collective-permute-start | bytes 12582920 | tf_op jit(solution)/shard_map/ppermute | solution.py:73
  205.5 156.5 %collective-permute-start.5 = (bf16[16,512,128]{2,1,0:T(8,128)(2,1)}, bf16[16,512,128]{2,1,0:T(8,128)(2,1)}, u32[]{:S(2)}, u32[]{:S(2)}) collective-permute-start(bf16[16,512,128]{2,1,0:T(8,128)(2,1)} %get-tuple-element.16), channel_id=1, source_target_pairs={{0,64},{16,80},{1,65},{17,81},{2,66},{18,82},{3,67},{19,83},{4,68}... | collective-permute-start | bytes 6291464 | tf_op jit(solution)/shard_map/ppermute | solution.py:57
  214.6 150.8 %collective-permute-start.6 = (bf16[16,512,128]{2,1,0:T(8,128)(2,1)}, bf16[16,512,128]{2,1,0:T(8,128)(2,1)}, u32[]{:S(2)}, u32[]{:S(2)}) collective-permute-start(bf16[16,512,128]{2,1,0:T(8,128)(2,1)} %get-tuple-element.16), channel_id=1, source_target_pairs={{0,80},{1,81},{2,82},{3,83},{4,84},{5,85},{6,86},{7,87},{8,88},{9,... | collective-permute-start | bytes 6291464 | tf_op jit(solution)/shard_map/ppermute | solution.py:57
  217.3 9.3 %collective-permute-start = (f32[1,512]{1,0:T(1,128)S(1)}, f32[1,512]{1,0:T(1,128)S(1)}, u32[]{:S(2)}, u32[]{:S(2)}) collective-permute-start(f32[1,512]{1,0:T(1,128)S(1)} %get-tuple-element.21), channel_id=1, source_target_pairs={{0,1},{1,2},{2,3},{3,4},{4,5},{5,6},{6,7},{7,8},{8,9},{9,10},{10,1... | collective-permute-start | bytes 6152 | tf_op jit(solution)/shard_map/ppermute | solution.py:14
  221.0 7.4 %collective-permute-start.1 = (f32[1,512]{1,0:T(1,128)S(1)}, f32[1,512]{1,0:T(1,128)S(1)}, u32[]{:S(2)}, u32[]{:S(2)}) collective-permute-start(f32[1,512]{1,0:T(1,128)S(1)} %get-tuple-element.22), channel_id=1, source_target_pairs={{1,0},{2,1},{3,2},{4,3},{5,4},{6,5},{7,6},{8,7},{9,8},{10,9},{11,1... | collective-permute-start | bytes 6152 | tf_op jit(solution)/shard_map/ppermute | solution.py:15
  226.5 142.3 %collective-permute-start.7 = (bf16[16,512,128]{2,1,0:T(8,128)(2,1)}, bf16[16,512,128]{2,1,0:T(8,128)(2,1)S(1)}, u32[]{:S(2)}, u32[]{:S(2)}) collective-permute-start(bf16[16,512,128]{2,1,0:T(8,128)(2,1)} %get-tuple-element.16), channel_id=1, source_target_pairs={} | collective-permute-start | bytes 6291464 | tf_op jit(solution)/shard_map/ppermute | solution.py:57
  349.9 91.1 %collective-permute-start.11 = (f32[16,128,512]{1,2,0:T(8,128)}, f32[16,128,512]{1,2,0:T(8,128)S(1)}, u32[]{:S(2)}, u32[]{:S(2)}) collective-permute-start(f32[16,128,512]{1,2,0:T(8,128)} %collective-permute-done.10), channel_id=1, source_target_pairs={{0,96},{16,112},{1,97},{17,113},{2,98},{18,114},{3,99},{19,115},{4... | collective-permute-start | bytes 12582920 | tf_op jit(solution)/shard_map/ppermute | solution.py:74
  441.5 7.4 %copy-start = (f32[16,128,512]{1,2,0:T(8,128)}, f32[16,128,512]{1,2,0:T(8,128)S(1)}, u32[]{:S(2)}) copy-start(f32[16,128,512]{1,2,0:T(8,128)S(1)} %bitcast_add_fusion) | copy-start | bytes 12582916
  442.6 10.6 %collective-permute-start.12 = (f32[2,128,512]{1,2,0:T(8,128)}, f32[2,128,512]{1,2,0:T(8,128)}, u32[]{:S(2)}, u32[]{:S(2)}) collective-permute-start(f32[2,128,512]{1,2,0:T(8,128)} %get-tuple-element.7), channel_id=1, source_target_pairs={{0,1},{1,2},{2,3},{3,4},{4,5},{5,6},{6,7},{7,8},{8,9},{9,10},{10,1... | collective-permute-start | bytes 1572872 | tf_op jit(solution)/shard_map/ppermute | solution.py:14
  446.8 12.9 %collective-permute-start.13 = (f32[2,128,512]{1,2,0:T(8,128)}, f32[2,128,512]{1,2,0:T(8,128)}, u32[]{:S(2)}, u32[]{:S(2)}) collective-permute-start(f32[2,128,512]{1,2,0:T(8,128)} %get-tuple-element.8), channel_id=1, source_target_pairs={{1,0},{2,1},{3,2},{4,3},{5,4},{6,5},{7,6},{8,7},{9,8},{10,9},{11,1... | collective-permute-start | bytes 1572872 | tf_op jit(solution)/shard_map/ppermute | solution.py:15
  459.8 2.7 copy-start.7
  464.5 0.7 copy-start.5
  466.7 3.1 copy-start.6
  476.2 13.4 %copy-start.2 = (f32[4,128,512]{2,1,0:T(8,128)S(1)}, f32[4,128,512]{2,1,0:T(8,128)}, u32[]{:S(2)}) copy-start(f32[4,128,512]{2,1,0:T(8,128)} %copy.72) | copy-start | bytes 3145732
  498.5 3.7 copy-start.1
Sparse Core Ops, SparseCore 0:
  11.3 320.8 all-gather.2

commit v11 on v6

--- a/solution.py
+++ b/solution.py
@@ -1,6 +1,8 @@
 import jax
 import jax.numpy as jnp
 from jax import lax
+from jax.experimental import pallas as pl
+from jax.experimental.pallas import tpu as pltpu
 from jax.sharding import PartitionSpec as P
 
 EDGE = 8
@@ -34,6 +36,92 @@
     return gain_out * once[1:-1] - (once[:-2] + once[2:] + side_sum(once[1:-1]))
 
 
+def _side(v):
+    width = v.shape[-1]
+    wrapped = pltpu.roll(v, 1, 1) + pltpu.roll(v, width - 1, 1)
+    lanes = lax.broadcasted_iota(jnp.int32, v.shape, 1)
+    first = jnp.broadcast_to(v[:, 0:1], v.shape)
+    last = jnp.broadcast_to(v[:, width - 1:width], v.shape)
+    wrapped = jnp.where(lanes == 0, wrapped - last, wrapped)
+    return jnp.where(lanes == width - 1, wrapped - first, wrapped)
+
+
+def _middle_kernel(lower_ref, g_ref, top_ref, bot_ref, gain_ref, out_ref, ext_ref, once_ref):
+    i = pl.program_id(0)
+    steps = pl.num_programs(0)
+    halo = top_ref.shape[0]
+    acc = jnp.zeros(out_ref.shape[1:], jnp.float32)
+    for e in range(lower_ref.shape[0]):
+        acc = acc + lax.dot_general(
+            lower_ref[e], g_ref[e], (((1,), (1,)), ((), ())), preferred_element_type=jnp.float32
+        )
+    ext_ref[halo + i] = acc
+
+    @pl.when(i == steps - 1)
+    def _():
+        rows = ext_ref.shape[0]
+        for r in range(halo):
+            ext_ref[r] = top_ref[r]
+            ext_ref[rows - halo + r] = bot_ref[r]
+
+        def once_row(r, carry):
+            c = ext_ref[r + 1]
+            once_ref[r] = gain_ref[r] * c - (ext_ref[r] + ext_ref[r + 2] + _side(c))
+            return carry
+
+        lax.fori_loop(0, rows - 2, once_row, 0)
+
+        def out_row(r, carry):
+            c = once_ref[r + 1]
+            out_ref[r] = gain_ref[r + 1] * c - (once_ref[r] + once_ref[r + 2] + _side(c))
+            return carry
+
+        lax.fori_loop(0, rows - 4, out_row, 0)
+
+
+def _pin_kernel(x_ref, o_ref):
+    o_ref[...] = x_ref[...]
+
+
+def pinned(x):
+    return pl.pallas_call(_pin_kernel, out_shape=jax.ShapeDtypeStruct(x.shape, x.dtype))(x)
+
+
+def middle_stencil(lower_e, gathered, top, bottom, gain_rows):
+    count, epochs, _ = lower_e.shape
+    _, rows, width, _ = gathered.shape
+    halo = top.shape[0]
+    ext_rows = rows + 2 * halo
+    out_rows = ext_rows - 4
+    flops = 2 * epochs * count * epochs * rows * width + 20 * ext_rows * epochs * width
+    cost = pl.CostEstimate(
+        flops=flops,
+        transcendentals=0,
+        bytes_accessed=gathered.size * 2 + (out_rows + 2 * halo) * epochs * width * 4,
+    )
+    return pl.pallas_call(
+        _middle_kernel,
+        out_shape=jax.ShapeDtypeStruct((out_rows, epochs, width), jnp.float32),
+        grid=(rows,),
+        in_specs=[
+            pl.BlockSpec((count, epochs, epochs), lambda i: (0, 0, 0)),
+            pl.BlockSpec((count, None, width, epochs), lambda i: (0, i, 0, 0)),
+            pl.BlockSpec((halo, epochs, width), lambda i: (0, 0, 0)),
+            pl.BlockSpec((halo, epochs, width), lambda i: (0, 0, 0)),
+            pl.BlockSpec((ext_rows - 2, 1, width), lambda i: (0, 0, 0)),
+        ],
+        out_specs=pl.BlockSpec((out_rows, epochs, width), lambda i: (0, 0, 0)),
+        scratch_shapes=[
+            pltpu.VMEM((ext_rows, epochs, width), jnp.float32),
+            pltpu.VMEM((ext_rows - 2, epochs, width), jnp.float32),
+        ],
+        compiler_params=pltpu.CompilerParams(
+            dimension_semantics=("arbitrary",), vmem_limit_bytes=60 * 1024 * 1024
+        ),
+        cost_estimate=cost,
+    )(lower_e, gathered, top, bottom, gain_rows)
+
+
 def body(field, factor, kappa):
     epochs, slab, width = field.shape
     count = lax.axis_size("epoch")
@@ -43,7 +131,7 @@
     global_cols = lax.broadcasted_iota(jnp.int32, (epochs, order), 1)
     lower = jnp.where(global_cols <= global_rows, factor, jnp.zeros_like(factor))
     lower = lower.reshape(epochs, count, epochs)
-    middle = jnp.transpose(field[:, EDGE:slab - EDGE], (1, 2, 0))
+    middle = pinned(jnp.transpose(field[:, EDGE:slab - EDGE], (1, 2, 0)))
     gathered = lax.all_gather(middle, "epoch", axis=0)
     edges = jnp.transpose(
         jnp.concatenate([field[:, :EDGE], field[:, slab - EDGE:]], axis=1), (1, 2, 0)
@@ -71,9 +159,13 @@
         jnp.concatenate([bottom, below], axis=0),
         gain[slab - EDGE + 2:slab + 2], gain[slab - EDGE + 3:slab + 1], last_outside=pos == last,
     )
-    timed_middle = jnp.einsum("tes,eijs->itj", lower, gathered, preferred_element_type=jnp.float32)
-    ext = jnp.concatenate([top[EDGE - 2 * HALO:], timed_middle, bottom[:2 * HALO]], axis=0)
-    out_middle = double_stencil(ext, gain[EDGE - 2:slab - EDGE + 4], gain[EDGE - 1:slab - EDGE + 3])
+    out_middle = middle_stencil(
+        jnp.transpose(lower, (1, 0, 2)),
+        gathered,
+        top[EDGE - 2 * HALO:],
+        bottom[:2 * HALO],
+        gain[EDGE - 2:slab - EDGE + 4],
+    )
     product = jnp.concatenate([out_top, out_middle, out_bottom], axis=0)
     return jnp.transpose(product, (1, 0, 2))
 

time: 404 us -> 410 us (1.015)
  Pallas kernels: 0 us -> 31.5 us
  other arithmetic: 28.7 us -> 11.2 us
  matrix products: 23.8 us -> 15.5 us
  waiting for transfers between devices: 262 us -> 270 us
  local copies, waits for them, and re-layouts: 49 us -> 42.4 us
    pallas_call x0 -> x2, Pallas kernels: none -> 31.5 us  [the longest x1 28.5 us: middle_stencil(): pl.pallas_call(_middle_kernel, out_shape=jax.ShapeDtypeStruct((out_rows,...]
    dot_general x1 -> x0, matrix products: 13.4 us -> none  [body(): jnp.einsum('tes,eijs->itj', lower, gathered, preferred_element_type=jnp.f...]
    all_gather x1, waiting for transfers between devices: 104 us -> 111 us  [body(): gathered = lax.all_gather(middle, 'epoch', axis=0)]
    dot_general x1, matrix products: 10.4 us -> 15.5 us  [body(): jnp.einsum('tes,eijs->itj', weights, stacked, preferred_element_type=jnp....]
    sub x2 -> x0, local copies, waits for them, and re-layouts: 4.71 us -> none  [double_stencil(): return gain_out * once[1:-1] - (once[:-2] + once[2:] + side_sum(once[1:-1]))]
    sub x1 -> x0, other arithmetic: 4.29 us -> none  [double_stencil(): once = gain_once * ext[1:-1] - (ext[:-2] + ext[2:] + side_sum(ext[1:-1]))]
    sub x3 -> x2, other arithmetic: 5.9 us -> 1.77 us  [double_stencil(): return gain_out * once[1:-1] - (once[:-2] + once[2:] + side_sum(once[1:-1]))]
    unnamed x26 -> x19, local copies, waits for them, and re-layouts: 22.4 us -> 21.9 us
  transfers between devices with their start and end apart: 12 -> 12, of which waited for: 5 -> 6; matrix products, arithmetic and copies ran while one was open for 15% -> 13% of each run, Pallas kernels for 0% -> 0%
where the time goes in v11:
time: 410 us
  waiting for transfers between devices  270 us (66%)
  local copies, waits for them, and re-layouts  42.4 us (10%)
  Pallas kernels  31.5 us (8%)
  starting transfers between devices  25.5 us (6%)
  matrix products  15.5 us (4%)
  between operations  13.7 us (3%)
  other arithmetic  11.2 us (3%)
    ppermute x7, waiting for transfers between devices, body(): slots.append(lax.ppermute(edges, 'epoch', pairs))  154 us
    all_gather x1, waiting for transfers between devices, body(): gathered = lax.all_gather(middle, 'epoch', axis=0)  111 us
    pallas_call x1, Pallas kernels, middle_stencil(): pl.pallas_call(_middle_kernel, out_shape=jax.ShapeDtypeStruct((out_rows,...  28.5 us
    unnamed x19, local copies, waits for them, and re-layouts  21.9 us
    ppermute x7, starting transfers between devices, body(): slots.append(lax.ppermute(edges, 'epoch', pairs))  16.1 us
    dot_general x1, matrix products, body(): jnp.einsum('tes,eijs->itj', weights, stacked, preferred_element_type=jnp....  15.5 us
    transpose x1, local copies, waits for them, and re-layouts, body(): return jnp.transpose(product, (1, 0, 2))  8.25 us
  transfers between devices with their start and end apart: 12, of which 6 were waited for; matrix products, arithmetic and copies ran while one was open for 13% of the time, Pallas kernels for 0%

profile of v11, /device:TPU:62, one launch (start us, length us, event | category | flops | bytes accessed | tf_op | source)
XLA Modules:
  0.0 409.5 jit_solution(10151642718100297789)
XLA Ops:
  6.5 1.6 slice-done
  8.1 3.0 copy.56
  11.1 3.0 shard_map.37
  14.2 1.7 fusion.29
  17.9 1.5 fusion.18
  19.4 4.5 %collective-permute-start.2 = (bf16[16,512,128]{2,1,0:T(8,128)(2,1)}, bf16[16,512,128]{2,1,0:T(8,128)(2,1)}, u32[]{:S(2)}, u32[]{:S(2)}) collective-permute-start(bf16[16,512,128]{2,1,0:T(8,128)(2,1)} %fusion.18), channel_id=1, source_target_pairs={{0,16},{16,32},{32,48},{48,64},{64,80},{80,96},{96,112},{1,17},{17... | collective-permute-start | bytes 6291464 | tf_op jit(solution)/shard_map/ppermute | solution.py:142
  23.9 3.5 collective-permute-start.3
  27.4 3.0 collective-permute-start.4
  30.5 2.7 collective-permute-start.5
  33.2 1.9 collective-permute-start
  35.3 1.6 bitcast_dynamic-update-slice_fusion.6
  38.0 2.7 collective-permute-start.1
  43.8 50.3 %collective-permute-done.2 = bf16[16,512,128]{2,1,0:T(8,128)(2,1)} collective-permute-done((bf16[16,512,128]{2,1,0:T(8,128)(2,1)}, bf16[16,512,128]{2,1,0:T(8,128)(2,1)}, u32[]{:S(2)}, u32[]{:S(2)}) %collective-permute-start.2) | collective-permute-done | bytes 2097184 | tf_op jit(solution)/shard_map/ppermute | solution.py:142
  94.9 103.3 %collective-permute-done.3 = bf16[16,512,128]{2,1,0:T(8,128)(2,1)} collective-permute-done((bf16[16,512,128]{2,1,0:T(8,128)(2,1)}, bf16[16,512,128]{2,1,0:T(8,128)(2,1)}, u32[]{:S(2)}, u32[]{:S(2)}) %collective-permute-start.3) | collective-permute-done | bytes 2097184 | tf_op jit(solution)/shard_map/ppermute | solution.py:142
  199.1 3.3 bitcast_dynamic-update-slice_fusion.5
  202.4 3.3 bitcast_dynamic-update-slice_fusion.4
  205.7 3.4 bitcast_dynamic-update-slice_fusion.3
  209.1 3.3 bitcast_dynamic-update-slice_fusion.2
  212.4 1.7 bitcast_dynamic-update-slice_fusion.1
  214.1 1.7 bitcast_dynamic-update-slice_fusion
  215.8 1.7 bitcast_dynamic-update-slice_fusion.7
  217.4 15.5 %convolution_bitcast_fusion = f32[16,128,512]{2,1,0:T(8,128)} fusion(bf16[8,16,512,128]{3,2,0,1:T(8,128)(2,1)} %bitcast_dynamic-update-slice_fusion.7, bf16[8,128,128]{1,2,0:T(8,128)(2,1)S(1)} %gather_fusion, pred[8]{0:T(512)(128)(4,1)S(1)} %compare_and_fusion.1), kind=kOutput, calls=%fused_computation.10 | convolution fusion | flops 2147614720 | bytes 21233672 | tf_op jit(solution)/shard_map/tes,eijs->itj/dot_general | solution.py:146
  232.9 1.3 fusion.27
  234.2 1.9 collective-permute-start.10
  236.2 2.9 collective-permute-start.9
  239.1 3.0 fusion.28
  242.9 4.1 %collective-permute-done.9 = f32[2,128,512]{2,1,0:T(8,128)S(1)} collective-permute-done((f32[2,128,512]{2,1,0:T(8,128)S(1)}, f32[2,128,512]{2,1,0:T(8,128)S(1)}, u32[]{:S(2)}, u32[]{:S(2)}) %collective-permute-start.9) | collective-permute-done | bytes 524320 | tf_op jit(solution)/shard_map/ppermute | solution.py:16
  247.5 1.3 fusion.5
  252.2 110.7 %all-gather.3.cloned.1.call-done = bf16[128,512,128]{2,1,0:T(8,128)(2,1)} async-done(((bf16[16,512,128]{2,1,0:T(8,128)(2,1)}), bf16[128,512,128]{2,1,0:T(8,128)(2,1)}) %all-gather.3.cloned.1.call-update) | async-done | bytes 16777232 | tf_op jit(solution)/shard_map/all_gather | solution.py:135
  362.9 28.5 %shard_map.38 = f32[20,128,512]{2,1,0:T(8,128)} custom-call(bf16[8,128,128]{2,1,0:T(8,128)(2,1)} %bitcast.67, bf16[8,16,512,128]{3,2,1,0:T(8,128)(2,1)} %bitcast.63, f32[4,128,512]{2,1,0:T(8,128)} %get-tuple-element.10.top_ref, f32[4,128,512]{2,1,0:T(8,128)} %get-tuple-element.9.bot_ref, f32[22,1,512]{2,1,0:T(1,128)} %slice.157.gain_ref), custom_call_target="tpu_custom_call" | custom-call | flops 2178940928 | bytes 24117248 | tf_op jit(solution)/shard_map/pallas_call | solution.py:102
  391.4 3.0 maximum_bitcast_fusion
  394.4 8.3 %copy.45 = f32[128,32,512]{2,1,0:T(8,128)} copy(f32[128,32,512]{2,0,1:T(8,128)S(1)} %maximum_bitcast_fusion) | data formatting | bytes 16777216 | tf_op jit(solution)/shard_map/transpose | solution.py:170
  (48 shorter events, 12.5 us)
Async XLA Ops:
  6.5 1.6 slice-start
  6.5 356.3 %all-gather.3.cloned.1.call-start = ((), (), s32[]{:S(2)}) async-start(), calls=%async_computation | async-start | bytes 18874368 | tf_op jit(solution)/shard_map/all_gather | solution.py:135
  17.9 15.3 %copy-start.2 = (f32[32,512]{1,0:T(8,128)S(1)}, f32[32,512]{1,0:T(8,128)}, u32[]{:S(2)}) copy-start(f32[32,512]{1,0:T(8,128)} %param.5) | copy-start | bytes 196612
  17.9 17.2 %copy-start.1 = (bf16[128,1024]{1,0:T(8,128)(2,1)S(1)}, bf16[128,1024]{1,0:T(8,128)(2,1)}, u32[]{:S(2)}) copy-start(bf16[128,1024]{1,0:T(8,128)(2,1)} %param.4) | copy-start | bytes 786436
  19.4 74.7 %collective-permute-start.2 = (bf16[16,512,128]{2,1,0:T(8,128)(2,1)}, bf16[16,512,128]{2,1,0:T(8,128)(2,1)}, u32[]{:S(2)}, u32[]{:S(2)}) collective-permute-start(bf16[16,512,128]{2,1,0:T(8,128)(2,1)} %fusion.18), channel_id=1, source_target_pairs={{0,16},{16,32},{32,48},{48,64},{64,80},{80,96},{96,112},{1,17},{17... | collective-permute-start | bytes 6291464 | tf_op jit(solution)/shard_map/ppermute | solution.py:142
  23.9 174.4 %collective-permute-start.3 = (bf16[16,512,128]{2,1,0:T(8,128)(2,1)}, bf16[16,512,128]{2,1,0:T(8,128)(2,1)}, u32[]{:S(2)}, u32[]{:S(2)}) collective-permute-start(bf16[16,512,128]{2,1,0:T(8,128)(2,1)} %fusion.18), channel_id=1, source_target_pairs={{0,32},{16,48},{32,64},{48,80},{64,96},{80,112},{1,33},{17,49},{33... | collective-permute-start | bytes 6291464 | tf_op jit(solution)/shard_map/ppermute | solution.py:142
  27.4 178.3 %collective-permute-start.4 = (bf16[16,512,128]{2,1,0:T(8,128)(2,1)}, bf16[16,512,128]{2,1,0:T(8,128)(2,1)}, u32[]{:S(2)}, u32[]{:S(2)}) collective-permute-start(bf16[16,512,128]{2,1,0:T(8,128)(2,1)} %fusion.18), channel_id=1, source_target_pairs={{0,48},{16,64},{32,80},{48,96},{64,112},{1,49},{17,65},{33,81},{49... | collective-permute-start | bytes 6291464 | tf_op jit(solution)/shard_map/ppermute | solution.py:142
  30.5 178.6 %collective-permute-start.5 = (bf16[16,512,128]{2,1,0:T(8,128)(2,1)}, bf16[16,512,128]{2,1,0:T(8,128)(2,1)}, u32[]{:S(2)}, u32[]{:S(2)}) collective-permute-start(bf16[16,512,128]{2,1,0:T(8,128)(2,1)} %fusion.18), channel_id=1, source_target_pairs={{0,64},{16,80},{32,96},{48,112},{1,65},{17,81},{33,97},{49,113},{2... | collective-permute-start | bytes 6291464 | tf_op jit(solution)/shard_map/ppermute | solution.py:142
  33.2 4.9 %collective-permute-start = (f32[1,512]{1,0:T(1,128)S(1)}, f32[1,512]{1,0:T(1,128)S(1)}, u32[]{:S(2)}, u32[]{:S(2)}) collective-permute-start(f32[1,512]{1,0:T(1,128)S(1)} %get-tuple-element.17), channel_id=1, source_target_pairs={{0,1},{1,2},{2,3},{3,4},{4,5},{5,6},{6,7},{7,8},{8,9},{9,10},{10,1... | collective-permute-start | bytes 6152 | tf_op jit(solution)/shard_map/ppermute | solution.py:16
  38.0 4.2 %collective-permute-start.1 = (f32[1,512]{1,0:T(1,128)S(1)}, f32[1,512]{1,0:T(1,128)S(1)}, u32[]{:S(2)}, u32[]{:S(2)}) collective-permute-start(f32[1,512]{1,0:T(1,128)S(1)} %get-tuple-element.18), channel_id=1, source_target_pairs={{1,0},{2,1},{3,2},{4,3},{5,4},{6,5},{7,6},{8,7},{9,8},{10,9},{11,1... | collective-permute-start | bytes 6152 | tf_op jit(solution)/shard_map/ppermute | solution.py:17
  42.3 170.2 %collective-permute-start.6 = (bf16[16,512,128]{2,1,0:T(8,128)(2,1)}, bf16[16,512,128]{2,1,0:T(8,128)(2,1)S(1)}, u32[]{:S(2)}, u32[]{:S(2)}) collective-permute-start(bf16[16,512,128]{2,1,0:T(8,128)(2,1)} %fusion.18), channel_id=1, source_target_pairs={{0,80},{16,96},{32,112},{1,81},{17,97},{33,113},{2,82},{18,98},{34... | collective-permute-start | bytes 6291464 | tf_op jit(solution)/shard_map/ppermute | solution.py:142
  94.1 120.0 %collective-permute-start.7 = (bf16[16,512,128]{2,1,0:T(8,128)(2,1)}, bf16[16,512,128]{2,1,0:T(8,128)(2,1)S(1)}, u32[]{:S(2)}, u32[]{:S(2)}) collective-permute-start(bf16[16,512,128]{2,1,0:T(8,128)(2,1)} %fusion.18), channel_id=1, source_target_pairs={{0,96},{16,112},{1,97},{17,113},{2,98},{18,114},{3,99},{19,115},{4... | collective-permute-start | bytes 6291464 | tf_op jit(solution)/shard_map/ppermute | solution.py:142
  198.2 17.5 %collective-permute-start.8 = (bf16[16,512,128]{2,1,0:T(8,128)(2,1)}, bf16[16,512,128]{2,1,0:T(8,128)(2,1)S(1)}, u32[]{:S(2)}, u32[]{:S(2)}) collective-permute-start(bf16[16,512,128]{2,1,0:T(8,128)(2,1)} %fusion.18), channel_id=1, source_target_pairs={{0,112},{1,113},{2,114},{3,115},{4,116},{5,117},{6,118},{7,119},{8... | collective-permute-start | bytes 6291464 | tf_op jit(solution)/shard_map/ppermute | solution.py:142
  234.2 8.6 %collective-permute-start.10 = (f32[2,128,512]{2,1,0:T(8,128)S(1)}, f32[2,128,512]{2,1,0:T(8,128)S(1)}, u32[]{:S(2)}, u32[]{:S(2)}) collective-permute-start(f32[2,128,512]{2,1,0:T(8,128)S(1)} %get-tuple-element.8), channel_id=1, source_target_pairs={{1,0},{2,1},{3,2},{4,3},{5,4},{6,5},{7,6},{8,7},{9,8},{10,9},{11,1... | collective-permute-start | bytes 1572872 | tf_op jit(solution)/shard_map/ppermute | solution.py:17
  236.2 5.9 %copy-start = (f32[16,128,512]{2,1,0:T(8,128)S(1)}, f32[16,128,512]{2,1,0:T(8,128)}, u32[]{:S(2)}) copy-start(f32[16,128,512]{2,1,0:T(8,128)} %convolution_bitcast_fusion) | copy-start | bytes 12582916
  236.2 10.8 %collective-permute-start.9 = (f32[2,128,512]{2,1,0:T(8,128)S(1)}, f32[2,128,512]{2,1,0:T(8,128)S(1)}, u32[]{:S(2)}, u32[]{:S(2)}) collective-permute-start(f32[2,128,512]{2,1,0:T(8,128)S(1)} %get-tuple-element.7), channel_id=1, source_target_pairs={{0,1},{1,2},{2,3},{3,4},{4,5},{5,6},{6,7},{7,8},{8,9},{9,10},{10,1... | collective-permute-start | bytes 1572872 | tf_op jit(solution)/shard_map/ppermute | solution.py:16
Sparse Core Ops, SparseCore 0:
  14.3 348.5 all-gather.2

commit v12 on v6

--- a/solution.py
+++ b/solution.py
@@ -1,6 +1,8 @@
 import jax
 import jax.numpy as jnp
 from jax import lax
+from jax.experimental import pallas as pl
+from jax.experimental.pallas import tpu as pltpu
 from jax.sharding import PartitionSpec as P
 
 EDGE = 8
@@ -34,6 +36,44 @@
     return gain_out * once[1:-1] - (once[:-2] + once[2:] + side_sum(once[1:-1]))
 
 
+def _pin_kernel(x_ref, o_ref):
+    o_ref[...] = x_ref[...]
+
+
+def pinned(x):
+    return pl.pallas_call(_pin_kernel, out_shape=jax.ShapeDtypeStruct(x.shape, x.dtype))(x)
+
+
+def _dot_kernel(lower_ref, g_ref, out_ref):
+    acc = jnp.zeros(out_ref.shape, jnp.float32)
+    for e in range(lower_ref.shape[0]):
+        acc = acc + lax.dot_general(
+            lower_ref[e], g_ref[e], (((1,), (1,)), ((), ())), preferred_element_type=jnp.float32
+        )
+    out_ref[...] = acc
+
+
+def middle_dot(lower_e, gathered):
+    count, epochs, _ = lower_e.shape
+    _, rows, width, _ = gathered.shape
+    cost = pl.CostEstimate(
+        flops=2 * epochs * count * epochs * rows * width,
+        transcendentals=0,
+        bytes_accessed=gathered.size * 2 + rows * epochs * width * 4,
+    )
+    return pl.pallas_call(
+        _dot_kernel,
+        out_shape=jax.ShapeDtypeStruct((rows, epochs, width), jnp.float32),
+        grid=(rows,),
+        in_specs=[
+            pl.BlockSpec((count, epochs, epochs), lambda i: (0, 0, 0)),
+            pl.BlockSpec((count, None, width, epochs), lambda i: (0, i, 0, 0)),
+        ],
+        out_specs=pl.BlockSpec((None, epochs, width), lambda i: (i, 0, 0)),
+        cost_estimate=cost,
+    )(lower_e, gathered)
+
+
 def body(field, factor, kappa):
     epochs, slab, width = field.shape
     count = lax.axis_size("epoch")
@@ -43,7 +83,7 @@
     global_cols = lax.broadcasted_iota(jnp.int32, (epochs, order), 1)
     lower = jnp.where(global_cols <= global_rows, factor, jnp.zeros_like(factor))
     lower = lower.reshape(epochs, count, epochs)
-    middle = jnp.transpose(field[:, EDGE:slab - EDGE], (1, 2, 0))
+    middle = pinned(jnp.transpose(field[:, EDGE:slab - EDGE], (1, 2, 0)))
     gathered = lax.all_gather(middle, "epoch", axis=0)
     edges = jnp.transpose(
         jnp.concatenate([field[:, :EDGE], field[:, slab - EDGE:]], axis=1), (1, 2, 0)
@@ -71,7 +111,7 @@
         jnp.concatenate([bottom, below], axis=0),
         gain[slab - EDGE + 2:slab + 2], gain[slab - EDGE + 3:slab + 1], last_outside=pos == last,
     )
-    timed_middle = jnp.einsum("tes,eijs->itj", lower, gathered, preferred_element_type=jnp.float32)
+    timed_middle = middle_dot(jnp.transpose(lower, (1, 0, 2)), gathered)
     ext = jnp.concatenate([top[EDGE - 2 * HALO:], timed_middle, bottom[:2 * HALO]], axis=0)
     out_middle = double_stencil(ext, gain[EDGE - 2:slab - EDGE + 4], gain[EDGE - 1:slab - EDGE + 3])
     product = jnp.concatenate([out_top, out_middle, out_bottom], axis=0)

time: 404 us -> 411 us (1.017)
  Pallas kernels: 0 us -> 18.9 us
  matrix products: 23.8 us -> 15.5 us
  waiting for transfers between devices: 262 us -> 268 us
  other arithmetic: 28.7 us -> 23.4 us
  local copies, waits for them, and re-layouts: 49 us -> 44.5 us
    pallas_call x0 -> x2, Pallas kernels: none -> 18.9 us  [the longest x1 15.9 us: middle_dot(): pl.pallas_call(_dot_kernel, out_shape=jax.ShapeDtypeStruct((rows, epochs,...]
    dot_general x1 -> x0, matrix products: 13.4 us -> none  [body(): jnp.einsum('tes,eijs->itj', lower, gathered, preferred_element_type=jnp.f...]
    all_gather x1, waiting for transfers between devices: 104 us -> 109 us  [body(): gathered = lax.all_gather(middle, 'epoch', axis=0)]
    dot_general x1, matrix products: 10.4 us -> 15.5 us  [body(): jnp.einsum('tes,eijs->itj', weights, stacked, preferred_element_type=jnp....]
    sub x2 -> x0, local copies, waits for them, and re-layouts: 4.71 us -> none  [double_stencil(): return gain_out * once[1:-1] - (once[:-2] + once[2:] + side_sum(once[1:-1]))]
    unnamed x26 -> x18, local copies, waits for them, and re-layouts: 22.4 us -> 22 us
  transfers between devices with their start and end apart: 12 -> 12, of which waited for: 5 -> 6; matrix products, arithmetic and copies ran while one was open for 15% -> 13% of each run, Pallas kernels for 0% -> 0%
where the time goes in v12:
time: 411 us; the launch traced here: 410 us
  waiting for transfers between devices  268 us (65%)
  local copies, waits for them, and re-layouts  44.5 us (11%)
  starting transfers between devices  25.5 us (6%)
  other arithmetic  23.4 us (6%)
  Pallas kernels  18.9 us (5%)
  matrix products  15.5 us (4%)
  between operations  13.7 us (3%)
    ppermute x7, waiting for transfers between devices, body(): slots.append(lax.ppermute(edges, 'epoch', pairs))  153 us
    all_gather x1, waiting for transfers between devices, body(): gathered = lax.all_gather(middle, 'epoch', axis=0)  109 us
    unnamed x18, local copies, waits for them, and re-layouts  22 us
    ppermute x7, starting transfers between devices, body(): slots.append(lax.ppermute(edges, 'epoch', pairs))  16.1 us
    pallas_call x1, Pallas kernels, middle_dot(): pl.pallas_call(_dot_kernel, out_shape=jax.ShapeDtypeStruct((rows, epochs,...  15.9 us
    dot_general x1, matrix products, body(): jnp.einsum('tes,eijs->itj', weights, stacked, preferred_element_type=jnp....  15.5 us
    transpose x1, local copies, waits for them, and re-layouts, body(): return jnp.transpose(product, (1, 0, 2))  8.25 us
  transfers between devices with their start and end apart: 12, of which 6 were waited for; matrix products, arithmetic and copies ran while one was open for 13% of the time, Pallas kernels for 0%

profile of v12, /device:TPU:62, one launch (start us, length us, event | category | flops | bytes accessed | tf_op | source)
XLA Modules:
  0.0 409.8 jit_solution(14507653446360269063)
XLA Ops:
  8.1 3.0 copy.52
  11.1 3.0 shard_map.37
  14.2 1.7 fusion.35
  19.4 4.5 %collective-permute-start.2 = (bf16[16,512,128]{2,1,0:T(8,128)(2,1)}, bf16[16,512,128]{2,1,0:T(8,128)(2,1)}, u32[]{:S(2)}, u32[]{:S(2)}) collective-permute-start(bf16[16,512,128]{2,1,0:T(8,128)(2,1)} %fusion.24), channel_id=1, source_target_pairs={{0,16},{16,32},{32,48},{48,64},{64,80},{80,96},{96,112},{1,17},{17... | collective-permute-start | bytes 6291464 | tf_op jit(solution)/shard_map/ppermute | solution.py:94
  23.9 3.5 collective-permute-start.3
  27.4 3.0 collective-permute-start.4
  30.5 2.7 collective-permute-start.5
  33.2 1.9 collective-permute-start
  35.4 1.6 bitcast_dynamic-update-slice_fusion.6
  38.0 2.7 collective-permute-start.1
  44.3 49.8 %collective-permute-done.2 = bf16[16,512,128]{2,1,0:T(8,128)(2,1)} collective-permute-done((bf16[16,512,128]{2,1,0:T(8,128)(2,1)}, bf16[16,512,128]{2,1,0:T(8,128)(2,1)}, u32[]{:S(2)}, u32[]{:S(2)}) %collective-permute-start.2) | collective-permute-done | bytes 2097184 | tf_op jit(solution)/shard_map/ppermute | solution.py:94
  94.9 103.3 %collective-permute-done.3 = bf16[16,512,128]{2,1,0:T(8,128)(2,1)} collective-permute-done((bf16[16,512,128]{2,1,0:T(8,128)(2,1)}, bf16[16,512,128]{2,1,0:T(8,128)(2,1)}, u32[]{:S(2)}, u32[]{:S(2)}) %collective-permute-start.3) | collective-permute-done | bytes 2097184 | tf_op jit(solution)/shard_map/ppermute | solution.py:94
  199.1 3.3 bitcast_dynamic-update-slice_fusion.5
  202.4 3.3 bitcast_dynamic-update-slice_fusion.4
  205.7 3.4 bitcast_dynamic-update-slice_fusion.3
  209.1 3.3 bitcast_dynamic-update-slice_fusion.2
  212.4 1.7 bitcast_dynamic-update-slice_fusion.1
  214.1 1.7 bitcast_dynamic-update-slice_fusion
  215.8 1.7 bitcast_dynamic-update-slice_fusion.7
  217.4 15.5 %convolution_bitcast_fusion = f32[16,128,512]{2,1,0:T(8,128)} fusion(bf16[8,16,512,128]{3,2,0,1:T(8,128)(2,1)} %bitcast_dynamic-update-slice_fusion.7, bf16[8,128,128]{1,2,0:T(8,128)(2,1)S(1)} %gather_fusion, pred[8]{0:T(512)(128)(4,1)S(1)} %compare_and_fusion.1), kind=kOutput, calls=%fused_computation.23 | convolution fusion | flops 2147614720 | bytes 21233672 | tf_op jit(solution)/shard_map/tes,eijs->itj/dot_general | solution.py:98
  234.2 1.9 collective-permute-start.10
  236.2 2.9 collective-permute-start.9
  239.1 2.8 fusion.34
  242.9 4.1 collective-permute-done.9
  251.3 2.1 fusion.23
  253.4 109.5 %all-gather.3.cloned.1.call-done = bf16[128,512,128]{2,1,0:T(8,128)(2,1)} async-done(((bf16[16,512,128]{2,1,0:T(8,128)(2,1)}), bf16[128,512,128]{2,1,0:T(8,128)(2,1)}) %all-gather.3.cloned.1.call-update) | async-done | bytes 16777232 | tf_op jit(solution)/shard_map/all_gather | solution.py:87
  362.9 15.9 %shard_map.38 = f32[16,128,512]{2,1,0:T(8,128)} custom-call(bf16[8,128,128]{2,1,0:T(8,128)(2,1)} %bitcast.70, bf16[8,16,512,128]{3,2,1,0:T(8,128)(2,1)} %bitcast.66), custom_call_target="tpu_custom_call" | custom-call | flops 2147483648 | bytes 20971520 | tf_op jit(solution)/shard_map/pallas_call | solution.py:64
  378.8 3.2 pad_maximum_fusion
  383.0 5.1 %fusion.2 = f32[22,128,512]{2,1,0:T(8,128)S(1)} fusion(f32[22,128,512]{2,1,0:T(8,128)S(1)} %slice.205, f32[24,128,512]{2,1,0:T(8,128)S(1)} %pad_maximum_fusion, f32[22,512]{1,0:T(8,128)} %slice_bitcast_fusion), kind=kLoop, calls=%fused_computation.9 | loop fusion | flops 7208960 | bytes 23113728 | tf_op jit(solution)/shard_map/sub | solution.py:27
  388.9 3.6 fusion.5
  392.6 2.2 maximum_bitcast_fusion
  394.7 8.3 %copy.45 = f32[128,32,512]{2,1,0:T(8,128)} copy(f32[128,32,512]{2,0,1:T(8,128)S(1)} %maximum_bitcast_fusion) | data formatting | bytes 16777216 | tf_op jit(solution)/shard_map/transpose | solution.py:118
  (52 shorter events, 19.9 us)
Async XLA Ops:
  6.5 1.6 slice-start
  6.5 356.3 %all-gather.3.cloned.1.call-start = ((), (), s32[]{:S(2)}) async-start(), calls=%async_computation | async-start | bytes 18874368 | tf_op jit(solution)/shard_map/all_gather | solution.py:87
  17.9 15.3 %copy-start.3 = (f32[32,512]{1,0:T(8,128)S(1)}, f32[32,512]{1,0:T(8,128)}, u32[]{:S(2)}) copy-start(f32[32,512]{1,0:T(8,128)} %param.5) | copy-start | bytes 196612
  17.9 17.2 %copy-start.1 = (bf16[128,1024]{1,0:T(8,128)(2,1)S(1)}, bf16[128,1024]{1,0:T(8,128)(2,1)}, u32[]{:S(2)}) copy-start(bf16[128,1024]{1,0:T(8,128)(2,1)} %param.4) | copy-start | bytes 786436
  19.4 74.7 %collective-permute-start.2 = (bf16[16,512,128]{2,1,0:T(8,128)(2,1)}, bf16[16,512,128]{2,1,0:T(8,128)(2,1)}, u32[]{:S(2)}, u32[]{:S(2)}) collective-permute-start(bf16[16,512,128]{2,1,0:T(8,128)(2,1)} %fusion.24), channel_id=1, source_target_pairs={{0,16},{16,32},{32,48},{48,64},{64,80},{80,96},{96,112},{1,17},{17... | collective-permute-start | bytes 6291464 | tf_op jit(solution)/shard_map/ppermute | solution.py:94
  23.9 174.4 %collective-permute-start.3 = (bf16[16,512,128]{2,1,0:T(8,128)(2,1)}, bf16[16,512,128]{2,1,0:T(8,128)(2,1)}, u32[]{:S(2)}, u32[]{:S(2)}) collective-permute-start(bf16[16,512,128]{2,1,0:T(8,128)(2,1)} %fusion.24), channel_id=1, source_target_pairs={{0,32},{16,48},{32,64},{48,80},{64,96},{80,112},{1,33},{17,49},{33... | collective-permute-start | bytes 6291464 | tf_op jit(solution)/shard_map/ppermute | solution.py:94
  27.4 178.3 %collective-permute-start.4 = (bf16[16,512,128]{2,1,0:T(8,128)(2,1)}, bf16[16,512,128]{2,1,0:T(8,128)(2,1)}, u32[]{:S(2)}, u32[]{:S(2)}) collective-permute-start(bf16[16,512,128]{2,1,0:T(8,128)(2,1)} %fusion.24), channel_id=1, source_target_pairs={{0,48},{16,64},{32,80},{48,96},{64,112},{1,49},{17,65},{33,81},{49... | collective-permute-start | bytes 6291464 | tf_op jit(solution)/shard_map/ppermute | solution.py:94
  30.5 178.6 %collective-permute-start.5 = (bf16[16,512,128]{2,1,0:T(8,128)(2,1)}, bf16[16,512,128]{2,1,0:T(8,128)(2,1)}, u32[]{:S(2)}, u32[]{:S(2)}) collective-permute-start(bf16[16,512,128]{2,1,0:T(8,128)(2,1)} %fusion.24), channel_id=1, source_target_pairs={{0,64},{16,80},{32,96},{48,112},{1,65},{17,81},{33,97},{49,113},{2... | collective-permute-start | bytes 6291464 | tf_op jit(solution)/shard_map/ppermute | solution.py:94
  33.2 4.9 %collective-permute-start = (f32[1,512]{1,0:T(1,128)S(1)}, f32[1,512]{1,0:T(1,128)S(1)}, u32[]{:S(2)}, u32[]{:S(2)}) collective-permute-start(f32[1,512]{1,0:T(1,128)S(1)} %get-tuple-element.17), channel_id=1, source_target_pairs={{0,1},{1,2},{2,3},{3,4},{4,5},{5,6},{6,7},{7,8},{8,9},{9,10},{10,1... | collective-permute-start | bytes 6152 | tf_op jit(solution)/shard_map/ppermute | solution.py:16
  38.0 4.2 %collective-permute-start.1 = (f32[1,512]{1,0:T(1,128)S(1)}, f32[1,512]{1,0:T(1,128)S(1)}, u32[]{:S(2)}, u32[]{:S(2)}) collective-permute-start(f32[1,512]{1,0:T(1,128)S(1)} %get-tuple-element.18), channel_id=1, source_target_pairs={{1,0},{2,1},{3,2},{4,3},{5,4},{6,5},{7,6},{8,7},{9,8},{10,9},{11,1... | collective-permute-start | bytes 6152 | tf_op jit(solution)/shard_map/ppermute | solution.py:17
  42.2 170.2 %collective-permute-start.6 = (bf16[16,512,128]{2,1,0:T(8,128)(2,1)}, bf16[16,512,128]{2,1,0:T(8,128)(2,1)S(1)}, u32[]{:S(2)}, u32[]{:S(2)}) collective-permute-start(bf16[16,512,128]{2,1,0:T(8,128)(2,1)} %fusion.24), channel_id=1, source_target_pairs={{0,80},{16,96},{32,112},{1,81},{17,97},{33,113},{2,82},{18,98},{34... | collective-permute-start | bytes 6291464 | tf_op jit(solution)/shard_map/ppermute | solution.py:94
  94.1 120.0 %collective-permute-start.7 = (bf16[16,512,128]{2,1,0:T(8,128)(2,1)}, bf16[16,512,128]{2,1,0:T(8,128)(2,1)S(1)}, u32[]{:S(2)}, u32[]{:S(2)}) collective-permute-start(bf16[16,512,128]{2,1,0:T(8,128)(2,1)} %fusion.24), channel_id=1, source_target_pairs={{0,96},{16,112},{1,97},{17,113},{2,98},{18,114},{3,99},{19,115},{4... | collective-permute-start | bytes 6291464 | tf_op jit(solution)/shard_map/ppermute | solution.py:94
  198.2 17.5 %collective-permute-start.8 = (bf16[16,512,128]{2,1,0:T(8,128)(2,1)}, bf16[16,512,128]{2,1,0:T(8,128)(2,1)S(1)}, u32[]{:S(2)}, u32[]{:S(2)}) collective-permute-start(bf16[16,512,128]{2,1,0:T(8,128)(2,1)} %fusion.24), channel_id=1, source_target_pairs={{0,112},{1,113},{2,114},{3,115},{4,116},{5,117},{6,118},{7,119},{8... | collective-permute-start | bytes 6291464 | tf_op jit(solution)/shard_map/ppermute | solution.py:94
  234.2 8.6 %collective-permute-start.10 = (f32[2,128,512]{2,1,0:T(8,128)S(1)}, f32[2,128,512]{2,1,0:T(8,128)S(1)}, u32[]{:S(2)}, u32[]{:S(2)}) collective-permute-start(f32[2,128,512]{2,1,0:T(8,128)S(1)} %get-tuple-element.8), channel_id=1, source_target_pairs={{1,0},{2,1},{3,2},{4,3},{5,4},{6,5},{7,6},{8,7},{9,8},{10,9},{11,1... | collective-permute-start | bytes 1572872 | tf_op jit(solution)/shard_map/ppermute | solution.py:17
  236.2 5.7 %copy-start = (f32[16,128,512]{2,1,0:T(8,128)S(1)}, f32[16,128,512]{2,1,0:T(8,128)}, u32[]{:S(2)}) copy-start(f32[16,128,512]{2,1,0:T(8,128)} %convolution_bitcast_fusion) | copy-start | bytes 12582916
  236.2 10.8 %collective-permute-start.9 = (f32[2,128,512]{2,1,0:T(8,128)S(1)}, f32[2,128,512]{2,1,0:T(8,128)S(1)}, u32[]{:S(2)}, u32[]{:S(2)}) collective-permute-start(f32[2,128,512]{2,1,0:T(8,128)S(1)} %get-tuple-element.7), channel_id=1, source_target_pairs={{0,1},{1,2},{2,3},{3,4},{4,5},{5,6},{6,7},{7,8},{8,9},{9,10},{10,1... | collective-permute-start | bytes 1572872 | tf_op jit(solution)/shard_map/ppermute | solution.py:16
  388.1 0.8 copy-start.2
Sparse Core Ops, SparseCore 0:
  14.3 348.5 all-gather.2

commit v13 on v12

--- a/solution.py
+++ b/solution.py
@@ -45,16 +45,15 @@
 
 
 def _dot_kernel(lower_ref, g_ref, out_ref):
-    acc = jnp.zeros(out_ref.shape, jnp.float32)
-    for e in range(lower_ref.shape[0]):
-        acc = acc + lax.dot_general(
-            lower_ref[e], g_ref[e], (((1,), (1,)), ((), ())), preferred_element_type=jnp.float32
-        )
-    out_ref[...] = acc
+    for r in range(out_ref.shape[0]):
+        acc = jnp.zeros(out_ref.shape[1:], jnp.float32)
+        for e in range(lower_ref.shape[0]):
+            acc = acc + jnp.dot(g_ref[e, r], lower_ref[e], preferred_element_type=jnp.float32)
+        out_ref[r] = acc
 
 
-def middle_dot(lower_e, gathered):
-    count, epochs, _ = lower_e.shape
+def middle_dot(lower_t, gathered, step=2):
+    count, _, epochs = lower_t.shape
     _, rows, width, _ = gathered.shape
     cost = pl.CostEstimate(
         flops=2 * epochs * count * epochs * rows * width,
@@ -63,15 +62,15 @@
     )
     return pl.pallas_call(
         _dot_kernel,
-        out_shape=jax.ShapeDtypeStruct((rows, epochs, width), jnp.float32),
-        grid=(rows,),
+        out_shape=jax.ShapeDtypeStruct((rows, width, epochs), jnp.float32),
+        grid=(rows // step,),
         in_specs=[
             pl.BlockSpec((count, epochs, epochs), lambda i: (0, 0, 0)),
-            pl.BlockSpec((count, None, width, epochs), lambda i: (0, i, 0, 0)),
+            pl.BlockSpec((count, step, width, epochs), lambda i: (0, i, 0, 0)),
         ],
-        out_specs=pl.BlockSpec((None, epochs, width), lambda i: (i, 0, 0)),
+        out_specs=pl.BlockSpec((step, width, epochs), lambda i: (i, 0, 0)),
         cost_estimate=cost,
-    )(lower_e, gathered)
+    )(lower_t, gathered)
 
 
 def body(field, factor, kappa):
@@ -111,7 +110,7 @@
         jnp.concatenate([bottom, below], axis=0),
         gain[slab - EDGE + 2:slab + 2], gain[slab - EDGE + 3:slab + 1], last_outside=pos == last,
     )
-    timed_middle = middle_dot(jnp.transpose(lower, (1, 0, 2)), gathered)
+    timed_middle = jnp.transpose(middle_dot(jnp.transpose(lower, (1, 2, 0)), gathered), (0, 2, 1))
     ext = jnp.concatenate([top[EDGE - 2 * HALO:], timed_middle, bottom[:2 * HALO]], axis=0)
     out_middle = double_stencil(ext, gain[EDGE - 2:slab - EDGE + 4], gain[EDGE - 1:slab - EDGE + 3])
     product = jnp.concatenate([out_top, out_middle, out_bottom], axis=0)

time: 411 us -> 407 us (level)
  waiting for transfers between devices: 268 us -> 279 us
  matrix products: 15.5 us -> 10.3 us
    all_gather x1, waiting for transfers between devices: 109 us -> 117 us  [body(): gathered = lax.all_gather(middle, 'epoch', axis=0)]
    dot_general x1, matrix products: 15.5 us -> 10.3 us  [body(): jnp.einsum('tes,eijs->itj', weights, stacked, preferred_element_type=jnp....]
    pallas_call x1, Pallas kernels: 15.9 us -> 11.8 us  [middle_dot(): pl.pallas_call(_dot_kernel, out_shape=jax.ShapeDtypeStruct((rows, width,...]
    unnamed x18 -> x19, local copies, waits for them, and re-layouts: 22 us -> 22.1 us
  transfers between devices with their start and end apart: 12 -> 12, of which waited for: 6 -> 7; matrix products, arithmetic and copies ran while one was open for 13% -> 11% of each run, Pallas kernels for 0% -> 0%
where the time goes in v13:
time: 407 us; the launch traced here: 405 us
  waiting for transfers between devices  279 us (69%)
  local copies, waits for them, and re-layouts  42.1 us (10%)
  starting transfers between devices  25.1 us (6%)
  other arithmetic  20.5 us (5%)
  Pallas kernels  14.8 us (4%)
  between operations  13.7 us (3%)
  matrix products  10.3 us (3%)
    ppermute x7, waiting for transfers between devices, body(): slots.append(lax.ppermute(edges, 'epoch', pairs))  154 us
    all_gather x1, waiting for transfers between devices, body(): gathered = lax.all_gather(middle, 'epoch', axis=0)  117 us
    unnamed x19, local copies, waits for them, and re-layouts  22.1 us
    ppermute x7, starting transfers between devices, body(): slots.append(lax.ppermute(edges, 'epoch', pairs))  16.1 us
    pallas_call x1, Pallas kernels, middle_dot(): pl.pallas_call(_dot_kernel, out_shape=jax.ShapeDtypeStruct((rows, width,...  11.8 us
    dot_general x1, matrix products, body(): jnp.einsum('tes,eijs->itj', weights, stacked, preferred_element_type=jnp....  10.3 us
    transpose x1, local copies, waits for them, and re-layouts, body(): return jnp.transpose(product, (1, 0, 2))  10.3 us
  transfers between devices with their start and end apart: 12, of which 7 were waited for; matrix products, arithmetic and copies ran while one was open for 11% of the time, Pallas kernels for 0%

profile of v13, /device:TPU:62, one launch (start us, length us, event | category | flops | bytes accessed | tf_op | source)
XLA Modules:
  0.0 405.5 jit_solution(6243214445232655188)
XLA Ops:
  6.5 1.6 slice-done
  8.1 3.0 copy.35
  11.1 3.0 shard_map.37
  14.2 1.7 fusion.29
  19.4 4.5 %collective-permute-start.2 = (bf16[16,512,128]{2,1,0:T(8,128)(2,1)}, bf16[16,512,128]{2,1,0:T(8,128)(2,1)}, u32[]{:S(2)}, u32[]{:S(2)}) collective-permute-start(bf16[16,512,128]{2,1,0:T(8,128)(2,1)} %fusion.18), channel_id=1, source_target_pairs={{0,16},{16,32},{32,48},{48,64},{64,80},{80,96},{96,112},{1,17},{17... | collective-permute-start | bytes 6291464 | tf_op jit(solution)/shard_map/ppermute | solution.py:93
  23.9 3.5 collective-permute-start.3
  27.4 3.0 collective-permute-start.4
  30.5 2.7 collective-permute-start.5
  33.1 1.9 collective-permute-start
  35.3 1.6 bitcast_dynamic-update-slice_fusion.6
  38.0 2.6 collective-permute-start.1
  43.9 50.2 %collective-permute-done.2 = bf16[16,512,128]{2,1,0:T(8,128)(2,1)} collective-permute-done((bf16[16,512,128]{2,1,0:T(8,128)(2,1)}, bf16[16,512,128]{2,1,0:T(8,128)(2,1)}, u32[]{:S(2)}, u32[]{:S(2)}) %collective-permute-start.2) | collective-permute-done | bytes 2097184 | tf_op jit(solution)/shard_map/ppermute | solution.py:93
  94.9 103.3 %collective-permute-done.3 = bf16[16,512,128]{2,1,0:T(8,128)(2,1)} collective-permute-done((bf16[16,512,128]{2,1,0:T(8,128)(2,1)}, bf16[16,512,128]{2,1,0:T(8,128)(2,1)}, u32[]{:S(2)}, u32[]{:S(2)}) %collective-permute-start.3) | collective-permute-done | bytes 2097184 | tf_op jit(solution)/shard_map/ppermute | solution.py:93
  199.0 3.3 bitcast_dynamic-update-slice_fusion.5
  202.4 3.4 bitcast_dynamic-update-slice_fusion.4
  205.8 3.4 bitcast_dynamic-update-slice_fusion.3
  209.1 3.3 bitcast_dynamic-update-slice_fusion.2
  212.5 1.7 bitcast_dynamic-update-slice_fusion.1
  214.1 1.7 bitcast_dynamic-update-slice_fusion
  215.8 1.7 bitcast_dynamic-update-slice_fusion.7
  217.5 10.3 %convolution_bitcast_fusion = f32[16,128,512]{1,2,0:T(8,128)S(1)} fusion(bf16[8,16,512,128]{3,2,0,1:T(8,128)(2,1)} %bitcast_dynamic-update-slice_fusion.7, bf16[8,128,128]{1,2,0:T(8,128)(2,1)S(1)} %gather_fusion, pred[8]{0:T(512)(128)(4,1)S(1)} %compare_and_fusion.1), kind=kOutput, calls=%fused_computation.13 | convolution fusion | flops 2147614720 | bytes 21233672 | tf_op jit(solution)/shard_map/tes,eijs->itj/dot_general | solution.py:97
  227.9 1.9 collective-permute-start.10
  229.9 2.6 collective-permute-start.9
  233.9 2.6 collective-permute-done.10
  236.6 3.8 collective-permute-done.9
  245.5 117.4 %all-gather.3.cloned.1.call-done = bf16[128,512,128]{2,1,0:T(8,128)(2,1)} async-done(((bf16[16,512,128]{2,1,0:T(8,128)(2,1)}), bf16[128,512,128]{2,1,0:T(8,128)(2,1)}) %all-gather.3.cloned.1.call-update) | async-done | bytes 16777232 | tf_op jit(solution)/shard_map/all_gather | solution.py:86
  362.9 11.8 %shard_map.38 = f32[16,512,128]{2,1,0:T(8,128)} custom-call(bf16[8,128,128]{2,1,0:T(8,128)(2,1)} %bitcast.73, bf16[8,16,512,128]{3,2,1,0:T(8,128)(2,1)} %bitcast.69), custom_call_target="tpu_custom_call" | custom-call | flops 2147483648 | bytes 20971520 | tf_op jit(solution)/shard_map/pallas_call | solution.py:63
  374.7 2.9 pad_maximum_fusion
  378.2 3.6 fusion.1
  382.6 2.1 fusion.3
  384.8 3.6 maximum_bitcast_fusion
  388.4 10.3 %copy.29 = f32[128,32,512]{2,1,0:T(8,128)} copy(f32[128,32,512]{0,2,1:T(8,128)} %maximum_bitcast_fusion) | data formatting | bytes 16777216 | tf_op jit(solution)/shard_map/transpose | solution.py:117
  (53 shorter events, 17.6 us)
Async XLA Ops:
  6.5 1.6 slice-start
  6.5 356.3 %all-gather.3.cloned.1.call-start = ((), (), s32[]{:S(2)}) async-start(), calls=%async_computation | async-start | bytes 18874368 | tf_op jit(solution)/shard_map/all_gather | solution.py:86
  17.9 15.3 %copy-start.4 = (f32[32,512]{1,0:T(8,128)S(1)}, f32[32,512]{1,0:T(8,128)}, u32[]{:S(2)}) copy-start(f32[32,512]{1,0:T(8,128)} %param.5) | copy-start | bytes 196612
  17.9 17.2 %copy-start.2 = (bf16[128,1024]{1,0:T(8,128)(2,1)S(1)}, bf16[128,1024]{1,0:T(8,128)(2,1)}, u32[]{:S(2)}) copy-start(bf16[128,1024]{1,0:T(8,128)(2,1)} %param.4) | copy-start | bytes 786436
  19.4 74.7 %collective-permute-start.2 = (bf16[16,512,128]{2,1,0:T(8,128)(2,1)}, bf16[16,512,128]{2,1,0:T(8,128)(2,1)}, u32[]{:S(2)}, u32[]{:S(2)}) collective-permute-start(bf16[16,512,128]{2,1,0:T(8,128)(2,1)} %fusion.18), channel_id=1, source_target_pairs={{0,16},{16,32},{32,48},{48,64},{64,80},{80,96},{96,112},{1,17},{17... | collective-permute-start | bytes 6291464 | tf_op jit(solution)/shard_map/ppermute | solution.py:93
  23.9 174.4 %collective-permute-start.3 = (bf16[16,512,128]{2,1,0:T(8,128)(2,1)}, bf16[16,512,128]{2,1,0:T(8,128)(2,1)}, u32[]{:S(2)}, u32[]{:S(2)}) collective-permute-start(bf16[16,512,128]{2,1,0:T(8,128)(2,1)} %fusion.18), channel_id=1, source_target_pairs={{0,32},{16,48},{32,64},{48,80},{64,96},{80,112},{1,33},{17,49},{33... | collective-permute-start | bytes 6291464 | tf_op jit(solution)/shard_map/ppermute | solution.py:93
  27.4 178.3 %collective-permute-start.4 = (bf16[16,512,128]{2,1,0:T(8,128)(2,1)}, bf16[16,512,128]{2,1,0:T(8,128)(2,1)}, u32[]{:S(2)}, u32[]{:S(2)}) collective-permute-start(bf16[16,512,128]{2,1,0:T(8,128)(2,1)} %fusion.18), channel_id=1, source_target_pairs={{0,48},{16,64},{32,80},{48,96},{64,112},{1,49},{17,65},{33,81},{49... | collective-permute-start | bytes 6291464 | tf_op jit(solution)/shard_map/ppermute | solution.py:93
  30.5 178.7 %collective-permute-start.5 = (bf16[16,512,128]{2,1,0:T(8,128)(2,1)}, bf16[16,512,128]{2,1,0:T(8,128)(2,1)}, u32[]{:S(2)}, u32[]{:S(2)}) collective-permute-start(bf16[16,512,128]{2,1,0:T(8,128)(2,1)} %fusion.18), channel_id=1, source_target_pairs={{0,64},{16,80},{32,96},{48,112},{1,65},{17,81},{33,97},{49,113},{2... | collective-permute-start | bytes 6291464 | tf_op jit(solution)/shard_map/ppermute | solution.py:93
  33.1 4.9 %collective-permute-start = (f32[1,512]{1,0:T(1,128)S(1)}, f32[1,512]{1,0:T(1,128)S(1)}, u32[]{:S(2)}, u32[]{:S(2)}) collective-permute-start(f32[1,512]{1,0:T(1,128)S(1)} %get-tuple-element.17), channel_id=1, source_target_pairs={{0,1},{1,2},{2,3},{3,4},{4,5},{5,6},{6,7},{7,8},{8,9},{9,10},{10,1... | collective-permute-start | bytes 6152 | tf_op jit(solution)/shard_map/ppermute | solution.py:16
  38.0 3.8 collective-permute-start.1
  40.8 161.6 %copy-start.1 = (bf16[128,1024]{0,1:T(8,128)(2,1)}, bf16[128,1024]{0,1:T(8,128)(2,1)S(1)}, u32[]{:S(2)}) copy-start(bf16[128,1024]{0,1:T(8,128)(2,1)S(1)} %copy.26) | copy-start | bytes 786436
  41.9 170.6 %collective-permute-start.6 = (bf16[16,512,128]{2,1,0:T(8,128)(2,1)}, bf16[16,512,128]{2,1,0:T(8,128)(2,1)S(1)}, u32[]{:S(2)}, u32[]{:S(2)}) collective-permute-start(bf16[16,512,128]{2,1,0:T(8,128)(2,1)} %fusion.18), channel_id=1, source_target_pairs={{0,80},{16,96},{32,112},{1,81},{17,97},{33,113},{2,82},{18,98},{34... | collective-permute-start | bytes 6291464 | tf_op jit(solution)/shard_map/ppermute | solution.py:93
  94.1 120.0 %collective-permute-start.7 = (bf16[16,512,128]{2,1,0:T(8,128)(2,1)}, bf16[16,512,128]{2,1,0:T(8,128)(2,1)S(1)}, u32[]{:S(2)}, u32[]{:S(2)}) collective-permute-start(bf16[16,512,128]{2,1,0:T(8,128)(2,1)} %fusion.18), channel_id=1, source_target_pairs={{0,96},{16,112},{1,97},{17,113},{2,98},{18,114},{3,99},{19,115},{4... | collective-permute-start | bytes 6291464 | tf_op jit(solution)/shard_map/ppermute | solution.py:93
  198.2 17.6 %collective-permute-start.8 = (bf16[16,512,128]{2,1,0:T(8,128)(2,1)}, bf16[16,512,128]{2,1,0:T(8,128)(2,1)S(1)}, u32[]{:S(2)}, u32[]{:S(2)}) collective-permute-start(bf16[16,512,128]{2,1,0:T(8,128)(2,1)} %fusion.18), channel_id=1, source_target_pairs={{0,112},{1,113},{2,114},{3,115},{4,116},{5,117},{6,118},{7,119},{8... | collective-permute-start | bytes 6291464 | tf_op jit(solution)/shard_map/ppermute | solution.py:93
  227.9 8.6 %collective-permute-start.10 = (f32[2,128,512]{1,2,0:T(8,128)S(1)}, f32[2,128,512]{1,2,0:T(8,128)S(1)}, u32[]{:S(2)}, u32[]{:S(2)}) collective-permute-start(f32[2,128,512]{1,2,0:T(8,128)S(1)} %get-tuple-element.6), channel_id=1, source_target_pairs={{1,0},{2,1},{3,2},{4,3},{5,4},{6,5},{7,6},{8,7},{9,8},{10,9},{11,1... | collective-permute-start | bytes 1572872 | tf_op jit(solution)/shard_map/ppermute | solution.py:17
  229.9 10.5 %collective-permute-start.9 = (f32[2,128,512]{1,2,0:T(8,128)S(1)}, f32[2,128,512]{1,2,0:T(8,128)S(1)}, u32[]{:S(2)}, u32[]{:S(2)}) collective-permute-start(f32[2,128,512]{1,2,0:T(8,128)S(1)} %get-tuple-element.5), channel_id=1, source_target_pairs={{0,1},{1,2},{2,3},{3,4},{4,5},{5,6},{6,7},{7,8},{8,9},{9,10},{10,1... | collective-permute-start | bytes 1572872 | tf_op jit(solution)/shard_map/ppermute | solution.py:16
  381.8 0.8 copy-start.3
  382.6 2.2 copy-start
Sparse Core Ops, SparseCore 0:
  14.3 348.5 all-gather.2

commit v14 on v6

--- a/solution.py
+++ b/solution.py
@@ -51,7 +51,8 @@
     slots = [edges]
     for shift in range(1, count):
         pairs = [(e, e + shift) for e in range(count - shift)]
-        slots.append(lax.ppermute(edges, "epoch", pairs))
+        halves = [lax.ppermute(edges[h * EDGE:(h + 1) * EDGE], "epoch", pairs) for h in range(2)]
+        slots.append(jnp.concatenate(halves, axis=0))
     stacked = jnp.stack(slots, axis=0)
     source = jnp.clip(me - jnp.arange(count), 0, count - 1)
     weights = jnp.take(lower, source, axis=1)

time: 404 us -> 452 us (1.12)
  the two profiles are of different devices: /device:TPU:62 before, /device:TPU:7 now
where the time goes in v14:
time: 452 us; the launch traced here: 451 us
  waiting for transfers between devices  295 us (65%)
  starting transfers between devices  61.3 us (14%)
  local copies, waits for them, and re-layouts  32.2 us (7%)
  other arithmetic  31.1 us (7%)
  matrix products  18 us (4%)
  between operations  13.9 us (3%)
    ppermute x14, waiting for transfers between devices, body(): lax.ppermute(edges[h * EDGE:(h + 1) * EDGE], 'epoch', pairs)  284 us
    ppermute x14, starting transfers between devices, body(): lax.ppermute(edges[h * EDGE:(h + 1) * EDGE], 'epoch', pairs)  47.5 us
    dot_general x1, matrix products, body(): jnp.einsum('tes,eijs->itj', lower, gathered, preferred_element_type=jnp.f...  13.4 us
    ppermute x2, waiting for transfers between devices, neighbours(): below = lax.ppermute(top[:width], 'row', down)  10.7 us
  transfers between devices with their start and end apart: 19, of which 14 were waited for; matrix products, arithmetic and copies ran while one was open for 9% of the time, Pallas kernels for 0%

profile of v14, /device:TPU:7, one launch (start us, length us, event | category | flops | bytes accessed | tf_op | source)
XLA Modules:
  0.0 451.5 jit_solution(10432073539360183816)
XLA Ops:
  8.1 3.1 copy.79
  16.6 5.8 %collective-permute-start.2 = (bf16[8,512,128]{2,1,0:T(8,128)(2,1)}, bf16[8,512,128]{2,1,0:T(8,128)(2,1)}, u32[]{:S(2)}, u32[]{:S(2)}) collective-permute-start(bf16[8,512,128]{2,1,0:T(8,128)(2,1)} %get-tuple-element.13), channel_id=1, source_target_pairs={{0,16},{16,32},{32,48},{48,64},{64,80},{80,96},{96,112},{1,17},{17... | collective-permute-start | bytes 3145736 | tf_op jit(solution)/shard_map/ppermute | solution.py:54
  22.4 3.3 collective-permute-start.3
  25.7 3.5 collective-permute-start.4
  29.3 3.3 collective-permute-start.5
  32.6 4.8 %collective-permute-start = (f32[1,512]{1,0:T(1,128)S(1)}, f32[1,512]{1,0:T(1,128)S(1)}, u32[]{:S(2)}, u32[]{:S(2)}) collective-permute-start(f32[1,512]{1,0:T(1,128)S(1)} %get-tuple-element.19), channel_id=1, source_target_pairs={{0,1},{1,2},{2,3},{3,4},{4,5},{5,6},{6,7},{7,8},{8,9},{9,10},{10,1... | collective-permute-start | bytes 6152 | tf_op jit(solution)/shard_map/ppermute | solution.py:14
  38.1 3.1 collective-permute-start.1
  42.0 4.1 collective-permute-done.1
  46.1 2.8 collective-permute-start.6
  49.5 11.1 %collective-permute-done.2 = bf16[8,512,128]{2,1,0:T(8,128)(2,1)} collective-permute-done((bf16[8,512,128]{2,1,0:T(8,128)(2,1)}, bf16[8,512,128]{2,1,0:T(8,128)(2,1)}, u32[]{:S(2)}, u32[]{:S(2)}) %collective-permute-start.2) | collective-permute-done | bytes 1048608 | tf_op jit(solution)/shard_map/ppermute | solution.py:54
  60.6 7.4 %collective-permute-start.7 = (bf16[8,512,128]{2,1,0:T(8,128)(2,1)}, bf16[8,512,128]{2,1,0:T(8,128)(2,1)S(1)}, u32[]{:S(2)}, u32[]{:S(2)}) collective-permute-start(bf16[8,512,128]{2,1,0:T(8,128)(2,1)} %get-tuple-element.14), channel_id=1, source_target_pairs={{0,48},{16,64},{32,80},{48,96},{64,112},{1,49},{17,65},{33,81},{49... | collective-permute-start | bytes 3145736 | tf_op jit(solution)/shard_map/ppermute | solution.py:54
  68.0 20.5 %collective-permute-done.3 = bf16[8,512,128]{2,1,0:T(8,128)(2,1)} collective-permute-done((bf16[8,512,128]{2,1,0:T(8,128)(2,1)}, bf16[8,512,128]{2,1,0:T(8,128)(2,1)}, u32[]{:S(2)}, u32[]{:S(2)}) %collective-permute-start.3) | collective-permute-done | bytes 1048608 | tf_op jit(solution)/shard_map/ppermute | solution.py:54
  88.5 7.2 %collective-permute-start.8 = (bf16[8,512,128]{2,1,0:T(8,128)(2,1)}, bf16[8,512,128]{2,1,0:T(8,128)(2,1)S(1)}, u32[]{:S(2)}, u32[]{:S(2)}) collective-permute-start(bf16[8,512,128]{2,1,0:T(8,128)(2,1)} %get-tuple-element.13), channel_id=1, source_target_pairs={{0,64},{16,80},{32,96},{48,112},{1,65},{17,81},{33,97},{49,113},{2... | collective-permute-start | bytes 3145736 | tf_op jit(solution)/shard_map/ppermute | solution.py:54
  95.7 62.2 %collective-permute-done.4 = bf16[8,512,128]{2,1,0:T(8,128)(2,1)} collective-permute-done((bf16[8,512,128]{2,1,0:T(8,128)(2,1)}, bf16[8,512,128]{2,1,0:T(8,128)(2,1)}, u32[]{:S(2)}, u32[]{:S(2)}) %collective-permute-start.4) | collective-permute-done | bytes 1048608 | tf_op jit(solution)/shard_map/ppermute | solution.py:54
  158.0 6.1 %collective-permute-start.9 = (bf16[8,512,128]{2,1,0:T(8,128)(2,1)}, bf16[8,512,128]{2,1,0:T(8,128)(2,1)S(1)}, u32[]{:S(2)}, u32[]{:S(2)}) collective-permute-start(bf16[8,512,128]{2,1,0:T(8,128)(2,1)} %get-tuple-element.14), channel_id=1, source_target_pairs={{0,64},{16,80},{32,96},{48,112},{1,65},{17,81},{33,97},{49,113},{2... | collective-permute-start | bytes 3145736 | tf_op jit(solution)/shard_map/ppermute | solution.py:54
  164.1 29.7 %collective-permute-done.5 = bf16[8,512,128]{2,1,0:T(8,128)(2,1)} collective-permute-done((bf16[8,512,128]{2,1,0:T(8,128)(2,1)}, bf16[8,512,128]{2,1,0:T(8,128)(2,1)}, u32[]{:S(2)}, u32[]{:S(2)}) %collective-permute-start.5) | collective-permute-done | bytes 1048608 | tf_op jit(solution)/shard_map/ppermute | solution.py:54
  198.6 40.1 %collective-permute-done.8 = bf16[8,512,128]{2,1,0:T(8,128)(2,1)S(1)} collective-permute-done((bf16[8,512,128]{2,1,0:T(8,128)(2,1)}, bf16[8,512,128]{2,1,0:T(8,128)(2,1)S(1)}, u32[]{:S(2)}, u32[]{:S(2)}) %collective-permute-start.8) | collective-permute-done | bytes 1048608 | tf_op jit(solution)/shard_map/ppermute | solution.py:54
  240.1 35.8 %collective-permute-done.9 = bf16[8,512,128]{2,1,0:T(8,128)(2,1)S(1)} collective-permute-done((bf16[8,512,128]{2,1,0:T(8,128)(2,1)}, bf16[8,512,128]{2,1,0:T(8,128)(2,1)S(1)}, u32[]{:S(2)}, u32[]{:S(2)}) %collective-permute-start.9) | collective-permute-done | bytes 1048608 | tf_op jit(solution)/shard_map/ppermute | solution.py:54
  285.5 36.6 %collective-permute-done.13 = bf16[8,512,128]{2,1,0:T(8,128)(2,1)S(1)} collective-permute-done((bf16[8,512,128]{2,1,0:T(8,128)(2,1)}, bf16[8,512,128]{2,1,0:T(8,128)(2,1)S(1)}, u32[]{:S(2)}, u32[]{:S(2)}) %collective-permute-start.13) | collective-permute-done | bytes 1048608 | tf_op jit(solution)/shard_map/ppermute | solution.py:54
  322.4 7.7 %collective-permute-done.14 = bf16[8,512,128]{2,1,0:T(8,128)(2,1)S(1)} collective-permute-done((bf16[8,512,128]{2,1,0:T(8,128)(2,1)}, bf16[8,512,128]{2,1,0:T(8,128)(2,1)S(1)}, u32[]{:S(2)}, u32[]{:S(2)}) %collective-permute-start.14) | collective-permute-done | bytes 1048608 | tf_op jit(solution)/shard_map/ppermute | solution.py:54
  330.2 38.3 %collective-permute-done.15 = bf16[8,512,128]{2,1,0:T(8,128)(2,1)S(1)} collective-permute-done((bf16[8,512,128]{2,1,0:T(8,128)(2,1)}, bf16[8,512,128]{2,1,0:T(8,128)(2,1)S(1)}, u32[]{:S(2)}, u32[]{:S(2)}) %collective-permute-start.15) | collective-permute-done | bytes 1048608 | tf_op jit(solution)/shard_map/ppermute | solution.py:54
  368.8 4.6 %convolution_bitcast_fusion.1 = f32[16,128,512]{1,2,0:T(8,128)S(1)} fusion(bf16[8,16,512,128]{3,2,0,1:T(8,128)(2,1)S(1)} %fusion.22, bf16[8,128,128]{2,1,0:T(8,128)(2,1)S(1)} %gather_fusion, pred[8]{0:T(512)(128)(4,1)S(1)} %compare_and_fusion.1), kind=kOutput, calls=%fused_computation.20 | convolution fusion | flops 2147614720 | bytes 21233672 | tf_op jit(solution)/shard_map/tes,eijs->itj/dot_general | solution.py:59
  374.5 3.9 collective-permute-start.16
  384.9 6.5 %collective-permute-done.17 = f32[2,128,512]{1,2,0:T(8,128)} collective-permute-done((f32[2,128,512]{1,2,0:T(8,128)}, f32[2,128,512]{1,2,0:T(8,128)}, u32[]{:S(2)}, u32[]{:S(2)}) %collective-permute-start.17) | collective-permute-done | bytes 524320 | tf_op jit(solution)/shard_map/ppermute | solution.py:15
  391.4 2.7 fusion.6
  398.4 3.0 copy.70
  401.4 4.2 fusion.11
  408.0 13.4 %convolution_bitcast_fusion = f32[16,128,512]{2,1,0:T(8,128)} fusion(bf16[128,8,128,1]{0,2,3,1:T(8,128)(2,1)S(1)} %bitcast.96, bf16[8,16,512,128]{3,2,1,0:T(8,128)(2,1)} %bitcast.93), kind=kOutput, calls=%fused_computation.19 | convolution fusion | flops 2147483648 | bytes 21233664 | tf_op jit(solution)/shard_map/tes,eijs->itj/dot_general | solution.py:75
  421.4 2.9 pad_maximum_fusion
  425.3 4.3 fusion.2
  430.3 3.7 fusion.5
  436.4 8.3 %copy.72 = f32[128,32,512]{2,1,0:T(8,128)} copy(f32[128,32,512]{2,0,1:T(8,128)S(1)} %maximum_bitcast_fusion) | data formatting | bytes 16777216 | tf_op jit(solution)/shard_map/transpose | solution.py:79
  (78 shorter events, 43.4 us)
Async XLA Ops:
  6.5 1.6 slice-start
  6.5 401.5 %all-gather.3.cloned.1.call-start = ((), (), s32[]{:S(2)}) async-start(), calls=%async_computation | async-start | bytes 18874368 | tf_op jit(solution)/shard_map/all_gather | solution.py:47
  15.1 17.5 %copy-start.4 = (f32[32,512]{1,0:T(8,128)S(1)}, f32[32,512]{1,0:T(8,128)}, u32[]{:S(2)}) copy-start(f32[32,512]{1,0:T(8,128)} %param.5) | copy-start | bytes 196612
  15.1 22.3 %copy-start.3 = (bf16[128,1024]{1,0:T(8,128)(2,1)S(1)}, bf16[128,1024]{1,0:T(8,128)(2,1)}, u32[]{:S(2)}) copy-start(bf16[128,1024]{1,0:T(8,128)(2,1)} %param.4) | copy-start | bytes 786436
  16.6 44.0 %collective-permute-start.2 = (bf16[8,512,128]{2,1,0:T(8,128)(2,1)}, bf16[8,512,128]{2,1,0:T(8,128)(2,1)}, u32[]{:S(2)}, u32[]{:S(2)}) collective-permute-start(bf16[8,512,128]{2,1,0:T(8,128)(2,1)} %get-tuple-element.13), channel_id=1, source_target_pairs={{0,16},{16,32},{32,48},{48,64},{64,80},{80,96},{96,112},{1,17},{17... | collective-permute-start | bytes 3145736 | tf_op jit(solution)/shard_map/ppermute | solution.py:54
  22.4 66.0 %collective-permute-start.3 = (bf16[8,512,128]{2,1,0:T(8,128)(2,1)}, bf16[8,512,128]{2,1,0:T(8,128)(2,1)}, u32[]{:S(2)}, u32[]{:S(2)}) collective-permute-start(bf16[8,512,128]{2,1,0:T(8,128)(2,1)} %get-tuple-element.14), channel_id=1, source_target_pairs={{0,16},{16,32},{32,48},{48,64},{64,80},{80,96},{96,112},{1,17},{17... | collective-permute-start | bytes 3145736 | tf_op jit(solution)/shard_map/ppermute | solution.py:54
  25.7 132.2 %collective-permute-start.4 = (bf16[8,512,128]{2,1,0:T(8,128)(2,1)}, bf16[8,512,128]{2,1,0:T(8,128)(2,1)}, u32[]{:S(2)}, u32[]{:S(2)}) collective-permute-start(bf16[8,512,128]{2,1,0:T(8,128)(2,1)} %get-tuple-element.13), channel_id=1, source_target_pairs={{0,32},{16,48},{32,64},{48,80},{64,96},{80,112},{1,33},{17,49},{33... | collective-permute-start | bytes 3145736 | tf_op jit(solution)/shard_map/ppermute | solution.py:54
  29.3 164.6 %collective-permute-start.5 = (bf16[8,512,128]{2,1,0:T(8,128)(2,1)}, bf16[8,512,128]{2,1,0:T(8,128)(2,1)}, u32[]{:S(2)}, u32[]{:S(2)}) collective-permute-start(bf16[8,512,128]{2,1,0:T(8,128)(2,1)} %get-tuple-element.14), channel_id=1, source_target_pairs={{0,32},{16,48},{32,64},{48,80},{64,96},{80,112},{1,33},{17,49},{33... | collective-permute-start | bytes 3145736 | tf_op jit(solution)/shard_map/ppermute | solution.py:54
  32.6 5.5 %collective-permute-start = (f32[1,512]{1,0:T(1,128)S(1)}, f32[1,512]{1,0:T(1,128)S(1)}, u32[]{:S(2)}, u32[]{:S(2)}) collective-permute-start(f32[1,512]{1,0:T(1,128)S(1)} %get-tuple-element.19), channel_id=1, source_target_pairs={{0,1},{1,2},{2,3},{3,4},{4,5},{5,6},{6,7},{7,8},{8,9},{9,10},{10,1... | collective-permute-start | bytes 6152 | tf_op jit(solution)/shard_map/ppermute | solution.py:14
  38.1 8.0 %collective-permute-start.1 = (f32[1,512]{1,0:T(1,128)S(1)}, f32[1,512]{1,0:T(1,128)S(1)}, u32[]{:S(2)}, u32[]{:S(2)}) collective-permute-start(f32[1,512]{1,0:T(1,128)S(1)} %get-tuple-element.20), channel_id=1, source_target_pairs={{1,0},{2,1},{3,2},{4,3},{5,4},{6,5},{7,6},{8,7},{9,8},{10,9},{11,1... | collective-permute-start | bytes 6152 | tf_op jit(solution)/shard_map/ppermute | solution.py:15
  46.1 149.7 %collective-permute-start.6 = (bf16[8,512,128]{2,1,0:T(8,128)(2,1)}, bf16[8,512,128]{2,1,0:T(8,128)(2,1)S(1)}, u32[]{:S(2)}, u32[]{:S(2)}) collective-permute-start(bf16[8,512,128]{2,1,0:T(8,128)(2,1)} %get-tuple-element.13), channel_id=1, source_target_pairs={{0,48},{16,64},{32,80},{48,96},{64,112},{1,49},{17,65},{33,81},{49... | collective-permute-start | bytes 3145736 | tf_op jit(solution)/shard_map/ppermute | solution.py:54
  60.6 136.7 %collective-permute-start.7 = (bf16[8,512,128]{2,1,0:T(8,128)(2,1)}, bf16[8,512,128]{2,1,0:T(8,128)(2,1)S(1)}, u32[]{:S(2)}, u32[]{:S(2)}) collective-permute-start(bf16[8,512,128]{2,1,0:T(8,128)(2,1)} %get-tuple-element.14), channel_id=1, source_target_pairs={{0,48},{16,64},{32,80},{48,96},{64,112},{1,49},{17,65},{33,81},{49... | collective-permute-start | bytes 3145736 | tf_op jit(solution)/shard_map/ppermute | solution.py:54
  88.5 150.3 %collective-permute-start.8 = (bf16[8,512,128]{2,1,0:T(8,128)(2,1)}, bf16[8,512,128]{2,1,0:T(8,128)(2,1)S(1)}, u32[]{:S(2)}, u32[]{:S(2)}) collective-permute-start(bf16[8,512,128]{2,1,0:T(8,128)(2,1)} %get-tuple-element.13), channel_id=1, source_target_pairs={{0,64},{16,80},{32,96},{48,112},{1,65},{17,81},{33,97},{49,113},{2... | collective-permute-start | bytes 3145736 | tf_op jit(solution)/shard_map/ppermute | solution.py:54
  158.0 117.9 %collective-permute-start.9 = (bf16[8,512,128]{2,1,0:T(8,128)(2,1)}, bf16[8,512,128]{2,1,0:T(8,128)(2,1)S(1)}, u32[]{:S(2)}, u32[]{:S(2)}) collective-permute-start(bf16[8,512,128]{2,1,0:T(8,128)(2,1)} %get-tuple-element.14), channel_id=1, source_target_pairs={{0,64},{16,80},{32,96},{48,112},{1,65},{17,81},{33,97},{49,113},{2... | collective-permute-start | bytes 3145736 | tf_op jit(solution)/shard_map/ppermute | solution.py:54
  193.8 83.4 %collective-permute-start.10 = (bf16[8,512,128]{2,1,0:T(8,128)(2,1)}, bf16[8,512,128]{2,1,0:T(8,128)(2,1)S(1)}, u32[]{:S(2)}, u32[]{:S(2)}) collective-permute-start(bf16[8,512,128]{2,1,0:T(8,128)(2,1)} %get-tuple-element.13), channel_id=1, source_target_pairs={{0,80},{16,96},{32,112},{1,81},{17,97},{33,113},{2,82},{18,98},{34... | collective-permute-start | bytes 3145736 | tf_op jit(solution)/shard_map/ppermute | solution.py:54
  195.9 89.3 %collective-permute-start.11 = (bf16[8,512,128]{2,1,0:T(8,128)(2,1)}, bf16[8,512,128]{2,1,0:T(8,128)(2,1)S(1)}, u32[]{:S(2)}, u32[]{:S(2)}) collective-permute-start(bf16[8,512,128]{2,1,0:T(8,128)(2,1)} %get-tuple-element.14), channel_id=1, source_target_pairs={{0,80},{16,96},{32,112},{1,81},{17,97},{33,113},{2,82},{18,98},{34... | collective-permute-start | bytes 3145736 | tf_op jit(solution)/shard_map/ppermute | solution.py:54
  197.3 88.2 %collective-permute-start.12 = (bf16[8,512,128]{2,1,0:T(8,128)(2,1)}, bf16[8,512,128]{2,1,0:T(8,128)(2,1)S(1)}, u32[]{:S(2)}, u32[]{:S(2)}) collective-permute-start(bf16[8,512,128]{2,1,0:T(8,128)(2,1)} %get-tuple-element.13), channel_id=1, source_target_pairs={{0,96},{16,112},{1,97},{17,113},{2,98},{18,114},{3,99},{19,115},{4... | collective-permute-start | bytes 3145736 | tf_op jit(solution)/shard_map/ppermute | solution.py:54
  238.8 83.3 %collective-permute-start.13 = (bf16[8,512,128]{2,1,0:T(8,128)(2,1)}, bf16[8,512,128]{2,1,0:T(8,128)(2,1)S(1)}, u32[]{:S(2)}, u32[]{:S(2)}) collective-permute-start(bf16[8,512,128]{2,1,0:T(8,128)(2,1)} %get-tuple-element.14), channel_id=1, source_target_pairs={{0,96},{16,112},{1,97},{17,113},{2,98},{18,114},{3,99},{19,115},{4... | collective-permute-start | bytes 3145736 | tf_op jit(solution)/shard_map/ppermute | solution.py:54
  275.9 54.3 %collective-permute-start.14 = (bf16[8,512,128]{2,1,0:T(8,128)(2,1)}, bf16[8,512,128]{2,1,0:T(8,128)(2,1)S(1)}, u32[]{:S(2)}, u32[]{:S(2)}) collective-permute-start(bf16[8,512,128]{2,1,0:T(8,128)(2,1)} %get-tuple-element.13), channel_id=1, source_target_pairs={{0,112},{1,113},{2,114},{3,115},{4,116},{5,117},{6,118},{7,119},{8... | collective-permute-start | bytes 3145736 | tf_op jit(solution)/shard_map/ppermute | solution.py:54
  277.2 91.3 %collective-permute-start.15 = (bf16[8,512,128]{2,1,0:T(8,128)(2,1)}, bf16[8,512,128]{2,1,0:T(8,128)(2,1)S(1)}, u32[]{:S(2)}, u32[]{:S(2)}) collective-permute-start(bf16[8,512,128]{2,1,0:T(8,128)(2,1)} %get-tuple-element.14), channel_id=1, source_target_pairs={{0,112},{1,113},{2,114},{3,115},{4,116},{5,117},{6,118},{7,119},{8... | collective-permute-start | bytes 3145736 | tf_op jit(solution)/shard_map/ppermute | solution.py:54
  373.4 7.1 %copy-start = (f32[16,128,512]{1,2,0:T(8,128)}, f32[16,128,512]{1,2,0:T(8,128)S(1)}, u32[]{:S(2)}) copy-start(f32[16,128,512]{1,2,0:T(8,128)S(1)} %convolution_bitcast_fusion.1) | copy-start | bytes 12582916
  374.5 10.3 %collective-permute-start.16 = (f32[2,128,512]{1,2,0:T(8,128)}, f32[2,128,512]{1,2,0:T(8,128)}, u32[]{:S(2)}, u32[]{:S(2)}) collective-permute-start(f32[2,128,512]{1,2,0:T(8,128)} %get-tuple-element.5), channel_id=1, source_target_pairs={{0,1},{1,2},{2,3},{3,4},{4,5},{5,6},{6,7},{7,8},{8,9},{9,10},{10,1... | collective-permute-start | bytes 1572872 | tf_op jit(solution)/shard_map/ppermute | solution.py:14
  378.5 12.9 %collective-permute-start.17 = (f32[2,128,512]{1,2,0:T(8,128)}, f32[2,128,512]{1,2,0:T(8,128)}, u32[]{:S(2)}, u32[]{:S(2)}) collective-permute-start(f32[2,128,512]{1,2,0:T(8,128)} %get-tuple-element.6), channel_id=1, source_target_pairs={{1,0},{2,1},{3,2},{4,3},{5,4},{6,5},{7,6},{8,7},{9,8},{10,9},{11,1... | collective-permute-start | bytes 1572872 | tf_op jit(solution)/shard_map/ppermute | solution.py:15
  391.4 2.7 copy-start.6
  396.1 0.7 copy-start.5
  398.4 3.0 copy-start.7
  408.0 13.4 %copy-start.2 = (f32[4,128,512]{2,1,0:T(8,128)S(1)}, f32[4,128,512]{2,1,0:T(8,128)}, u32[]{:S(2)}) copy-start(f32[4,128,512]{2,1,0:T(8,128)} %copy.69) | copy-start | bytes 3145732
  430.3 3.7 copy-start.1
Sparse Core Ops, SparseCore 0:
  11.3 350.0 all-gather.2

commit v15 on v6

--- a/solution.py
+++ b/solution.py
@@ -1,7 +1,7 @@
 import jax
 import jax.numpy as jnp
 from jax import lax
-from jax.sharding import PartitionSpec as P
+from jax.sharding import Mesh, PartitionSpec as P
 
 EDGE = 8
 HALO = 2
@@ -36,22 +36,24 @@
 
 def body(field, factor, kappa):
     epochs, slab, width = field.shape
-    count = lax.axis_size("epoch")
+    planes, sides = lax.axis_size("z"), lax.axis_size("yh")
+    count = planes * sides
     order = epochs * count
-    me = lax.axis_index("epoch")
+    me = lax.axis_index("z") * sides + lax.axis_index("yh")
     global_rows = me * epochs + lax.broadcasted_iota(jnp.int32, (epochs, order), 0)
     global_cols = lax.broadcasted_iota(jnp.int32, (epochs, order), 1)
     lower = jnp.where(global_cols <= global_rows, factor, jnp.zeros_like(factor))
     lower = lower.reshape(epochs, count, epochs)
     middle = jnp.transpose(field[:, EDGE:slab - EDGE], (1, 2, 0))
-    gathered = lax.all_gather(middle, "epoch", axis=0)
+    pair = lax.all_gather(middle, "yh", axis=0)
+    gathered = lax.all_gather(pair, "z", axis=0).reshape((count,) + middle.shape)
     edges = jnp.transpose(
         jnp.concatenate([field[:, :EDGE], field[:, slab - EDGE:]], axis=1), (1, 2, 0)
     )
     slots = [edges]
     for shift in range(1, count):
         pairs = [(e, e + shift) for e in range(count - shift)]
-        slots.append(lax.ppermute(edges, "epoch", pairs))
+        slots.append(lax.ppermute(edges, ("z", "yh"), pairs))
     stacked = jnp.stack(slots, axis=0)
     source = jnp.clip(me - jnp.arange(count), 0, count - 1)
     weights = jnp.take(lower, source, axis=1)
@@ -79,6 +81,12 @@
 
 
 def solution(mesh):
-    in_specs = (P("epoch", "row", None), P("epoch", None), P("row", None))
-    out_specs = P("epoch", "row", None)
-    return jax.shard_map(body, mesh=mesh, in_specs=in_specs, out_specs=out_specs, check_vma=False)
+    devices = mesh.devices
+    planes = 4 if devices.shape[0] % 4 == 0 else 1
+    view = Mesh(
+        devices.reshape(planes, devices.shape[0] // planes, devices.shape[1]), ("z", "yh", "row")
+    )
+    epoch = ("z", "yh")
+    in_specs = (P(epoch, "row", None), P(epoch, None), P("row", None))
+    out_specs = P(epoch, "row", None)
+    return jax.shard_map(body, mesh=view, in_specs=in_specs, out_specs=out_specs, check_vma=False)

time: 404 us -> 455 us (1.13)
  waiting for transfers between devices: 262 us -> 306 us
  local copies, waits for them, and re-layouts: 49 us -> 54 us
    all_gather x1 -> x2, waiting for transfers between devices: 104 us -> 136 us  [the longest x1 75.5 us: body(): lax.all_gather(pair, 'z', axis=0).reshape((count,) + middle.shape)]
    ppermute x7, waiting for transfers between devices: 154 us -> 166 us  [body(): slots.append(lax.ppermute(edges, ('z', 'yh'), pairs))]
    all_gather x0 -> x1, local copies, waits for them, and re-layouts: none -> 4.7 us  [body(): pair = lax.all_gather(middle, 'yh', axis=0)]
  transfers between devices with their start and end apart: 12 -> 13, of which waited for: 5 -> 6; matrix products, arithmetic and copies ran while one was open for 15% -> 13% of each run, Pallas kernels for 0% -> 0%
where the time goes in v15:
time: 455 us; the launch traced here: 450 us
  waiting for transfers between devices  306 us (67%)
  local copies, waits for them, and re-layouts  54 us (12%)
  other arithmetic  28.6 us (6%)
  starting transfers between devices  25.6 us (6%)
  matrix products  21.7 us (5%)
  between operations  13.8 us (3%)
    ppermute x7, waiting for transfers between devices, body(): slots.append(lax.ppermute(edges, ('z', 'yh'), pairs))  166 us
    all_gather x1, waiting for transfers between devices, body(): lax.all_gather(pair, 'z', axis=0).reshape((count,) + middle.shape)  75.5 us
    all_gather x1, waiting for transfers between devices, body(): pair = lax.all_gather(middle, 'yh', axis=0)  61 us
    unnamed x26, local copies, waits for them, and re-layouts  22.8 us
    ppermute x7, starting transfers between devices, body(): slots.append(lax.ppermute(edges, ('z', 'yh'), pairs))  15.3 us
    dot_general x1, matrix products, body(): jnp.einsum('tes,eijs->itj', lower, gathered, preferred_element_type=jnp.f...  13.4 us
  transfers between devices with their start and end apart: 13, of which 6 were waited for; matrix products, arithmetic and copies ran while one was open for 13% of the time, Pallas kernels for 0%

profile of v15, /device:TPU:62, one launch (start us, length us, event | category | flops | bytes accessed | tf_op | source)
XLA Modules:
  0.0 449.9 jit_solution(11974642727708213297)
XLA Ops:
  8.1 3.0 copy.79
  11.2 61.0 %all-gather.5.cloned.1.call-done = bf16[32,512,128]{2,1,0:T(8,128)(2,1)} async-done(((bf16[16,512,128]{2,1,0:T(8,128)(2,1)}), bf16[32,512,128]{2,1,0:T(8,128)(2,1)}) %all-gather.5.cloned.1.call-update) | async-done | bytes 4194320 | tf_op jit(solution)/shard_map/all_gather | solution.py:48
  72.2 4.7 %copy.66 = bf16[2,16,512,128]{3,2,0,1:T(8,128)(2,1)} copy(bf16[2,16,512,128]{3,2,1,0:T(8,128)(2,1)} %bitcast.76) | data formatting | bytes 8388608 | tf_op jit(solution)/shard_map/all_gather | solution.py:48
  82.1 5.0 %collective-permute-start.2 = (bf16[16,512,128]{2,1,0:T(8,128)(2,1)}, bf16[16,512,128]{2,1,0:T(8,128)(2,1)}, u32[]{:S(2)}, u32[]{:S(2)}) collective-permute-start(bf16[16,512,128]{2,1,0:T(8,128)(2,1)} %fusion.20), channel_id=1, source_target_pairs={{0,16},{16,32},{32,48},{48,64},{64,80},{80,96},{96,112},{1,17},{17... | collective-permute-start | bytes 6291464 | tf_op jit(solution)/shard_map/ppermute | solution.py:56
  87.1 3.2 collective-permute-start.3
  90.3 2.1 collective-permute-start.4
  92.5 2.6 collective-permute-start.5
  95.1 1.9 collective-permute-start
  100.0 3.2 collective-permute-start.1
  105.4 29.0 %collective-permute-done.2 = bf16[16,512,128]{2,1,0:T(8,128)(2,1)} collective-permute-done((bf16[16,512,128]{2,1,0:T(8,128)(2,1)}, bf16[16,512,128]{2,1,0:T(8,128)(2,1)}, u32[]{:S(2)}, u32[]{:S(2)}) %collective-permute-start.2) | collective-permute-done | bytes 2097184 | tf_op jit(solution)/shard_map/ppermute | solution.py:56
  135.2 136.9 %collective-permute-done.3 = bf16[16,512,128]{2,1,0:T(8,128)(2,1)} collective-permute-done((bf16[16,512,128]{2,1,0:T(8,128)(2,1)}, bf16[16,512,128]{2,1,0:T(8,128)(2,1)}, u32[]{:S(2)}, u32[]{:S(2)}) %collective-permute-start.3) | collective-permute-done | bytes 2097184 | tf_op jit(solution)/shard_map/ppermute | solution.py:56
  273.5 3.4 bitcast_dynamic-update-slice_fusion.5
  276.9 3.4 bitcast_dynamic-update-slice_fusion.4
  280.4 3.3 bitcast_dynamic-update-slice_fusion.3
  283.7 3.4 bitcast_dynamic-update-slice_fusion.2
  288.8 1.7 bitcast_dynamic-update-slice_fusion
  292.2 8.3 %convolution_bitcast_fusion.1 = f32[16,128,512]{1,2,0:T(8,128)S(1)} fusion(bf16[8,16,512,128]{3,2,0,1:T(8,128)(2,1)} %bitcast_dynamic-update-slice_fusion.7, bf16[8,128,128]{2,1,0:T(8,128)(2,1)S(1)} %gather_fusion, pred[8]{0:T(512)(128)(4,1)S(1)} %compare_and_fusion.1), kind=kOutput, calls=%fused_computation.20 | convolution fusion | flops 2147614720 | bytes 21233672 | tf_op jit(solution)/shard_map/tes,eijs->itj/dot_general | solution.py:60
  301.7 1.9 collective-permute-start.10
  303.6 3.2 collective-permute-start.9
  308.6 2.5 fusion.29
  311.1 3.3 collective-permute-done.9
  314.4 2.7 fusion.6
  317.1 2.0 fusion.15
  321.3 3.1 copy.70
  324.4 4.0 fusion.11
  330.9 75.5 %all-gather.7.cloned.1.call-done = bf16[8,16,512,128]{3,2,0,1:T(8,128)(2,1)} async-done(((bf16[2,16,512,128]{3,2,0,1:T(8,128)(2,1)}), bf16[8,16,512,128]{3,2,0,1:T(8,128)(2,1)}) %all-gather.7.cloned.1.call-update) | async-done | bytes 16777232 | tf_op jit(solution)/shard_map/all_gather | solution.py:49
  406.4 13.4 %convolution_bitcast_fusion = f32[16,128,512]{2,1,0:T(8,128)} fusion(bf16[128,8,128,1]{0,2,1,3:T(8,128)(2,1)S(1)} %bitcast.78, bf16[8,16,512,128]{3,2,0,1:T(8,128)(2,1)} %all-gather.7.cloned.1.call-done), kind=kOutput, calls=%fused_computation.19 | convolution fusion | flops 2147483648 | bytes 21233664 | tf_op jit(solution)/shard_map/tes,eijs->itj/dot_general | solution.py:76
  419.8 2.9 pad_maximum_fusion
  423.7 4.3 fusion.2
  428.6 3.7 fusion.5
  432.4 2.4 maximum_bitcast_fusion
  434.8 8.3 %copy.72 = f32[128,32,512]{2,1,0:T(8,128)} copy(f32[128,32,512]{2,0,1:T(8,128)S(1)} %maximum_bitcast_fusion) | data formatting | bytes 16777216 | tf_op jit(solution)/shard_map/transpose | solution.py:80
  (67 shorter events, 26.6 us)
Async XLA Ops:
  6.5 1.6 slice-start
  6.5 65.7 %all-gather.5.cloned.1.call-start = ((), (), s32[]{:S(2)}) async-start(), calls=%async_computation | async-start | bytes 6291456 | tf_op jit(solution)/shard_map/all_gather | solution.py:48
  11.2 395.2 %all-gather.7.cloned.1.call-start = ((), (), s32[]{:S(2)}) async-start(), calls=%async_computation.1 | async-start | bytes 20971520 | tf_op jit(solution)/shard_map/all_gather | solution.py:49
  80.6 14.5 %copy-start.4 = (f32[32,512]{1,0:T(8,128)S(1)}, f32[32,512]{1,0:T(8,128)}, u32[]{:S(2)}) copy-start(f32[32,512]{1,0:T(8,128)} %param.5) | copy-start | bytes 196612
  80.6 16.4 %copy-start.3 = (bf16[128,1024]{1,0:T(8,128)(2,1)S(1)}, bf16[128,1024]{1,0:T(8,128)(2,1)}, u32[]{:S(2)}) copy-start(bf16[128,1024]{1,0:T(8,128)(2,1)} %param.4) | copy-start | bytes 786436
  82.1 52.2 %collective-permute-start.2 = (bf16[16,512,128]{2,1,0:T(8,128)(2,1)}, bf16[16,512,128]{2,1,0:T(8,128)(2,1)}, u32[]{:S(2)}, u32[]{:S(2)}) collective-permute-start(bf16[16,512,128]{2,1,0:T(8,128)(2,1)} %fusion.20), channel_id=1, source_target_pairs={{0,16},{16,32},{32,48},{48,64},{64,80},{80,96},{96,112},{1,17},{17... | collective-permute-start | bytes 6291464 | tf_op jit(solution)/shard_map/ppermute | solution.py:56
  87.1 185.0 %collective-permute-start.3 = (bf16[16,512,128]{2,1,0:T(8,128)(2,1)}, bf16[16,512,128]{2,1,0:T(8,128)(2,1)}, u32[]{:S(2)}, u32[]{:S(2)}) collective-permute-start(bf16[16,512,128]{2,1,0:T(8,128)(2,1)} %fusion.20), channel_id=1, source_target_pairs={{0,32},{16,48},{32,64},{48,80},{64,96},{80,112},{1,33},{17,49},{33... | collective-permute-start | bytes 6291464 | tf_op jit(solution)/shard_map/ppermute | solution.py:56
  90.3 190.0 %collective-permute-start.4 = (bf16[16,512,128]{2,1,0:T(8,128)(2,1)}, bf16[16,512,128]{2,1,0:T(8,128)(2,1)}, u32[]{:S(2)}, u32[]{:S(2)}) collective-permute-start(bf16[16,512,128]{2,1,0:T(8,128)(2,1)} %fusion.20), channel_id=1, source_target_pairs={{0,48},{16,64},{32,80},{48,96},{64,112},{1,49},{17,65},{33,81},{49... | collective-permute-start | bytes 6291464 | tf_op jit(solution)/shard_map/ppermute | solution.py:56
  92.5 191.2 %collective-permute-start.5 = (bf16[16,512,128]{2,1,0:T(8,128)(2,1)}, bf16[16,512,128]{2,1,0:T(8,128)(2,1)}, u32[]{:S(2)}, u32[]{:S(2)}) collective-permute-start(bf16[16,512,128]{2,1,0:T(8,128)(2,1)} %fusion.20), channel_id=1, source_target_pairs={{0,64},{16,80},{32,96},{48,112},{1,65},{17,81},{33,97},{49,113},{2... | collective-permute-start | bytes 6291464 | tf_op jit(solution)/shard_map/ppermute | solution.py:56
  95.1 4.9 %collective-permute-start = (f32[1,512]{1,0:T(1,128)S(1)}, f32[1,512]{1,0:T(1,128)S(1)}, u32[]{:S(2)}, u32[]{:S(2)}) collective-permute-start(f32[1,512]{1,0:T(1,128)S(1)} %get-tuple-element.17), channel_id=1, source_target_pairs={{0,1},{1,2},{2,3},{3,4},{4,5},{5,6},{6,7},{7,8},{8,9},{9,10},{10,1... | collective-permute-start | bytes 6152 | tf_op jit(solution)/shard_map/ppermute | solution.py:14
  100.0 4.6 %collective-permute-start.1 = (f32[1,512]{1,0:T(1,128)S(1)}, f32[1,512]{1,0:T(1,128)S(1)}, u32[]{:S(2)}, u32[]{:S(2)}) collective-permute-start(f32[1,512]{1,0:T(1,128)S(1)} %get-tuple-element.18), channel_id=1, source_target_pairs={{1,0},{2,1},{3,2},{4,3},{5,4},{6,5},{7,6},{8,7},{9,8},{10,9},{11,1... | collective-permute-start | bytes 6152 | tf_op jit(solution)/shard_map/ppermute | solution.py:15
  104.6 182.6 %collective-permute-start.6 = (bf16[16,512,128]{2,1,0:T(8,128)(2,1)}, bf16[16,512,128]{2,1,0:T(8,128)(2,1)S(1)}, u32[]{:S(2)}, u32[]{:S(2)}) collective-permute-start(bf16[16,512,128]{2,1,0:T(8,128)(2,1)} %fusion.20), channel_id=1, source_target_pairs={{0,80},{16,96},{32,112},{1,81},{17,97},{33,113},{2,82},{18,98},{34... | collective-permute-start | bytes 6291464 | tf_op jit(solution)/shard_map/ppermute | solution.py:56
  134.4 154.4 %collective-permute-start.7 = (bf16[16,512,128]{2,1,0:T(8,128)(2,1)}, bf16[16,512,128]{2,1,0:T(8,128)(2,1)S(1)}, u32[]{:S(2)}, u32[]{:S(2)}) collective-permute-start(bf16[16,512,128]{2,1,0:T(8,128)(2,1)} %fusion.20), channel_id=1, source_target_pairs={{0,96},{16,112},{1,97},{17,113},{2,98},{18,114},{3,99},{19,115},{4... | collective-permute-start | bytes 6291464 | tf_op jit(solution)/shard_map/ppermute | solution.py:56
  272.1 18.4 %collective-permute-start.8 = (bf16[16,512,128]{2,1,0:T(8,128)(2,1)}, bf16[16,512,128]{2,1,0:T(8,128)(2,1)S(1)}, u32[]{:S(2)}, u32[]{:S(2)}) collective-permute-start(bf16[16,512,128]{2,1,0:T(8,128)(2,1)} %fusion.20), channel_id=1, source_target_pairs={{0,112},{1,113},{2,114},{3,115},{4,116},{5,117},{6,118},{7,119},{8... | collective-permute-start | bytes 6291464 | tf_op jit(solution)/shard_map/ppermute | solution.py:56
  300.5 6.4 %copy-start = (f32[16,128,512]{1,2,0:T(8,128)}, f32[16,128,512]{1,2,0:T(8,128)S(1)}, u32[]{:S(2)}) copy-start(f32[16,128,512]{1,2,0:T(8,128)S(1)} %convolution_bitcast_fusion.1) | copy-start | bytes 12582916
  301.7 9.5 %collective-permute-start.10 = (f32[2,128,512]{1,2,0:T(8,128)}, f32[2,128,512]{1,2,0:T(8,128)}, u32[]{:S(2)}, u32[]{:S(2)}) collective-permute-start(f32[2,128,512]{1,2,0:T(8,128)} %get-tuple-element.6), channel_id=1, source_target_pairs={{1,0},{2,1},{3,2},{4,3},{5,4},{6,5},{7,6},{8,7},{9,8},{10,9},{11,1... | collective-permute-start | bytes 1572872 | tf_op jit(solution)/shard_map/ppermute | solution.py:15
  303.6 10.8 %collective-permute-start.9 = (f32[2,128,512]{1,2,0:T(8,128)}, f32[2,128,512]{1,2,0:T(8,128)}, u32[]{:S(2)}, u32[]{:S(2)}) collective-permute-start(f32[2,128,512]{1,2,0:T(8,128)} %get-tuple-element.5), channel_id=1, source_target_pairs={{0,1},{1,2},{2,3},{3,4},{4,5},{5,6},{6,7},{7,8},{8,9},{9,10},{10,1... | collective-permute-start | bytes 1572872 | tf_op jit(solution)/shard_map/ppermute | solution.py:14
  314.4 2.7 copy-start.7
  319.1 0.7 copy-start.5
  321.3 3.1 copy-start.6
  406.4 13.4 %copy-start.2 = (f32[4,128,512]{2,1,0:T(8,128)S(1)}, f32[4,128,512]{2,1,0:T(8,128)}, u32[]{:S(2)}) copy-start(f32[4,128,512]{2,1,0:T(8,128)} %copy.69) | copy-start | bytes 3145732
  428.6 3.7 copy-start.1
Sparse Core Ops, SparseCore 0:
  11.3 60.8 all-gather.4
  77.0 329.2 all-gather.6

commit v16 on v9

--- a/solution.py
+++ b/solution.py
@@ -3,7 +3,7 @@
 from jax import lax
 from jax.sharding import PartitionSpec as P
 
-EDGE = 10
+EDGE = 6
 HALO = 2
 
 

time: 407 us -> 427 us (1.049)
  other arithmetic: 25.9 us -> 34.1 us
  matrix products: 14.6 us -> 20.1 us
    ppermute x7, waiting for transfers between devices: 174 us -> 111 us  [body(): slots.append(lax.ppermute(edges, 'epoch', pairs))]
    all_gather x1, waiting for transfers between devices: 99.1 us -> 161 us  [body(): gathered = lax.all_gather(middle, 'epoch', axis=0)]
    sub x1, other arithmetic: 3.53 us -> 12.9 us  [double_stencil(): once = gain_once * ext[1:-1] - (ext[:-2] + ext[2:] + side_sum(ext[1:-1]))]
    dot_general x1, matrix products: 8.91 us -> 13.5 us  [body(): jnp.einsum('tes,eijs->itj', lower, gathered, preferred_element_type=jnp.f...]
    unnamed x40 -> x38, local copies, waits for them, and re-layouts: 18.1 us -> 19.4 us
  transfers between devices with their start and end apart: 12 -> 12, of which waited for: 4 -> 4; matrix products, arithmetic and copies ran while one was open for 14% -> 12% of each run, Pallas kernels for 0% -> 0%
where the time goes in v16:
time: 427 us; the launch traced here: 422 us
  waiting for transfers between devices  273 us (64%)
  local copies, waits for them, and re-layouts  55.7 us (13%)
  other arithmetic  34.1 us (8%)
  starting transfers between devices  25.6 us (6%)
  matrix products  20.1 us (5%)
  between operations  13.8 us (3%)
    all_gather x1, waiting for transfers between devices, body(): gathered = lax.all_gather(middle, 'epoch', axis=0)  161 us
    ppermute x7, waiting for transfers between devices, body(): slots.append(lax.ppermute(edges, 'epoch', pairs))  111 us
    unnamed x38, local copies, waits for them, and re-layouts  19.4 us
    ppermute x7, starting transfers between devices, body(): slots.append(lax.ppermute(edges, 'epoch', pairs))  14.7 us
    dot_general x1, matrix products, body(): jnp.einsum('tes,eijs->itj', lower, gathered, preferred_element_type=jnp.f...  13.5 us
    sub x1, other arithmetic, double_stencil(): once = gain_once * ext[1:-1] - (ext[:-2] + ext[2:] + side_sum(ext[1:-1]))  12.9 us
    sub x3, other arithmetic, double_stencil(): return gain_out * once[1:-1] - (once[:-2] + once[2:] + side_sum(once[1:-1]))  8.98 us
  transfers between devices with their start and end apart: 12, of which 4 were waited for; matrix products, arithmetic and copies ran while one was open for 12% of the time, Pallas kernels for 0%

profile of v16, /device:TPU:62, one launch (start us, length us, event | category | flops | bytes accessed | tf_op | source)
XLA Modules:
  0.0 422.3 jit_solution(16813240499059546876)
XLA Ops:
  6.5 4.1 slice.165
  10.6 3.2 copy.79
  13.9 2.9 fusion.28
  16.7 1.8 copy.77
  19.6 4.5 %collective-permute-start.2 = (bf16[12,512,128]{2,1,0:T(8,128)(2,1)S(1)}, bf16[12,512,128]{2,1,0:T(8,128)(2,1)}, u32[]{:S(2)}, u32[]{:S(2)}) collective-permute-start(bf16[12,512,128]{2,1,0:T(8,128)(2,1)S(1)} %fusion.20), channel_id=1, source_target_pairs={{0,16},{16,32},{32,48},{48,64},{64,80},{80,96},{96,112},{1,17},{17... | collective-permute-start | bytes 4718600 | tf_op jit(solution)/shard_map/ppermute | solution.py:54
  24.1 3.5 collective-permute-start.3
  27.6 3.0 collective-permute-start.4
  30.7 1.9 collective-permute-start
  32.6 3.6 collective-permute-start.1
  44.0 44.5 %collective-permute-done.2 = bf16[12,512,128]{2,1,0:T(8,128)(2,1)} collective-permute-done((bf16[12,512,128]{2,1,0:T(8,128)(2,1)S(1)}, bf16[12,512,128]{2,1,0:T(8,128)(2,1)}, u32[]{:S(2)}, u32[]{:S(2)}) %collective-permute-start.2) | collective-permute-done | bytes 1572896 | tf_op jit(solution)/shard_map/ppermute | solution.py:54
  89.8 66.8 %collective-permute-done.3 = bf16[12,512,128]{2,1,0:T(8,128)(2,1)} collective-permute-done((bf16[12,512,128]{2,1,0:T(8,128)(2,1)S(1)}, bf16[12,512,128]{2,1,0:T(8,128)(2,1)}, u32[]{:S(2)}, u32[]{:S(2)}) %collective-permute-start.3) | collective-permute-done | bytes 1572896 | tf_op jit(solution)/shard_map/ppermute | solution.py:54
  157.4 2.8 bitcast_dynamic-update-slice_fusion.5
  160.2 2.8 bitcast_dynamic-update-slice_fusion.4
  163.0 2.8 bitcast_dynamic-update-slice_fusion.3
  168.6 1.4 bitcast_dynamic-update-slice_fusion
  171.4 6.6 %convolution_bitcast_fusion.1 = f32[12,128,512]{1,2,0:T(8,128)S(1)} fusion(bf16[8,12,512,128]{3,2,0,1:T(8,128)(2,1)} %bitcast_dynamic-update-slice_fusion.7, bf16[8,128,128]{2,1,0:T(8,128)(2,1)S(1)} %copy-done.5, pred[8]{0:T(512)(128)(4,1)S(1)} %copy-done.11), kind=kOutput, calls=%fused_computation.20 | convolution fusion | flops 1610743808 | bytes 15990792 | tf_op jit(solution)/shard_map/tes,eijs->itj/dot_general | solution.py:58
  179.1 1.9 collective-permute-start.10
  181.0 3.4 collective-permute-start.9
  184.4 1.6 fusion.31
  186.0 2.5 copy.68
  188.6 2.6 copy.69
  193.2 1.7 fusion.15
  196.4 2.6 copy.70
  199.0 1.7 fusion.11
  201.5 161.2 %all-gather.3.cloned.1.call-done = bf16[160,512,128]{2,1,0:T(8,128)(2,1)} async-done(((bf16[20,512,128]{2,1,0:T(8,128)(2,1)}), bf16[160,512,128]{2,1,0:T(8,128)(2,1)}) %all-gather.3.cloned.1.call-update) | async-done | bytes 20971536 | tf_op jit(solution)/shard_map/all_gather | solution.py:47
  362.7 13.5 %convolution_bitcast_fusion = f32[20,128,512]{2,1,0:T(8,128)} fusion(bf16[128,8,128,1]{0,2,3,1:T(8,128)(2,1)S(1)} %bitcast.82, bf16[8,20,512,128]{3,2,1,0:T(8,128)(2,1)} %bitcast.79), kind=kOutput, calls=%fused_computation.15 | convolution fusion | flops 2684354560 | bytes 26476544 | tf_op jit(solution)/shard_map/tes,eijs->itj/dot_general | solution.py:74
  376.2 3.0 pad_maximum_fusion
  379.2 3.7 slice.205
  383.0 12.9 %fusion.2 = f32[26,128,512]{2,1,0:T(8,128)} fusion(f32[26,128,512]{2,1,0:T(8,128)} %slice.205, f32[28,128,512]{2,1,0:T(8,128)S(1)} %pad_maximum_fusion, f32[26,512]{1,0:T(8,128)S(1)} %slice_bitcast_fusion), kind=kLoop, calls=%fused_computation.9 | loop fusion | flops 8519680 | bytes 27316224 | tf_op jit(solution)/shard_map/sub | solution.py:25
  395.9 2.8 slice-done
  398.6 7.3 %fusion.5 = f32[24,128,512]{2,1,0:T(8,128)S(1)} fusion(f32[24,128,512]{2,1,0:T(8,128)S(1)} %slice-done, f32[26,128,512]{2,1,0:T(8,128)} %fusion.2, f32[24,512]{1,0:T(8,128)S(1)} %slice_bitcast_fusion.1), kind=kLoop, calls=%fused_computation.13 | loop fusion | flops 7864320 | bytes 25214976 | tf_op jit(solution)/shard_map/sub | solution.py:34
  407.2 8.3 %copy.72 = f32[128,32,512]{2,1,0:T(8,128)} copy(f32[128,32,512]{2,0,1:T(8,128)S(1)} %maximum_bitcast_fusion) | data formatting | bytes 16777216 | tf_op jit(solution)/shard_map/transpose | solution.py:78
  (75 shorter events, 21.5 us)
Async XLA Ops:
  6.5 356.1 %all-gather.3.cloned.1.call-start = ((), (), s32[]{:S(2)}) async-start(), calls=%async_computation | async-start | bytes 23592960 | tf_op jit(solution)/shard_map/all_gather | solution.py:47
  16.7 13.9 %copy-start.8 = (f32[32,512]{1,0:T(8,128)S(1)}, f32[32,512]{1,0:T(8,128)}, u32[]{:S(2)}) copy-start(f32[32,512]{1,0:T(8,128)} %param.5) | copy-start | bytes 196612
  16.7 20.7 %copy-start.7 = (bf16[128,1024]{1,0:T(8,128)(2,1)S(1)}, bf16[128,1024]{1,0:T(8,128)(2,1)}, u32[]{:S(2)}) copy-start(bf16[128,1024]{1,0:T(8,128)(2,1)} %param.4) | copy-start | bytes 786436
  19.6 68.9 %collective-permute-start.2 = (bf16[12,512,128]{2,1,0:T(8,128)(2,1)S(1)}, bf16[12,512,128]{2,1,0:T(8,128)(2,1)}, u32[]{:S(2)}, u32[]{:S(2)}) collective-permute-start(bf16[12,512,128]{2,1,0:T(8,128)(2,1)S(1)} %fusion.20), channel_id=1, source_target_pairs={{0,16},{16,32},{32,48},{48,64},{64,80},{80,96},{96,112},{1,17},{17... | collective-permute-start | bytes 4718600 | tf_op jit(solution)/shard_map/ppermute | solution.py:54
  24.1 132.6 %collective-permute-start.3 = (bf16[12,512,128]{2,1,0:T(8,128)(2,1)S(1)}, bf16[12,512,128]{2,1,0:T(8,128)(2,1)}, u32[]{:S(2)}, u32[]{:S(2)}) collective-permute-start(bf16[12,512,128]{2,1,0:T(8,128)(2,1)S(1)} %fusion.20), channel_id=1, source_target_pairs={{0,32},{16,48},{32,64},{48,80},{64,96},{80,112},{1,33},{17,49},{33... | collective-permute-start | bytes 4718600 | tf_op jit(solution)/shard_map/ppermute | solution.py:54
  27.6 135.4 %collective-permute-start.4 = (bf16[12,512,128]{2,1,0:T(8,128)(2,1)S(1)}, bf16[12,512,128]{2,1,0:T(8,128)(2,1)}, u32[]{:S(2)}, u32[]{:S(2)}) collective-permute-start(bf16[12,512,128]{2,1,0:T(8,128)(2,1)S(1)} %fusion.20), channel_id=1, source_target_pairs={{0,48},{16,64},{32,80},{48,96},{64,112},{1,49},{17,65},{33,81},{49... | collective-permute-start | bytes 4718600 | tf_op jit(solution)/shard_map/ppermute | solution.py:54
  30.7 11.1 %collective-permute-start = (f32[1,512]{1,0:T(1,128)S(1)}, f32[1,512]{1,0:T(1,128)S(1)}, u32[]{:S(2)}, u32[]{:S(2)}) collective-permute-start(f32[1,512]{1,0:T(1,128)S(1)} %get-tuple-element.17), channel_id=1, source_target_pairs={{0,1},{1,2},{2,3},{3,4},{4,5},{5,6},{6,7},{7,8},{8,9},{9,10},{10,1... | collective-permute-start | bytes 6152 | tf_op jit(solution)/shard_map/ppermute | solution.py:14
  32.6 10.5 %collective-permute-start.1 = (f32[1,512]{1,0:T(1,128)S(1)}, f32[1,512]{1,0:T(1,128)S(1)}, u32[]{:S(2)}, u32[]{:S(2)}) collective-permute-start(f32[1,512]{1,0:T(1,128)S(1)} %get-tuple-element.18), channel_id=1, source_target_pairs={{1,0},{2,1},{3,2},{4,3},{5,4},{6,5},{7,6},{8,7},{9,8},{10,9},{11,1... | collective-permute-start | bytes 6152 | tf_op jit(solution)/shard_map/ppermute | solution.py:15
  38.2 1.4 copy-start.6
  41.7 124.1 %collective-permute-start.5 = (bf16[12,512,128]{2,1,0:T(8,128)(2,1)S(1)}, bf16[12,512,128]{2,1,0:T(8,128)(2,1)S(1)}, u32[]{:S(2)}, u32[]{:S(2)}) collective-permute-start(bf16[12,512,128]{2,1,0:T(8,128)(2,1)S(1)} %fusion.20), channel_id=1, source_target_pairs={{0,64},{16,80},{32,96},{48,112},{1,65},{17,81},{33,97},{49,113},{2... | collective-permute-start | bytes 4718600 | tf_op jit(solution)/shard_map/ppermute | solution.py:54
  43.1 124.1 %collective-permute-start.6 = (bf16[12,512,128]{2,1,0:T(8,128)(2,1)S(1)}, bf16[12,512,128]{2,1,0:T(8,128)(2,1)S(1)}, u32[]{:S(2)}, u32[]{:S(2)}) collective-permute-start(bf16[12,512,128]{2,1,0:T(8,128)(2,1)S(1)} %fusion.20), channel_id=1, source_target_pairs={{0,80},{16,96},{32,112},{1,81},{17,97},{33,113},{2,82},{18,98},{34... | collective-permute-start | bytes 4718600 | tf_op jit(solution)/shard_map/ppermute | solution.py:54
  88.5 80.2 %collective-permute-start.7 = (bf16[12,512,128]{2,1,0:T(8,128)(2,1)S(1)}, bf16[12,512,128]{2,1,0:T(8,128)(2,1)S(1)}, u32[]{:S(2)}, u32[]{:S(2)}) collective-permute-start(bf16[12,512,128]{2,1,0:T(8,128)(2,1)S(1)} %fusion.20), channel_id=1, source_target_pairs={{0,96},{16,112},{1,97},{17,113},{2,98},{18,114},{3,99},{19,115},{4... | collective-permute-start | bytes 4718600 | tf_op jit(solution)/shard_map/ppermute | solution.py:54
  156.6 13.4 %collective-permute-start.8 = (bf16[12,512,128]{2,1,0:T(8,128)(2,1)S(1)}, bf16[12,512,128]{2,1,0:T(8,128)(2,1)S(1)}, u32[]{:S(2)}, u32[]{:S(2)}) collective-permute-start(bf16[12,512,128]{2,1,0:T(8,128)(2,1)S(1)} %fusion.20), channel_id=1, source_target_pairs={{0,112},{1,113},{2,114},{3,115},{4,116},{5,117},{6,118},{7,119},{8... | collective-permute-start | bytes 4718600 | tf_op jit(solution)/shard_map/ppermute | solution.py:54
  168.6 2.8 copy-start.5
  168.6 2.8 copy-start.11
  179.1 12.3 %collective-permute-start.10 = (f32[2,128,512]{1,2,0:T(8,128)}, f32[2,128,512]{1,2,0:T(8,128)}, u32[]{:S(2)}, u32[]{:S(2)}) collective-permute-start(f32[2,128,512]{1,2,0:T(8,128)} %get-tuple-element.8), channel_id=1, source_target_pairs={{1,0},{2,1},{3,2},{4,3},{5,4},{6,5},{7,6},{8,7},{9,8},{10,9},{11,1... | collective-permute-start | bytes 1572872 | tf_op jit(solution)/shard_map/ppermute | solution.py:15
  181.0 10.8 %collective-permute-start.9 = (f32[2,128,512]{1,2,0:T(8,128)}, f32[2,128,512]{1,2,0:T(8,128)}, u32[]{:S(2)}, u32[]{:S(2)}) collective-permute-start(f32[2,128,512]{1,2,0:T(8,128)} %get-tuple-element.7), channel_id=1, source_target_pairs={{0,1},{1,2},{2,3},{3,4},{4,5},{5,6},{6,7},{7,8},{8,9},{9,10},{10,1... | collective-permute-start | bytes 1572872 | tf_op jit(solution)/shard_map/ppermute | solution.py:14
  191.4 1.8 copy-start
  191.9 1.3 copy-start.13
  193.2 1.8 copy-start.10
  195.0 3.9 copy-start.1
  195.0 3.9 copy-start.12
  199.0 1.8 copy-start.9
  362.7 13.5 %copy-start.2 = (f32[4,128,512]{2,1,0:T(8,128)S(1)}, f32[4,128,512]{2,1,0:T(8,128)}, u32[]{:S(2)}) copy-start(f32[4,128,512]{2,1,0:T(8,128)} %copy.68) | copy-start | bytes 3145732
  362.7 13.5 %copy-start.3 = (f32[4,128,512]{2,1,0:T(8,128)S(1)}, f32[4,128,512]{2,1,0:T(8,128)}, u32[]{:S(2)}) copy-start(f32[4,128,512]{2,1,0:T(8,128)} %copy.69) | copy-start | bytes 3145732
  395.9 2.8 slice-start
  398.6 7.3 %copy-start.4 = (f32[4,128,512]{2,1,0:T(8,128)S(1)}, f32[4,128,512]{2,1,0:T(8,128)}, u32[]{:S(2)}) copy-start(f32[4,128,512]{2,1,0:T(8,128)} %copy.70) | copy-start | bytes 3145732
Sparse Core Ops, SparseCore 0:
  14.0 348.6 all-gather.2

commit v17 on v6

--- a/solution.py
+++ b/solution.py
@@ -44,7 +44,7 @@
     lower = jnp.where(global_cols <= global_rows, factor, jnp.zeros_like(factor))
     lower = lower.reshape(epochs, count, epochs)
     middle = jnp.transpose(field[:, EDGE:slab - EDGE], (1, 2, 0))
-    gathered = lax.all_gather(middle, "epoch", axis=0)
+    gathered = lax.all_gather(middle, "epoch", axis=2, tiled=True)
     edges = jnp.transpose(
         jnp.concatenate([field[:, :EDGE], field[:, slab - EDGE:]], axis=1), (1, 2, 0)
     )
@@ -71,7 +71,9 @@
         jnp.concatenate([bottom, below], axis=0),
         gain[slab - EDGE + 2:slab + 2], gain[slab - EDGE + 3:slab + 1], last_outside=pos == last,
     )
-    timed_middle = jnp.einsum("tes,eijs->itj", lower, gathered, preferred_element_type=jnp.float32)
+    timed_middle = jnp.einsum(
+        "tk,ijk->itj", lower.reshape(epochs, order), gathered, preferred_element_type=jnp.float32
+    )
     ext = jnp.concatenate([top[EDGE - 2 * HALO:], timed_middle, bottom[:2 * HALO]], axis=0)
     out_middle = double_stencil(ext, gain[EDGE - 2:slab - EDGE + 4], gain[EDGE - 1:slab - EDGE + 3])
     product = jnp.concatenate([out_top, out_middle, out_bottom], axis=0)

time: 404 us -> 420 us (1.040)
  waiting for transfers between devices: 262 us -> 276 us
    all_gather x1, waiting for transfers between devices: 104 us -> 132 us  [body(): gathered = lax.all_gather(middle, 'epoch', axis=2, tiled=True)]
    ppermute x7, waiting for transfers between devices: 154 us -> 140 us  [body(): slots.append(lax.ppermute(edges, 'epoch', pairs))]
  transfers between devices with their start and end apart: 12 -> 12, of which waited for: 5 -> 5; matrix products, arithmetic and copies ran while one was open for 15% -> 14% of each run, Pallas kernels for 0% -> 0%
where the time goes in v17:
time: 420 us; the launch traced here: 415 us
  waiting for transfers between devices  276 us (66%)
  local copies, waits for them, and re-layouts  49 us (12%)
  other arithmetic  28.7 us (7%)
  starting transfers between devices  26.5 us (6%)
  matrix products  21.8 us (5%)
  between operations  13.8 us (3%)
    ppermute x7, waiting for transfers between devices, body(): slots.append(lax.ppermute(edges, 'epoch', pairs))  140 us
    all_gather x1, waiting for transfers between devices, body(): gathered = lax.all_gather(middle, 'epoch', axis=2, tiled=True)  132 us
    unnamed x26, local copies, waits for them, and re-layouts  22.5 us
    ppermute x7, starting transfers between devices, body(): slots.append(lax.ppermute(edges, 'epoch', pairs))  16.1 us
    dot_general x1, matrix products, body(): jnp.einsum('tk,ijk->itj', lower.reshape(epochs, order), gathered, preferr...  13.5 us
  transfers between devices with their start and end apart: 12, of which 5 were waited for; matrix products, arithmetic and copies ran while one was open for 14% of the time, Pallas kernels for 0%

profile of v17, /device:TPU:62, one launch (start us, length us, event | category | flops | bytes accessed | tf_op | source)
XLA Modules:
  0.0 415.4 jit_solution(16540730485037769922)
XLA Ops:
  8.1 3.0 copy.57
  11.2 1.7 fusion.32
  16.4 4.5 %collective-permute-start.2 = (bf16[16,512,128]{2,1,0:T(8,128)(2,1)}, bf16[16,512,128]{2,1,0:T(8,128)(2,1)}, u32[]{:S(2)}, u32[]{:S(2)}) collective-permute-start(bf16[16,512,128]{2,1,0:T(8,128)(2,1)} %fusion.20), channel_id=1, source_target_pairs={{0,16},{16,32},{32,48},{48,64},{64,80},{80,96},{96,112},{1,17},{17... | collective-permute-start | bytes 6291464 | tf_op jit(solution)/shard_map/ppermute | solution.py:54
  20.9 3.5 collective-permute-start.3
  24.4 3.0 collective-permute-start.4
  27.4 2.7 collective-permute-start.5
  30.1 1.9 collective-permute-start
  35.0 3.2 collective-permute-start.1
  40.5 50.6 %collective-permute-done.2 = bf16[16,512,128]{2,1,0:T(8,128)(2,1)} collective-permute-done((bf16[16,512,128]{2,1,0:T(8,128)(2,1)}, bf16[16,512,128]{2,1,0:T(8,128)(2,1)}, u32[]{:S(2)}, u32[]{:S(2)}) %collective-permute-start.2) | collective-permute-done | bytes 2097184 | tf_op jit(solution)/shard_map/ppermute | solution.py:54
  91.9 89.8 %collective-permute-done.3 = bf16[16,512,128]{2,1,0:T(8,128)(2,1)} collective-permute-done((bf16[16,512,128]{2,1,0:T(8,128)(2,1)}, bf16[16,512,128]{2,1,0:T(8,128)(2,1)}, u32[]{:S(2)}, u32[]{:S(2)}) %collective-permute-start.3) | collective-permute-done | bytes 2097184 | tf_op jit(solution)/shard_map/ppermute | solution.py:54
  183.1 3.3 bitcast_dynamic-update-slice_fusion.5
  186.4 3.3 bitcast_dynamic-update-slice_fusion.4
  189.8 3.4 bitcast_dynamic-update-slice_fusion.3
  193.2 3.3 bitcast_dynamic-update-slice_fusion.2
  196.5 1.6 bitcast_dynamic-update-slice_fusion.1
  199.8 1.7 bitcast_dynamic-update-slice_fusion.7
  201.5 8.3 %convolution_bitcast_fusion.1 = f32[16,128,512]{1,2,0:T(8,128)S(1)} fusion(bf16[8,16,512,128]{3,2,0,1:T(8,128)(2,1)} %bitcast_dynamic-update-slice_fusion.7, bf16[8,128,128]{2,1,0:T(8,128)(2,1)S(1)} %gather_fusion, pred[8]{0:T(512)(128)(4,1)S(1)} %compare_and_fusion.1), kind=kOutput, calls=%fused_computation.20 | convolution fusion | flops 2147614720 | bytes 21233672 | tf_op jit(solution)/shard_map/tes,eijs->itj/dot_general | solution.py:58
  210.9 1.9 collective-permute-start.10
  212.9 3.4 collective-permute-start.9
  218.1 2.5 fusion.30
  220.6 3.1 collective-permute-done.9
  223.7 2.7 fusion.6
  226.4 2.0 fusion.15
  230.6 3.1 copy.49
  233.7 4.1 fusion.11
  240.2 131.6 %all-gather.2.cloned.1.call-done = bf16[16,512,1024]{2,1,0:T(8,128)(2,1)} async-done(((bf16[16,512,128]{2,1,0:T(8,128)(2,1)}), bf16[16,512,1024]{2,1,0:T(8,128)(2,1)}) %all-gather.2.cloned.1.call-update) | async-done | bytes 16777232 | tf_op jit(solution)/shard_map/all_gather | solution.py:47
  371.8 13.5 %convolution_bitcast_fusion = f32[16,128,512]{2,1,0:T(8,128)} fusion(bf16[16,512,1024]{2,1,0:T(8,128)(2,1)} %all-gather.2.cloned.1.call-done, bf16[128,1024]{0,1:T(8,128)(2,1)S(1)} %fusion.21), kind=kOutput, calls=%fused_computation.19 | convolution fusion | flops 2147483648 | bytes 21233664 | tf_op jit(solution)/shard_map/tk,ijk->itj/dot_general | solution.py:74
  385.3 2.9 pad_maximum_fusion
  389.2 4.3 %fusion.2 = f32[22,128,512]{2,1,0:T(8,128)S(1)} fusion(f32[22,128,512]{2,1,0:T(8,128)S(1)} %slice.205, f32[24,128,512]{2,1,0:T(8,128)S(1)} %pad_maximum_fusion, f32[22,512]{1,0:T(8,128)S(1)} %slice_bitcast_fusion), kind=kLoop, calls=%fused_computation.9 | loop fusion | flops 7208960 | bytes 23113728 | tf_op jit(solution)/shard_map/sub | solution.py:25
  394.2 3.9 fusion.5
  398.1 2.2 maximum_bitcast_fusion
  400.3 8.3 %copy.51 = f32[128,32,512]{2,1,0:T(8,128)} copy(f32[128,32,512]{2,0,1:T(8,128)S(1)} %maximum_bitcast_fusion) | data formatting | bytes 16777216 | tf_op jit(solution)/shard_map/transpose | solution.py:80
  (63 shorter events, 23.2 us)
Async XLA Ops:
  6.5 1.6 slice-start
  6.5 365.3 %all-gather.2.cloned.1.call-start = ((), (), s32[]{:S(2)}) async-start(), calls=%async_computation | async-start | bytes 18874368 | tf_op jit(solution)/shard_map/all_gather | solution.py:47
  14.9 15.3 %copy-start.4 = (f32[32,512]{1,0:T(8,128)S(1)}, f32[32,512]{1,0:T(8,128)}, u32[]{:S(2)}) copy-start(f32[32,512]{1,0:T(8,128)} %param.5) | copy-start | bytes 196612
  14.9 17.2 %copy-start.3 = (bf16[128,1024]{1,0:T(8,128)(2,1)S(1)}, bf16[128,1024]{1,0:T(8,128)(2,1)}, u32[]{:S(2)}) copy-start(bf16[128,1024]{1,0:T(8,128)(2,1)} %param.4) | copy-start | bytes 786436
  16.4 74.7 %collective-permute-start.2 = (bf16[16,512,128]{2,1,0:T(8,128)(2,1)}, bf16[16,512,128]{2,1,0:T(8,128)(2,1)}, u32[]{:S(2)}, u32[]{:S(2)}) collective-permute-start(bf16[16,512,128]{2,1,0:T(8,128)(2,1)} %fusion.20), channel_id=1, source_target_pairs={{0,16},{16,32},{32,48},{48,64},{64,80},{80,96},{96,112},{1,17},{17... | collective-permute-start | bytes 6291464 | tf_op jit(solution)/shard_map/ppermute | solution.py:54
  20.9 160.8 %collective-permute-start.3 = (bf16[16,512,128]{2,1,0:T(8,128)(2,1)}, bf16[16,512,128]{2,1,0:T(8,128)(2,1)}, u32[]{:S(2)}, u32[]{:S(2)}) collective-permute-start(bf16[16,512,128]{2,1,0:T(8,128)(2,1)} %fusion.20), channel_id=1, source_target_pairs={{0,32},{16,48},{32,64},{48,80},{64,96},{80,112},{1,33},{17,49},{33... | collective-permute-start | bytes 6291464 | tf_op jit(solution)/shard_map/ppermute | solution.py:54
  24.4 165.3 %collective-permute-start.4 = (bf16[16,512,128]{2,1,0:T(8,128)(2,1)}, bf16[16,512,128]{2,1,0:T(8,128)(2,1)}, u32[]{:S(2)}, u32[]{:S(2)}) collective-permute-start(bf16[16,512,128]{2,1,0:T(8,128)(2,1)} %fusion.20), channel_id=1, source_target_pairs={{0,48},{16,64},{32,80},{48,96},{64,112},{1,49},{17,65},{33,81},{49... | collective-permute-start | bytes 6291464 | tf_op jit(solution)/shard_map/ppermute | solution.py:54
  27.4 165.7 %collective-permute-start.5 = (bf16[16,512,128]{2,1,0:T(8,128)(2,1)}, bf16[16,512,128]{2,1,0:T(8,128)(2,1)}, u32[]{:S(2)}, u32[]{:S(2)}) collective-permute-start(bf16[16,512,128]{2,1,0:T(8,128)(2,1)} %fusion.20), channel_id=1, source_target_pairs={{0,64},{16,80},{32,96},{48,112},{1,65},{17,81},{33,97},{49,113},{2... | collective-permute-start | bytes 6291464 | tf_op jit(solution)/shard_map/ppermute | solution.py:54
  30.1 4.9 %collective-permute-start = (f32[1,512]{1,0:T(1,128)S(1)}, f32[1,512]{1,0:T(1,128)S(1)}, u32[]{:S(2)}, u32[]{:S(2)}) collective-permute-start(f32[1,512]{1,0:T(1,128)S(1)} %get-tuple-element.17), channel_id=1, source_target_pairs={{0,1},{1,2},{2,3},{3,4},{4,5},{5,6},{6,7},{7,8},{8,9},{9,10},{10,1... | collective-permute-start | bytes 6152 | tf_op jit(solution)/shard_map/ppermute | solution.py:14
  35.0 4.6 %collective-permute-start.1 = (f32[1,512]{1,0:T(1,128)S(1)}, f32[1,512]{1,0:T(1,128)S(1)}, u32[]{:S(2)}, u32[]{:S(2)}) collective-permute-start(f32[1,512]{1,0:T(1,128)S(1)} %get-tuple-element.18), channel_id=1, source_target_pairs={{1,0},{2,1},{3,2},{4,3},{5,4},{6,5},{7,6},{8,7},{9,8},{10,9},{11,1... | collective-permute-start | bytes 6152 | tf_op jit(solution)/shard_map/ppermute | solution.py:15
  39.6 156.9 %collective-permute-start.6 = (bf16[16,512,128]{2,1,0:T(8,128)(2,1)}, bf16[16,512,128]{2,1,0:T(8,128)(2,1)S(1)}, u32[]{:S(2)}, u32[]{:S(2)}) collective-permute-start(bf16[16,512,128]{2,1,0:T(8,128)(2,1)} %fusion.20), channel_id=1, source_target_pairs={{0,80},{16,96},{32,112},{1,81},{17,97},{33,113},{2,82},{18,98},{34... | collective-permute-start | bytes 6291464 | tf_op jit(solution)/shard_map/ppermute | solution.py:54
  91.1 107.1 %collective-permute-start.7 = (bf16[16,512,128]{2,1,0:T(8,128)(2,1)}, bf16[16,512,128]{2,1,0:T(8,128)(2,1)S(1)}, u32[]{:S(2)}, u32[]{:S(2)}) collective-permute-start(bf16[16,512,128]{2,1,0:T(8,128)(2,1)} %fusion.20), channel_id=1, source_target_pairs={{0,96},{16,112},{1,97},{17,113},{2,98},{18,114},{3,99},{19,115},{4... | collective-permute-start | bytes 6291464 | tf_op jit(solution)/shard_map/ppermute | solution.py:54
  181.7 18.1 %collective-permute-start.8 = (bf16[16,512,128]{2,1,0:T(8,128)(2,1)}, bf16[16,512,128]{2,1,0:T(8,128)(2,1)S(1)}, u32[]{:S(2)}, u32[]{:S(2)}) collective-permute-start(bf16[16,512,128]{2,1,0:T(8,128)(2,1)} %fusion.20), channel_id=1, source_target_pairs={{0,112},{1,113},{2,114},{3,115},{4,116},{5,117},{6,118},{7,119},{8... | collective-permute-start | bytes 6291464 | tf_op jit(solution)/shard_map/ppermute | solution.py:54
  209.8 6.6 %copy-start = (f32[16,128,512]{1,2,0:T(8,128)}, f32[16,128,512]{1,2,0:T(8,128)S(1)}, u32[]{:S(2)}) copy-start(f32[16,128,512]{1,2,0:T(8,128)S(1)} %convolution_bitcast_fusion.1) | copy-start | bytes 12582916
  210.9 9.6 %collective-permute-start.10 = (f32[2,128,512]{1,2,0:T(8,128)}, f32[2,128,512]{1,2,0:T(8,128)}, u32[]{:S(2)}, u32[]{:S(2)}) collective-permute-start(f32[2,128,512]{1,2,0:T(8,128)} %get-tuple-element.6), channel_id=1, source_target_pairs={{1,0},{2,1},{3,2},{4,3},{5,4},{6,5},{7,6},{8,7},{9,8},{10,9},{11,1... | collective-permute-start | bytes 1572872 | tf_op jit(solution)/shard_map/ppermute | solution.py:15
  212.9 10.8 %collective-permute-start.9 = (f32[2,128,512]{1,2,0:T(8,128)}, f32[2,128,512]{1,2,0:T(8,128)}, u32[]{:S(2)}, u32[]{:S(2)}) collective-permute-start(f32[2,128,512]{1,2,0:T(8,128)} %get-tuple-element.5), channel_id=1, source_target_pairs={{0,1},{1,2},{2,3},{3,4},{4,5},{5,6},{6,7},{7,8},{8,9},{9,10},{10,1... | collective-permute-start | bytes 1572872 | tf_op jit(solution)/shard_map/ppermute | solution.py:14
  223.7 2.7 copy-start.7
  228.4 0.7 copy-start.5
  230.6 3.1 copy-start.6
  240.2 145.1 %copy-start.2 = (f32[4,128,512]{2,1,0:T(8,128)S(1)}, f32[4,128,512]{2,1,0:T(8,128)}, u32[]{:S(2)}) copy-start(f32[4,128,512]{2,1,0:T(8,128)} %copy.48) | copy-start | bytes 3145732
  394.2 3.9 copy-start.1
Sparse Core Ops, SparseCore 0:
  11.3 360.4 all-gather.1

commit v18 on v16

--- a/solution.py
+++ b/solution.py
@@ -3,7 +3,7 @@
 from jax import lax
 from jax.sharding import PartitionSpec as P
 
-EDGE = 6
+EDGE = 9
 HALO = 2
 
 

time: 427 us -> 406 us (0.951)
  waiting for transfers between devices: 273 us -> 261 us
  other arithmetic: 34.1 us -> 25.8 us
    all_gather x1, waiting for transfers between devices: 161 us -> 97.7 us  [body(): gathered = lax.all_gather(middle, 'epoch', axis=0)]
    ppermute x7, waiting for transfers between devices: 111 us -> 160 us  [body(): slots.append(lax.ppermute(edges, 'epoch', pairs))]
    sub x1, other arithmetic: 12.9 us -> 3.99 us  [double_stencil(): once = gain_once * ext[1:-1] - (ext[:-2] + ext[2:] + side_sum(ext[1:-1]))]
    unnamed x38 -> x32, local copies, waits for them, and re-layouts: 19.4 us -> 26.6 us
  transfers between devices with their start and end apart: 12 -> 12, of which waited for: 4 -> 5; matrix products, arithmetic and copies ran while one was open for 12% -> 17% of each run, Pallas kernels for 0% -> 0%
where the time goes in v18:
time: 406 us; the launch traced here: 405 us
  waiting for transfers between devices  261 us (64%)
  local copies, waits for them, and re-layouts  58.1 us (14%)
  starting transfers between devices  26.7 us (7%)
  other arithmetic  25.8 us (6%)
  matrix products  19.4 us (5%)
  between operations  13.8 us (3%)
    ppermute x7, waiting for transfers between devices, body(): slots.append(lax.ppermute(edges, 'epoch', pairs))  160 us
    all_gather x1, waiting for transfers between devices, body(): gathered = lax.all_gather(middle, 'epoch', axis=0)  97.7 us
    unnamed x32, local copies, waits for them, and re-layouts  26.6 us
    ppermute x7, starting transfers between devices, body(): slots.append(lax.ppermute(edges, 'epoch', pairs))  16.2 us
    dot_general x1, matrix products, body(): jnp.einsum('tes,eijs->itj', lower, gathered, preferred_element_type=jnp.f...  10.1 us
    dot_general x1, matrix products, body(): jnp.einsum('tes,eijs->itj', weights, stacked, preferred_element_type=jnp....  9.3 us
    transpose x1, local copies, waits for them, and re-layouts, body(): return jnp.transpose(product, (1, 0, 2))  8.25 us
  transfers between devices with their start and end apart: 12, of which 5 were waited for; matrix products, arithmetic and copies ran while one was open for 17% of the time, Pallas kernels for 0%

profile of v18, /device:TPU:62, one launch (start us, length us, event | category | flops | bytes accessed | tf_op | source)
XLA Modules:
  0.0 405.1 jit_solution(12850516257064140035)
XLA Ops:
  6.5 3.0 slice.165
  9.6 3.0 copy.79
  12.6 4.6 %fusion.31 = (bf16[128,9,512]{2,1,0:T(8,128)(2,1)S(1)}, bf16[128,9,512]{2,1,0:T(8,128)(2,1)}) fusion(bf16[128,32,512]{2,1,0:T(8,128)(2,1)} %param.3), kind=kLoop, calls=%fused_computation.74 | loop fusion | bytes 4718592 | tf_op jit(solution)/shard_map/slice | solution.py:49
  18.9 3.1 copy.78
  23.6 4.5 %collective-permute-start.2 = (bf16[18,512,128]{2,1,0:T(8,128)(2,1)}, bf16[18,512,128]{2,1,0:T(8,128)(2,1)}, u32[]{:S(2)}, u32[]{:S(2)}) collective-permute-start(bf16[18,512,128]{2,1,0:T(8,128)(2,1)} %fusion.20), channel_id=1, source_target_pairs={{0,16},{16,32},{32,48},{48,64},{64,80},{80,96},{96,112},{1,17},{17... | collective-permute-start | bytes 7077896 | tf_op jit(solution)/shard_map/ppermute | solution.py:54
  28.1 3.5 collective-permute-start.3
  31.7 3.0 collective-permute-start.4
  34.7 2.7 collective-permute-start.5
  37.4 1.9 collective-permute-start
  42.3 3.3 collective-permute-start.1
  48.5 50.6 %collective-permute-done.2 = bf16[18,512,128]{2,1,0:T(8,128)(2,1)} collective-permute-done((bf16[18,512,128]{2,1,0:T(8,128)(2,1)}, bf16[18,512,128]{2,1,0:T(8,128)(2,1)}, u32[]{:S(2)}, u32[]{:S(2)}) %collective-permute-start.2) | collective-permute-done | bytes 2359328 | tf_op jit(solution)/shard_map/ppermute | solution.py:54
  100.0 109.7 %collective-permute-done.3 = bf16[18,512,128]{2,1,0:T(8,128)(2,1)} collective-permute-done((bf16[18,512,128]{2,1,0:T(8,128)(2,1)}, bf16[18,512,128]{2,1,0:T(8,128)(2,1)}, u32[]{:S(2)}, u32[]{:S(2)}) %collective-permute-start.3) | collective-permute-done | bytes 2359328 | tf_op jit(solution)/shard_map/ppermute | solution.py:54
  211.1 3.6 bitcast_dynamic-update-slice_fusion.5
  214.6 3.6 bitcast_dynamic-update-slice_fusion.4
  218.2 3.6 bitcast_dynamic-update-slice_fusion.3
  221.9 3.6 bitcast_dynamic-update-slice_fusion.2
  227.3 1.9 bitcast_dynamic-update-slice_fusion
  229.1 1.8 bitcast_dynamic-update-slice_fusion.7
  230.9 9.3 %convolution_bitcast_fusion = f32[18,128,512]{1,2,0:T(8,128)S(1)} fusion(bf16[8,18,512,128]{3,2,0,1:T(8,128)(2,1)} %bitcast_dynamic-update-slice_fusion.7, bf16[8,128,128]{2,1,0:T(8,128)(2,1)S(1)} %gather_fusion, pred[8]{0:T(512)(128)(4,1)S(1)} %compare_and_fusion.1), kind=kOutput, calls=%fused_computation.40 | convolution fusion | flops 2416050176 | bytes 23855112 | tf_op jit(solution)/shard_map/tes,eijs->itj/dot_general | solution.py:58
  241.5 1.9 collective-permute-start.10
  243.4 3.4 collective-permute-start.9
  248.5 2.7 fusion.29
  251.2 2.9 collective-permute-done.9
  254.2 2.7 fusion.6
  256.9 2.1 fusion.15
  261.5 2.8 copy.70
  264.3 4.1 %fusion.11 = f32[9,128,512]{1,2,0:T(8,128)S(1)} fusion(f32[9,128,512]{1,2,0:T(8,128)S(1)} %get-tuple-element.8, f32[2,128,512]{1,2,0:T(8,128)} %collective-permute-done.10, f32[9,128,512]{1,2,0:T(8,128)} %get-tuple-element.19, f32[9,512]{1,0:T(8,128)S(1)} %get-tuple-element.16, pred[9]{0:T(512)(128)(4,1)} %compare_and_fusion), kind=kLoop, calls=%fused_computation.25 | loop fusion | flops 4128768 | bytes 7620617 | tf_op jit(solution)/shard_map/jit(_where)/select_n | solution.py:33
  271.1 97.7 %all-gather.3.cloned.1.call-done = bf16[112,512,128]{2,1,0:T(8,128)(2,1)} async-done(((bf16[14,512,128]{2,1,0:T(8,128)(2,1)}), bf16[112,512,128]{2,1,0:T(8,128)(2,1)}) %all-gather.3.cloned.1.call-update) | async-done | bytes 14680080 | tf_op jit(solution)/shard_map/all_gather | solution.py:47
  368.7 10.1 %convolution_bitcast_fusion.1 = f32[14,128,512]{2,1,0:T(8,128)S(1)} fusion(bf16[128,8,128,1]{0,2,3,1:T(8,128)(2,1)S(1)} %bitcast.82, bf16[8,14,512,128]{3,2,1,0:T(8,128)(2,1)} %bitcast.79), kind=kOutput, calls=%fused_computation.41 | convolution fusion | flops 1879048192 | bytes 18612224 | tf_op jit(solution)/shard_map/tes,eijs->itj/dot_general | solution.py:74
  380.3 4.0 fusion.2
  385.0 3.3 fusion.5
  390.0 8.3 %copy.72 = f32[128,32,512]{2,1,0:T(8,128)} copy(f32[128,32,512]{2,0,1:T(8,128)S(1)} %maximum_bitcast_fusion) | data formatting | bytes 16777216 | tf_op jit(solution)/shard_map/transpose | solution.py:78
  (68 shorter events, 24.9 us)
Async XLA Ops:
  6.5 362.2 %all-gather.3.cloned.1.call-start = ((), (), s32[]{:S(2)}) async-start(), calls=%async_computation | async-start | bytes 16515072 | tf_op jit(solution)/shard_map/all_gather | solution.py:47
  22.0 15.4 %copy-start.8 = (f32[32,512]{1,0:T(8,128)S(1)}, f32[32,512]{1,0:T(8,128)}, u32[]{:S(2)}) copy-start(f32[32,512]{1,0:T(8,128)} %param.5) | copy-start | bytes 196612
  22.0 17.3 %copy-start.6 = (bf16[128,1024]{1,0:T(8,128)(2,1)S(1)}, bf16[128,1024]{1,0:T(8,128)(2,1)}, u32[]{:S(2)}) copy-start(bf16[128,1024]{1,0:T(8,128)(2,1)} %param.4) | copy-start | bytes 786436
  23.6 75.5 %collective-permute-start.2 = (bf16[18,512,128]{2,1,0:T(8,128)(2,1)}, bf16[18,512,128]{2,1,0:T(8,128)(2,1)}, u32[]{:S(2)}, u32[]{:S(2)}) collective-permute-start(bf16[18,512,128]{2,1,0:T(8,128)(2,1)} %fusion.20), channel_id=1, source_target_pairs={{0,16},{16,32},{32,48},{48,64},{64,80},{80,96},{96,112},{1,17},{17... | collective-permute-start | bytes 7077896 | tf_op jit(solution)/shard_map/ppermute | solution.py:54
  28.1 181.5 %collective-permute-start.3 = (bf16[18,512,128]{2,1,0:T(8,128)(2,1)}, bf16[18,512,128]{2,1,0:T(8,128)(2,1)}, u32[]{:S(2)}, u32[]{:S(2)}) collective-permute-start(bf16[18,512,128]{2,1,0:T(8,128)(2,1)} %fusion.20), channel_id=1, source_target_pairs={{0,32},{16,48},{32,64},{48,80},{64,96},{80,112},{1,33},{17,49},{33... | collective-permute-start | bytes 7077896 | tf_op jit(solution)/shard_map/ppermute | solution.py:54
  31.7 186.6 %collective-permute-start.4 = (bf16[18,512,128]{2,1,0:T(8,128)(2,1)}, bf16[18,512,128]{2,1,0:T(8,128)(2,1)}, u32[]{:S(2)}, u32[]{:S(2)}) collective-permute-start(bf16[18,512,128]{2,1,0:T(8,128)(2,1)} %fusion.20), channel_id=1, source_target_pairs={{0,48},{16,64},{32,80},{48,96},{64,112},{1,49},{17,65},{33,81},{49... | collective-permute-start | bytes 7077896 | tf_op jit(solution)/shard_map/ppermute | solution.py:54
  34.7 187.2 %collective-permute-start.5 = (bf16[18,512,128]{2,1,0:T(8,128)(2,1)}, bf16[18,512,128]{2,1,0:T(8,128)(2,1)}, u32[]{:S(2)}, u32[]{:S(2)}) collective-permute-start(bf16[18,512,128]{2,1,0:T(8,128)(2,1)} %fusion.20), channel_id=1, source_target_pairs={{0,64},{16,80},{32,96},{48,112},{1,65},{17,81},{33,97},{49,113},{2... | collective-permute-start | bytes 7077896 | tf_op jit(solution)/shard_map/ppermute | solution.py:54
  37.4 4.9 %collective-permute-start = (f32[1,512]{1,0:T(1,128)S(1)}, f32[1,512]{1,0:T(1,128)S(1)}, u32[]{:S(2)}, u32[]{:S(2)}) collective-permute-start(f32[1,512]{1,0:T(1,128)S(1)} %get-tuple-element.17), channel_id=1, source_target_pairs={{0,1},{1,2},{2,3},{3,4},{4,5},{5,6},{6,7},{7,8},{8,9},{9,10},{10,1... | collective-permute-start | bytes 6152 | tf_op jit(solution)/shard_map/ppermute | solution.py:14
  41.4 173.2 %copy-start.4 = (bf16[128,1024]{0,1:T(8,128)(2,1)}, bf16[128,1024]{0,1:T(8,128)(2,1)S(1)}, u32[]{:S(2)}) copy-start(bf16[128,1024]{0,1:T(8,128)(2,1)S(1)} %fusion.21) | copy-start | bytes 786436
  42.3 4.7 %collective-permute-start.1 = (f32[1,512]{1,0:T(1,128)S(1)}, f32[1,512]{1,0:T(1,128)S(1)}, u32[]{:S(2)}, u32[]{:S(2)}) collective-permute-start(f32[1,512]{1,0:T(1,128)S(1)} %get-tuple-element.18), channel_id=1, source_target_pairs={{1,0},{2,1},{3,2},{4,3},{5,4},{6,5},{7,6},{8,7},{9,8},{10,9},{11,1... | collective-permute-start | bytes 6152 | tf_op jit(solution)/shard_map/ppermute | solution.py:15
  47.0 178.4 %collective-permute-start.6 = (bf16[18,512,128]{2,1,0:T(8,128)(2,1)}, bf16[18,512,128]{2,1,0:T(8,128)(2,1)S(1)}, u32[]{:S(2)}, u32[]{:S(2)}) collective-permute-start(bf16[18,512,128]{2,1,0:T(8,128)(2,1)} %fusion.20), channel_id=1, source_target_pairs={{0,80},{16,96},{32,112},{1,81},{17,97},{33,113},{2,82},{18,98},{34... | collective-permute-start | bytes 7077896 | tf_op jit(solution)/shard_map/ppermute | solution.py:54
  99.1 128.1 %collective-permute-start.7 = (bf16[18,512,128]{2,1,0:T(8,128)(2,1)}, bf16[18,512,128]{2,1,0:T(8,128)(2,1)S(1)}, u32[]{:S(2)}, u32[]{:S(2)}) collective-permute-start(bf16[18,512,128]{2,1,0:T(8,128)(2,1)} %fusion.20), channel_id=1, source_target_pairs={{0,96},{16,112},{1,97},{17,113},{2,98},{18,114},{3,99},{19,115},{4... | collective-permute-start | bytes 7077896 | tf_op jit(solution)/shard_map/ppermute | solution.py:54
  209.6 19.5 %collective-permute-start.8 = (bf16[18,512,128]{2,1,0:T(8,128)(2,1)}, bf16[18,512,128]{2,1,0:T(8,128)(2,1)S(1)}, u32[]{:S(2)}, u32[]{:S(2)}) collective-permute-start(bf16[18,512,128]{2,1,0:T(8,128)(2,1)} %fusion.20), channel_id=1, source_target_pairs={{0,112},{1,113},{2,114},{3,115},{4,116},{5,117},{6,118},{7,119},{8... | collective-permute-start | bytes 7077896 | tf_op jit(solution)/shard_map/ppermute | solution.py:54
  240.2 6.6 %copy-start = (f32[18,128,512]{1,2,0:T(8,128)}, f32[18,128,512]{1,2,0:T(8,128)S(1)}, u32[]{:S(2)}) copy-start(f32[18,128,512]{1,2,0:T(8,128)S(1)} %convolution_bitcast_fusion) | copy-start | bytes 14155780
  241.5 9.8 %collective-permute-start.10 = (f32[2,128,512]{1,2,0:T(8,128)}, f32[2,128,512]{1,2,0:T(8,128)}, u32[]{:S(2)}, u32[]{:S(2)}) collective-permute-start(f32[2,128,512]{1,2,0:T(8,128)} %get-tuple-element.6), channel_id=1, source_target_pairs={{1,0},{2,1},{3,2},{4,3},{5,4},{6,5},{7,6},{8,7},{9,8},{10,9},{11,1... | collective-permute-start | bytes 1572872 | tf_op jit(solution)/shard_map/ppermute | solution.py:15
  243.4 10.8 %collective-permute-start.9 = (f32[2,128,512]{1,2,0:T(8,128)}, f32[2,128,512]{1,2,0:T(8,128)}, u32[]{:S(2)}, u32[]{:S(2)}) collective-permute-start(f32[2,128,512]{1,2,0:T(8,128)} %get-tuple-element.5), channel_id=1, source_target_pairs={{0,1},{1,2},{2,3},{3,4},{4,5},{5,6},{6,7},{7,8},{8,9},{9,10},{10,1... | collective-permute-start | bytes 1572872 | tf_op jit(solution)/shard_map/ppermute | solution.py:14
  254.2 2.8 copy-start.7
  254.2 2.8 copy-start.10
  259.1 0.7 copy-start.9
  269.4 99.4 %copy-start.5 = (bf16[128,1024]{0,1:T(8,128)(2,1)S(1)}, bf16[128,1024]{0,1:T(8,128)(2,1)}, u32[]{:S(2)}) copy-start(bf16[128,1024]{0,1:T(8,128)(2,1)} %copy-done.4) | copy-start | bytes 786436
  368.7 10.1 %copy-start.3 = (f32[4,128,512]{2,1,0:T(8,128)S(1)}, f32[4,128,512]{2,1,0:T(8,128)}, u32[]{:S(2)}) copy-start(f32[4,128,512]{2,1,0:T(8,128)} %copy.69) | copy-start | bytes 3145732
  384.9 3.3 copy-start.1
  385.0 3.3 copy-start.2
Sparse Core Ops, SparseCore 0:
  12.8 355.9 all-gather.2

commit v19 on v6

--- a/solution.py
+++ b/solution.py
@@ -72,7 +72,10 @@
         gain[slab - EDGE + 2:slab + 2], gain[slab - EDGE + 3:slab + 1], last_outside=pos == last,
     )
     timed_middle = jnp.einsum("tes,eijs->itj", lower, gathered, preferred_element_type=jnp.float32)
-    ext = jnp.concatenate([top[EDGE - 2 * HALO:], timed_middle, bottom[:2 * HALO]], axis=0)
+    frame = jnp.concatenate(
+        [top[EDGE - 2 * HALO:], jnp.zeros_like(timed_middle), bottom[:2 * HALO]], axis=0
+    )
+    ext = lax.dynamic_update_slice_in_dim(frame, timed_middle, 2 * HALO, 0)
     out_middle = double_stencil(ext, gain[EDGE - 2:slab - EDGE + 4], gain[EDGE - 1:slab - EDGE + 3])
     product = jnp.concatenate([out_top, out_middle, out_bottom], axis=0)
     return jnp.transpose(product, (1, 0, 2))

time: 404 us -> 441 us (1.092)
  local copies, waits for them, and re-layouts: 49 us -> 79.3 us
  other arithmetic: 28.7 us -> 44 us
  waiting for transfers between devices: 262 us -> 253 us
    dynamic_update_slice x0 -> x1, local copies, waits for them, and re-layouts: none -> 21.3 us  [body(): ext = lax.dynamic_update_slice_in_dim(frame, timed_middle, 2 * HALO, 0)]
    sub x1, other arithmetic: 4.29 us -> 10.7 us  [double_stencil(): once = gain_once * ext[1:-1] - (ext[:-2] + ext[2:] + side_sum(ext[1:-1]))]
    slice x1, local copies, waits for them, and re-layouts: 0.98 us -> 6.98 us  [double_stencil(): once = gain_once * ext[1:-1] - (ext[:-2] + ext[2:] + side_sum(ext[1:-1]))]
    all_gather x1, waiting for transfers between devices: 104 us -> 98.8 us  [body(): gathered = lax.all_gather(middle, 'epoch', axis=0)]
  transfers between devices with their start and end apart: 12 -> 12, of which waited for: 5 -> 4; matrix products, arithmetic and copies ran while one was open for 15% -> 16% of each run, Pallas kernels for 0% -> 0%
where the time goes in v19:
time: 441 us; the launch traced here: 440 us
  waiting for transfers between devices  253 us (57%)
  local copies, waits for them, and re-layouts  79.3 us (18%)
  other arithmetic  44 us (10%)
  starting transfers between devices  26.3 us (6%)
  matrix products  23.6 us (5%)
  between operations  13.7 us (3%)
    ppermute x7, waiting for transfers between devices, body(): slots.append(lax.ppermute(edges, 'epoch', pairs))  153 us
    all_gather x1, waiting for transfers between devices, body(): gathered = lax.all_gather(middle, 'epoch', axis=0)  98.8 us
    unnamed x26, local copies, waits for them, and re-layouts  22.4 us
    dynamic_update_slice x1, local copies, waits for them, and re-layouts, body(): ext = lax.dynamic_update_slice_in_dim(frame, timed_middle, 2 * HALO, 0)  21.3 us
    ppermute x7, starting transfers between devices, body(): slots.append(lax.ppermute(edges, 'epoch', pairs))  16.1 us
    dot_general x1, matrix products, body(): jnp.einsum('tes,eijs->itj', lower, gathered, preferred_element_type=jnp.f...  13.3 us
    sub x1, other arithmetic, double_stencil(): once = gain_once * ext[1:-1] - (ext[:-2] + ext[2:] + side_sum(ext[1:-1]))  10.7 us
    dot_general x1, matrix products, body(): jnp.einsum('tes,eijs->itj', weights, stacked, preferred_element_type=jnp....  10.4 us
  transfers between devices with their start and end apart: 12, of which 4 were waited for; matrix products, arithmetic and copies ran while one was open for 16% of the time, Pallas kernels for 0%

profile of v19, /device:TPU:62, one launch (start us, length us, event | category | flops | bytes accessed | tf_op | source)
XLA Modules:
  0.0 439.7 jit_solution(14363977838037120884)
XLA Ops:
  8.1 3.0 copy.79
  16.4 4.5 %collective-permute-start.2 = (bf16[16,512,128]{2,1,0:T(8,128)(2,1)}, bf16[16,512,128]{2,1,0:T(8,128)(2,1)}, u32[]{:S(2)}, u32[]{:S(2)}) collective-permute-start(bf16[16,512,128]{2,1,0:T(8,128)(2,1)} %fusion.20), channel_id=1, source_target_pairs={{0,16},{16,32},{32,48},{48,64},{64,80},{80,96},{96,112},{1,17},{17... | collective-permute-start | bytes 6291464 | tf_op jit(solution)/shard_map/ppermute | solution.py:54
  20.9 3.5 collective-permute-start.3
  24.4 3.0 collective-permute-start.4
  27.4 2.7 collective-permute-start.5
  30.1 1.9 collective-permute-start
  35.0 3.2 collective-permute-start.1
  41.0 50.1 %collective-permute-done.2 = bf16[16,512,128]{2,1,0:T(8,128)(2,1)} collective-permute-done((bf16[16,512,128]{2,1,0:T(8,128)(2,1)}, bf16[16,512,128]{2,1,0:T(8,128)(2,1)}, u32[]{:S(2)}, u32[]{:S(2)}) %collective-permute-start.2) | collective-permute-done | bytes 2097184 | tf_op jit(solution)/shard_map/ppermute | solution.py:54
  91.9 103.3 %collective-permute-done.3 = bf16[16,512,128]{2,1,0:T(8,128)(2,1)} collective-permute-done((bf16[16,512,128]{2,1,0:T(8,128)(2,1)}, bf16[16,512,128]{2,1,0:T(8,128)(2,1)}, u32[]{:S(2)}, u32[]{:S(2)}) %collective-permute-start.3) | collective-permute-done | bytes 2097184 | tf_op jit(solution)/shard_map/ppermute | solution.py:54
  196.6 3.3 bitcast_dynamic-update-slice_fusion.5
  200.0 3.3 bitcast_dynamic-update-slice_fusion.4
  203.3 3.4 bitcast_dynamic-update-slice_fusion.3
  206.7 3.3 bitcast_dynamic-update-slice_fusion.2
  215.0 10.4 %convolution_bitcast_fusion.1 = f32[16,128,512]{1,2,0:T(8,128)S(1)} fusion(bf16[8,16,512,128]{3,2,0,1:T(8,128)(2,1)} %bitcast_dynamic-update-slice_fusion.7, bf16[8,128,128]{2,1,0:T(8,128)(2,1)S(1)} %gather_fusion, pred[8]{0:T(512)(128)(4,1)S(1)} %compare_and_fusion.1), kind=kOutput, calls=%fused_computation.20 | convolution fusion | flops 2147614720 | bytes 21233672 | tf_op jit(solution)/shard_map/tes,eijs->itj/dot_general | solution.py:58
  226.4 1.9 collective-permute-start.10
  228.3 3.2 collective-permute-start.9
  234.7 1.7 copy.65
  236.4 2.6 copy.66
  239.0 5.0 %pad_maximum_fusion = f32[24,128,512]{2,0,1:T(8,128)} fusion(f32[4,128,512]{2,0,1:T(4,128)} %copy.66, f32[4,128,512]{2,0,1:T(4,128)S(1)} %copy.65, f32[24]{0:T(128)} %pad.34.clone), kind=kLoop, calls=%fused_computation.14 | loop fusion | flops 3145728 | bytes 8388704 | tf_op jit(solution)/shard_map/concatenate | solution.py:75
  244.1 2.7 fusion.6
  246.8 2.0 fusion.15
  251.1 3.0 copy.71
  254.1 4.2 fusion.11
  259.1 2.0 copy.72
  261.0 98.8 %all-gather.3.cloned.1.call-done = bf16[128,512,128]{2,1,0:T(8,128)(2,1)} async-done(((bf16[16,512,128]{2,1,0:T(8,128)(2,1)}), bf16[128,512,128]{2,1,0:T(8,128)(2,1)}) %all-gather.3.cloned.1.call-update) | async-done | bytes 16777232 | tf_op jit(solution)/shard_map/all_gather | solution.py:47
  359.8 13.3 %convolution_bitcast_fusion = f32[16,128,512]{2,1,0:T(8,128)} fusion(bf16[128,8,128,1]{0,2,3,1:T(8,128)(2,1)S(1)} %bitcast.82, bf16[8,16,512,128]{3,2,1,0:T(8,128)(2,1)} %bitcast.79), kind=kOutput, calls=%fused_computation.19 | convolution fusion | flops 2147483648 | bytes 21233664 | tf_op jit(solution)/shard_map/tes,eijs->itj/dot_general | solution.py:74
  373.1 6.6 %copy.70 = f32[16,128,512]{2,0,1:T(8,128)} copy(f32[16,128,512]{2,1,0:T(8,128)} %convolution_bitcast_fusion) | data formatting | bytes 8388608 | tf_op jit(solution)/shard_map/tes,eijs->itj/transpose | solution.py:74
  379.7 21.3 %dynamic_update_slice.3 = f32[24,128,512]{2,0,1:T(8,128)} dynamic-update-slice(f32[24,128,512]{2,0,1:T(8,128)} %pad_maximum_fusion, f32[16,128,512]{2,0,1:T(8,128)} %copy.70, s32[]{:T(128)} %constant.41.clone.1, s32[]{:T(128)} %constant.14.clone.1, s32[]{:T(128)} %constant.14.clone.1) | dynamic-update-slice | bytes 8388612 | tf_op jit(solution)/shard_map/dynamic_update_slice | solution.py:78
  401.0 7.0 %slice.205 = f32[22,128,512]{2,0,1:T(8,128)} slice(f32[24,128,512]{2,0,1:T(8,128)} %dynamic_update_slice.3), slice={[1:23], [0:128], [0:512]} | slice | bytes 11534336 | tf_op jit(solution)/shard_map/slice | solution.py:25
  407.9 10.7 %fusion.2 = f32[22,128,512]{2,0,1:T(8,128)S(1)} fusion(f32[22,128,512]{2,0,1:T(8,128)} %slice.205, f32[24,128,512]{2,0,1:T(8,128)S(1)} %copy-done, f32[22,512]{1,0:T(8,128)S(1)} %slice_bitcast_fusion), kind=kLoop, calls=%fused_computation.8 | loop fusion | flops 7208960 | bytes 23113728 | tf_op jit(solution)/shard_map/sub | solution.py:25
  420.0 6.4 %fusion.5 = f32[20,128,512]{2,0,1:T(8,128)} fusion(f32[20,128,512]{2,0,1:T(8,128)S(1)} %slice.208, f32[22,128,512]{2,0,1:T(8,128)S(1)} %fusion.2, f32[20,512]{1,0:T(8,128)S(1)} %slice_bitcast_fusion.1), kind=kLoop, calls=%fused_computation.11 | loop fusion | flops 6553600 | bytes 21012480 | tf_op jit(solution)/shard_map/sub | solution.py:34
  426.4 6.4 %maximum_bitcast_fusion = f32[128,32,512]{2,1,0:T(8,128)} fusion(f32[6,128,512]{2,0,1:T(8,128)} %copy.72, f32[20,128,512]{2,0,1:T(8,128)} %fusion.5, f32[6,128,512]{2,0,1:T(8,128)S(1)} %copy-done.2), kind=kLoop, calls=%fused_computation.1 | loop fusion | flops 4194304 | bytes 16777216 | tf_op jit(solution)/shard_map/transpose | solution.py:81
  (66 shorter events, 28.2 us)
Async XLA Ops:
  6.5 1.6 slice-start
  6.5 353.3 %all-gather.3.cloned.1.call-start = ((), (), s32[]{:S(2)}) async-start(), calls=%async_computation | async-start | bytes 18874368 | tf_op jit(solution)/shard_map/all_gather | solution.py:47
  14.9 15.3 %copy-start.4 = (f32[32,512]{1,0:T(8,128)S(1)}, f32[32,512]{1,0:T(8,128)}, u32[]{:S(2)}) copy-start(f32[32,512]{1,0:T(8,128)} %param.5) | copy-start | bytes 196612
  14.9 17.2 %copy-start.3 = (bf16[128,1024]{1,0:T(8,128)(2,1)S(1)}, bf16[128,1024]{1,0:T(8,128)(2,1)}, u32[]{:S(2)}) copy-start(bf16[128,1024]{1,0:T(8,128)(2,1)} %param.4) | copy-start | bytes 786436
  16.4 74.7 %collective-permute-start.2 = (bf16[16,512,128]{2,1,0:T(8,128)(2,1)}, bf16[16,512,128]{2,1,0:T(8,128)(2,1)}, u32[]{:S(2)}, u32[]{:S(2)}) collective-permute-start(bf16[16,512,128]{2,1,0:T(8,128)(2,1)} %fusion.20), channel_id=1, source_target_pairs={{0,16},{16,32},{32,48},{48,64},{64,80},{80,96},{96,112},{1,17},{17... | collective-permute-start | bytes 6291464 | tf_op jit(solution)/shard_map/ppermute | solution.py:54
  20.9 174.4 %collective-permute-start.3 = (bf16[16,512,128]{2,1,0:T(8,128)(2,1)}, bf16[16,512,128]{2,1,0:T(8,128)(2,1)}, u32[]{:S(2)}, u32[]{:S(2)}) collective-permute-start(bf16[16,512,128]{2,1,0:T(8,128)(2,1)} %fusion.20), channel_id=1, source_target_pairs={{0,32},{16,48},{32,64},{48,80},{64,96},{80,112},{1,33},{17,49},{33... | collective-permute-start | bytes 6291464 | tf_op jit(solution)/shard_map/ppermute | solution.py:54
  24.4 178.9 %collective-permute-start.4 = (bf16[16,512,128]{2,1,0:T(8,128)(2,1)}, bf16[16,512,128]{2,1,0:T(8,128)(2,1)}, u32[]{:S(2)}, u32[]{:S(2)}) collective-permute-start(bf16[16,512,128]{2,1,0:T(8,128)(2,1)} %fusion.20), channel_id=1, source_target_pairs={{0,48},{16,64},{32,80},{48,96},{64,112},{1,49},{17,65},{33,81},{49... | collective-permute-start | bytes 6291464 | tf_op jit(solution)/shard_map/ppermute | solution.py:54
  27.4 179.2 %collective-permute-start.5 = (bf16[16,512,128]{2,1,0:T(8,128)(2,1)}, bf16[16,512,128]{2,1,0:T(8,128)(2,1)}, u32[]{:S(2)}, u32[]{:S(2)}) collective-permute-start(bf16[16,512,128]{2,1,0:T(8,128)(2,1)} %fusion.20), channel_id=1, source_target_pairs={{0,64},{16,80},{32,96},{48,112},{1,65},{17,81},{33,97},{49,113},{2... | collective-permute-start | bytes 6291464 | tf_op jit(solution)/shard_map/ppermute | solution.py:54
  30.1 4.9 %collective-permute-start = (f32[1,512]{1,0:T(1,128)S(1)}, f32[1,512]{1,0:T(1,128)S(1)}, u32[]{:S(2)}, u32[]{:S(2)}) collective-permute-start(f32[1,512]{1,0:T(1,128)S(1)} %get-tuple-element.17), channel_id=1, source_target_pairs={{0,1},{1,2},{2,3},{3,4},{4,5},{5,6},{6,7},{7,8},{8,9},{9,10},{10,1... | collective-permute-start | bytes 6152 | tf_op jit(solution)/shard_map/ppermute | solution.py:14
  35.0 5.2 %collective-permute-start.1 = (f32[1,512]{1,0:T(1,128)S(1)}, f32[1,512]{1,0:T(1,128)S(1)}, u32[]{:S(2)}, u32[]{:S(2)}) collective-permute-start(f32[1,512]{1,0:T(1,128)S(1)} %get-tuple-element.18), channel_id=1, source_target_pairs={{1,0},{2,1},{3,2},{4,3},{5,4},{6,5},{7,6},{8,7},{9,8},{10,9},{11,1... | collective-permute-start | bytes 6152 | tf_op jit(solution)/shard_map/ppermute | solution.py:15
  40.2 169.8 %collective-permute-start.6 = (bf16[16,512,128]{2,1,0:T(8,128)(2,1)}, bf16[16,512,128]{2,1,0:T(8,128)(2,1)S(1)}, u32[]{:S(2)}, u32[]{:S(2)}) collective-permute-start(bf16[16,512,128]{2,1,0:T(8,128)(2,1)} %fusion.20), channel_id=1, source_target_pairs={{0,80},{16,96},{32,112},{1,81},{17,97},{33,113},{2,82},{18,98},{34... | collective-permute-start | bytes 6291464 | tf_op jit(solution)/shard_map/ppermute | solution.py:54
  91.1 120.6 %collective-permute-start.7 = (bf16[16,512,128]{2,1,0:T(8,128)(2,1)}, bf16[16,512,128]{2,1,0:T(8,128)(2,1)S(1)}, u32[]{:S(2)}, u32[]{:S(2)}) collective-permute-start(bf16[16,512,128]{2,1,0:T(8,128)(2,1)} %fusion.20), channel_id=1, source_target_pairs={{0,96},{16,112},{1,97},{17,113},{2,98},{18,114},{3,99},{19,115},{4... | collective-permute-start | bytes 6291464 | tf_op jit(solution)/shard_map/ppermute | solution.py:54
  195.2 18.1 %collective-permute-start.8 = (bf16[16,512,128]{2,1,0:T(8,128)(2,1)}, bf16[16,512,128]{2,1,0:T(8,128)(2,1)S(1)}, u32[]{:S(2)}, u32[]{:S(2)}) collective-permute-start(bf16[16,512,128]{2,1,0:T(8,128)(2,1)} %fusion.20), channel_id=1, source_target_pairs={{0,112},{1,113},{2,114},{3,115},{4,116},{5,117},{6,118},{7,119},{8... | collective-permute-start | bytes 6291464 | tf_op jit(solution)/shard_map/ppermute | solution.py:54
  226.4 17.6 %collective-permute-start.10 = (f32[2,128,512]{1,2,0:T(8,128)}, f32[2,128,512]{1,2,0:T(8,128)}, u32[]{:S(2)}, u32[]{:S(2)}) collective-permute-start(f32[2,128,512]{1,2,0:T(8,128)} %get-tuple-element.6), channel_id=1, source_target_pairs={{1,0},{2,1},{3,2},{4,3},{5,4},{6,5},{7,6},{8,7},{9,8},{10,9},{11,1... | collective-permute-start | bytes 1572872 | tf_op jit(solution)/shard_map/ppermute | solution.py:15
  228.3 15.7 %collective-permute-start.9 = (f32[2,128,512]{1,2,0:T(8,128)}, f32[2,128,512]{1,2,0:T(8,128)}, u32[]{:S(2)}, u32[]{:S(2)}) collective-permute-start(f32[2,128,512]{1,2,0:T(8,128)} %get-tuple-element.5), channel_id=1, source_target_pairs={{0,1},{1,2},{2,3},{3,4},{4,5},{5,6},{6,7},{7,8},{8,9},{9,10},{10,1... | collective-permute-start | bytes 1572872 | tf_op jit(solution)/shard_map/ppermute | solution.py:14
  239.0 5.0 %copy-start.1 = (f32[8,128,512]{1,2,0:T(8,128)S(1)}, f32[8,128,512]{1,2,0:T(8,128)}, u32[]{:S(2)}) copy-start(f32[8,128,512]{1,2,0:T(8,128)} %get-tuple-element.7) | copy-start | bytes 6291460
  244.1 2.8 copy-start.7
  248.8 0.7 copy-start.5
  251.1 3.0 copy-start.6
  401.0 7.0 %copy-start = (f32[24,128,512]{2,0,1:T(8,128)S(1)}, f32[24,128,512]{2,0,1:T(8,128)}, u32[]{:S(2)}) copy-start(f32[24,128,512]{2,0,1:T(8,128)} %dynamic_update_slice.3) | copy-start | bytes 18874372
  420.0 6.4 %copy-start.2 = (f32[6,128,512]{2,0,1:T(8,128)S(1)}, f32[6,128,512]{2,0,1:T(8,128)}, u32[]{:S(2)}) copy-start(f32[6,128,512]{2,0,1:T(8,128)} %copy.71) | copy-start | bytes 4718596
Sparse Core Ops, SparseCore 0:
  11.3 348.5 all-gather.2
